TPU v7x, 512 devices: a whole 4x8x8 slice. The times are simulated.
512 devices in a mesh: seq: 128 (over z, y_hi, x, core), head: 4 (over y_lo).
Axes of the slice: x: 4, y: 8 (y_hi: 2, y_lo: 4; y = y_hi * 4 + y_lo), z: 8, core: 2. Of those that a mesh axis runs over, the one named last changes fastest.
Arguments:
- query_rows: bfloat16 [32768, 8, 128], P('seq', 'head'), may hold values from -20 to 20
- key_rows: bfloat16 [32768, 8, 128], P('seq', 'head'), may hold values from -20 to 20
- value_rows: bfloat16 [32768, 8, 128], P('seq', 'head'), may hold values from -6 to 6
- cotangent: bfloat16 [32768, 8, 128], P('seq', 'head'), may hold values from -6 to 6
- norm_gain: float32 [8, 128], P('head'), may hold values from 0.5 to 2
- offsets: int32 [8], P('head'), may hold values from 0 to 31, as said below
Outputs:
- query_grad: bfloat16 [32768, 8, 128], P('seq', 'head')
- key_grad: bfloat16 [32768, 8, 128], P('seq', 'head')
- value_grad: bfloat16 [32768, 8, 128], P('seq', 'head')
Inputs may be any that keep to these rules, and one draw needn't show every extreme that they name: The heads' offsets are distinct.
All inputs are finite; a program needn't handle non-finite values.
Results may differ from a plain program's by a relative error of at most 0.018.
Values may be sent and summed in bfloat16 or wider, within the bound.
No kernel may reach another device: no remote copies, remote signals or barrier semaphores. Data moves between devices by JAX's collectives and lax.ppermute only.
A program may use at most 128 MiB of HBM per device.

v0:
```python
import numpy as np
import jax
import jax.numpy as jnp
from jax import lax
from jax.sharding import PartitionSpec as P

RATE2 = 4
RATE3 = 16
RATE4 = 32
RATES = (1, RATE2, RATE3, RATE4)

neg_fill = -1e30
epsilon = 1e-05
lane = 128


def pick_rows(source, wanted, stride):
    row_count = source.shape[0] // stride
    shaped = source.reshape((row_count, stride) + source.shape[1:])
    trailing = (1,) * (source.ndim - 2)
    target = wanted.reshape((1, 1, -1) + trailing)
    column = jnp.arange(stride, dtype=jnp.int32).reshape((1, stride, 1) + trailing)
    zeroed = jnp.where(column == target, shaped, jnp.zeros((), source.dtype))
    return jnp.sum(zeroed, axis=1, dtype=source.dtype)


def put_rows(compact, wanted, stride, filler):
    trailing = (1,) * (compact.ndim - 2)
    target = wanted.reshape((1, 1, -1) + trailing)
    column = jnp.arange(stride, dtype=jnp.int32).reshape((1, stride, 1) + trailing)
    spread = jnp.where(column == target, compact[:, None], jnp.asarray(filler, compact.dtype))
    return spread.reshape((compact.shape[0] * stride,) + compact.shape[1:])


def exchange_order(count):
    bits = [1 << bit for bit in range(max(0, (count - 1).bit_length()))]
    order = []
    for first in range(0, len(bits), 2):
        order.extend(reversed(bits[first : first + 2]))
    return order


def spread(order, slots):
    table = np.zeros(slots, np.int32)
    for slot in range(slots):
        for bit, offset in enumerate(order):
            if slot >> bit & 1:
                table[slot] ^= offset
    return table


def extend(parts, spans, order):
    count = lax.axis_size("seq")
    live = sorted(range(len(parts)), key=lambda index: -spans[index])
    sizes = [part.shape[0] for part in parts]
    state = jnp.concatenate([parts[index] for index in live], axis=0)[None]
    finished = {}
    for offset in order + [None]:
        while live and spans[live[-1]] <= state.shape[0]:
            index = live.pop()
            start = sum(sizes[other] for other in live)
            finished[index] = state[:, start : start + sizes[index]]
            state = state[:, :start]
        if not live:
            break
        moved = lax.ppermute(state, "seq", [(source, source ^ offset) for source in range(count)])
        state = jnp.concatenate([state, moved], axis=0)
    return [finished[index] for index in range(len(parts))]


def split_exact(value):
    high = lax.reduce_precision(value, exponent_bits=8, mantissa_bits=7)
    rest = value - high
    middle = lax.reduce_precision(rest, exponent_bits=8, mantissa_bits=7)
    low = rest - middle
    return jnp.stack([high, middle, low]).astype(jnp.bfloat16)


def stats_rows(rows, heads_dev):
    return -(-(rows * heads_dev * 6) // (16 * lane)) * 16


def pack_stats(lse_sel, delta_sel):
    rows, heads_dev = lse_sel.shape
    coded = split_exact(jnp.stack([lse_sel.T, delta_sel.T])).reshape(-1)
    padded = stats_rows(rows, heads_dev) * lane
    coded = jnp.pad(coded, (0, padded - coded.shape[0]))
    return coded.reshape(padded // lane, lane)


def unpack_stats(coded, slots, rows, heads_dev):
    width = 2 * heads_dev * rows
    parts = coded.reshape(slots, -1)[:, : 3 * width].reshape(slots, 3, width)
    parts = parts.astype(jnp.float32)
    values = (parts[:, 0] + parts[:, 1]) + parts[:, 2]
    values = values.reshape(slots, 2, heads_dev, rows).transpose(1, 2, 0, 3)
    values = values.reshape(2, heads_dev, slots * rows)
    return values[0], values[1]


def shards(query_rows, key_rows, value_rows, cotangent, norm_gain, offsets):
    tok_dev, heads_dev, head_size = query_rows.shape
    seq_count = lax.axis_size("seq")
    device = lax.axis_index("seq")
    group_rows = tok_dev * seq_count // RATE4
    score_scale = head_size ** (-0.5)
    features = heads_dev * head_size * lax.axis_size("head")

    levels = []
    for stride in RATES:
        span = max(1, stride * group_rows // tok_dev)
        rows = tok_dev // stride
        wanted = offsets % stride
        levels.append(
            dict(
                stride=stride,
                span=span,
                rows=rows,
                wanted=wanted,
                spot=device % span,
                key_sel=pick_rows(key_rows, wanted, stride),
                value_sel=pick_rows(value_rows, wanted, stride),
                query_sel=pick_rows(query_rows, wanted, stride),
            )
        )
    spans = [level["span"] for level in levels]
    order = exchange_order(seq_count)
    for level in levels:
        level["owner"] = level["spot"] ^ jnp.asarray(spread(order, level["span"]))

    key_sets = extend(
        [
            jnp.concatenate(
                [
                    level["key_sel"].reshape(-1, lane),
                    level["value_sel"].reshape(-1, lane),
                ],
                axis=0,
            )
            for level in levels
        ],
        spans,
        order,
    )
    query_sets = extend([level["query_sel"].reshape(-1, lane) for level in levels], spans, order)

    lse_total = jnp.full((tok_dev, heads_dev), neg_fill, jnp.float32)
    for level, key_set in zip(levels, key_sets):
        span, rows = level["span"], level["rows"]
        paired = key_set.reshape(span, 2, rows, heads_dev, head_size)
        keys = paired[:, 0].reshape(span * rows, heads_dev, head_size)
        level["key_all"] = keys
        level["value_all"] = paired[:, 1].reshape(span * rows, heads_dev, head_size)
        raw = (
            jnp.einsum("qhd,khd->hqk", level["query_sel"], keys, preferred_element_type=jnp.float32)
            * score_scale
        )
        key_at = (
            level["owner"][:, None] * rows + jnp.arange(rows, dtype=jnp.int32)[None, :]
        ).reshape(1, span * rows)
        query_at = (level["spot"] * rows + jnp.arange(rows, dtype=jnp.int32))[:, None]
        linked = key_at <= query_at
        scores = jnp.where(linked[None], raw, neg_fill)
        row_peak = jnp.max(scores, axis=2)
        level_lse = row_peak + jnp.log(jnp.sum(jnp.exp(scores - row_peak[:, :, None]), axis=2))
        level["scores"] = scores
        lse_total = jnp.logaddexp(
            lse_total, put_rows(level_lse.T, level["wanted"], level["stride"], neg_fill)
        )

    attended = jnp.zeros((tok_dev, heads_dev, head_size), jnp.float32)
    for level in levels:
        lse_sel = pick_rows(lse_total, level["wanted"], level["stride"])
        weights = jnp.exp(level["scores"] - lse_sel.T[:, :, None])
        level["lse_sel"] = lse_sel
        level["weights"] = weights
        out_sel = jnp.einsum(
            "hqk,khd->qhd", weights.astype(jnp.bfloat16), level["value_all"],
            preferred_element_type=jnp.float32,
        )
        attended = attended + put_rows(out_sel, level["wanted"], level["stride"], 0.0)

    grad_in = cotangent.astype(jnp.float32) * norm_gain[None]
    sums = lax.psum(
        jnp.stack(
            [
                jnp.sum(attended, axis=(1, 2)),
                jnp.sum(attended * attended, axis=(1, 2)),
                jnp.sum(grad_in, axis=(1, 2)),
                jnp.sum(grad_in * attended, axis=(1, 2)),
            ]
        ),
        "head",
    )
    centre = sums[0] / features
    variance = sums[1] / features - centre * centre
    inverse = lax.rsqrt(variance + epsilon)
    first_mean = sums[2] / features
    second_mean = inverse * (sums[3] / features - centre * first_mean)
    normed = (attended - centre[:, None, None]) * inverse[:, None, None]
    d_attended = (
        inverse[:, None, None]
        * (grad_in - first_mean[:, None, None] - normed * second_mean[:, None, None])
    ).astype(jnp.bfloat16)
    row_delta = jnp.sum(d_attended.astype(jnp.float32) * attended, axis=2)

    query_grad = jnp.zeros((tok_dev, heads_dev, head_size), jnp.float32)
    back_sets = []
    for level in levels:
        dout_sel = pick_rows(d_attended, level["wanted"], level["stride"])
        delta_sel = pick_rows(row_delta, level["wanted"], level["stride"])
        back_sets.append(
            jnp.concatenate(
                [dout_sel.reshape(-1, lane), pack_stats(level["lse_sel"], delta_sel)], axis=0
            )
        )
        weight_grad = jnp.einsum(
            "qhd,khd->hqk", dout_sel, level["value_all"], preferred_element_type=jnp.float32
        )
        score_grad = (level["weights"] * (weight_grad - delta_sel.T[:, :, None])).astype(
            jnp.bfloat16
        )
        grad_sel = jnp.einsum(
            "hqk,khd->qhd", score_grad, level["key_all"], preferred_element_type=jnp.float32
        )
        query_grad = query_grad + put_rows(
            grad_sel * score_scale, level["wanted"], level["stride"], 0.0
        )
    back_sets = extend(back_sets, spans, order)

    key_grad = jnp.zeros((tok_dev, heads_dev, head_size), jnp.float32)
    value_grad = jnp.zeros((tok_dev, heads_dev, head_size), jnp.float32)
    for level, query_set, back_set in zip(levels, query_sets, back_sets):
        span, rows = level["span"], level["rows"]
        queries = query_set.reshape(span * rows, heads_dev, head_size)
        back_slots = back_set.reshape(span, -1, lane)
        dout_all = back_slots[:, : rows * heads_dev].reshape(span * rows, heads_dev, head_size)
        lse_all, delta_all = unpack_stats(
            back_slots[:, rows * heads_dev :], span, rows, heads_dev
        )
        raw = (
            jnp.einsum(
                "qhd,khd->hqk", queries, level["key_sel"], preferred_element_type=jnp.float32
            )
            * score_scale
        )
        query_at = (
            level["owner"][:, None] * rows + jnp.arange(rows, dtype=jnp.int32)[None, :]
        ).reshape(span * rows, 1)
        key_at = (level["spot"] * rows + jnp.arange(rows, dtype=jnp.int32))[None, :]
        linked = query_at >= key_at
        scores = jnp.where(linked[None], raw, neg_fill)
        weights = jnp.exp(scores - lse_all[:, :, None])
        value_grad_sel = jnp.einsum(
            "hqk,qhd->khd", weights.astype(jnp.bfloat16), dout_all,
            preferred_element_type=jnp.float32,
        )
        weight_grad = jnp.einsum(
            "qhd,khd->hqk", dout_all, level["value_sel"], preferred_element_type=jnp.float32
        )
        score_grad = (weights * (weight_grad - delta_all[:, :, None])).astype(jnp.bfloat16)
        key_grad_sel = jnp.einsum(
            "hqk,qhd->khd", score_grad, queries, preferred_element_type=jnp.float32
        )
        key_grad = key_grad + put_rows(
            key_grad_sel * score_scale, level["wanted"], level["stride"], 0.0
        )
        value_grad = value_grad + put_rows(value_grad_sel, level["wanted"], level["stride"], 0.0)

    return (
        query_grad.astype(jnp.bfloat16),
        key_grad.astype(jnp.bfloat16),
        value_grad.astype(jnp.bfloat16),
    )


def solution(mesh):
    placed = (
        P("seq", "head", None),
        P("seq", "head", None),
        P("seq", "head", None),
        P("seq", "head", None),
        P("head", None),
        P("head"),
    )
    return jax.shard_map(
        shards,
        mesh=mesh,
        in_specs=placed,
        out_specs=(P("seq", "head", None), P("seq", "head", None), P("seq", "head", None)),
        check_vma=False,
    )
```

profile of v0, /device:TPU:201, one launch (start us, length us, event | category | flops | bytes accessed | tf_op | source)
XLA Modules:
  0.0 374.3 jit_solution(12395727593228231282)
XLA Ops:
  8.0 3.1 collective-permute-start
  11.2 2.3 collective-permute-start.7
  18.9 3.9 %collective-permute-done.7 = bf16[1,688,128]{2,1,0:T(8,128)(2,1)S(1)} collective-permute-done((bf16[1,688,128]{2,1,0:T(8,128)(2,1)S(1)}, bf16[1,688,128]{2,1,0:T(8,128)(2,1)S(1)}, u32[]{:S(2)}, u32[]{:S(2)}) %collective-permute-start.7) | collective-permute-done | bytes 176160 | tf_op jit(solution)/shard_map/ppermute | solution.py:66
  22.8 3.5 collective-permute-start.8
  27.2 1.9 collective-permute-start.1
  29.8 6.6 %collective-permute-start.11 = (bf16[4,176,128]{2,1,0:T(8,128)(2,1)S(1)}, bf16[4,176,128]{2,1,0:T(8,128)(2,1)S(1)}, u32[]{:S(2)}, u32[]{:S(2)}) collective-permute-start(bf16[4,176,128]{2,1,0:T(8,128)(2,1)S(1)} %pad_maximum_fusion.31), channel_id=1, source_target_pairs={{0,32},{4,36},{8,40},{12,44},{16,48},{20,52},{24,56},{28,60},{32,0... | collective-permute-start | bytes 540680 | tf_op jit(solution)/shard_map/ppermute | solution.py:66
  44.0 4.7 %collective-permute-start.12 = (bf16[8,176,128]{2,1,0:T(8,128)(2,1)S(1)}, bf16[8,176,128]{2,1,0:T(8,128)(2,1)S(1)}, u32[]{:S(2)}, u32[]{:S(2)}) collective-permute-start(bf16[8,176,128]{2,1,0:T(8,128)(2,1)S(1)} %pad_maximum_fusion.24), channel_id=1, source_target_pairs={{0,16},{4,20},{8,24},{12,28},{16,0},{20,4},{24,8},{28,12},{32,48},... | collective-permute-start | bytes 1081352 | tf_op jit(solution)/shard_map/ppermute | solution.py:66
  48.9 7.1 %collective-permute-start.2 = (bf16[4,352,128]{2,1,0:T(8,128)(2,1)S(1)}, bf16[4,352,128]{2,1,0:T(8,128)(2,1)S(1)}, u32[]{:S(2)}, u32[]{:S(2)}) collective-permute-start(bf16[4,352,128]{2,1,0:T(8,128)(2,1)S(1)} %pad_maximum_fusion.23), channel_id=1, source_target_pairs={{0,32},{4,36},{8,40},{12,44},{16,48},{20,52},{24,56},{28,60},{32,0... | collective-permute-start | bytes 1081352 | tf_op jit(solution)/shard_map/ppermute | solution.py:66
  56.9 1.9 collective-permute-start.15
  60.9 8.5 %collective-permute-done.15 = bf16[16,48,128]{2,1,0:T(8,128)(2,1)S(1)} collective-permute-done((bf16[16,48,128]{2,1,0:T(8,128)(2,1)S(1)}, bf16[16,48,128]{2,1,0:T(8,128)(2,1)S(1)}, u32[]{:S(2)}, u32[]{:S(2)}) %collective-permute-start.15) | collective-permute-done | bytes 196640 | tf_op jit(solution)/shard_map/ppermute | solution.py:66
  69.4 1.9 collective-permute-start.16
  71.4 4.2 %collective-permute-start.3 = (bf16[8,352,128]{2,1,0:T(8,128)(2,1)S(1)}, bf16[8,352,128]{2,1,0:T(8,128)(2,1)S(1)}, u32[]{:S(2)}, u32[]{:S(2)}) collective-permute-start(bf16[8,352,128]{2,1,0:T(8,128)(2,1)S(1)} %pad_maximum_fusion.8), channel_id=1, source_target_pairs={{0,16},{4,20},{8,24},{12,28},{16,0},{20,4},{24,8},{28,12},{32,48},... | collective-permute-start | bytes 2162696 | tf_op jit(solution)/shard_map/ppermute | solution.py:66
  78.0 2.9 collective-permute-done.16
  81.0 9.0 %collective-permute-start.19 = (bf16[64,16,128]{2,1,0:T(8,128)(2,1)S(1)}, bf16[64,16,128]{2,1,0:T(8,128)(2,1)S(1)}, u32[]{:S(2)}, u32[]{:S(2)}) collective-permute-start(bf16[64,16,128]{2,1,0:T(8,128)(2,1)S(1)} %pad_maximum_fusion.27), channel_id=1, source_target_pairs={{0,256},{4,260},{8,264},{12,268},{16,272},{20,276},{24,280},{28,28... | collective-permute-start | bytes 786440 | tf_op jit(solution)/shard_map/ppermute | solution.py:66
  91.0 1.9 collective-permute-start.4
  93.8 3.8 %collective-permute-done.19 = bf16[64,16,128]{2,1,0:T(8,128)(2,1)S(1)} collective-permute-done((bf16[64,16,128]{2,1,0:T(8,128)(2,1)S(1)}, bf16[64,16,128]{2,1,0:T(8,128)(2,1)S(1)}, u32[]{:S(2)}, u32[]{:S(2)}) %collective-permute-start.19) | collective-permute-done | bytes 262176 | tf_op jit(solution)/shard_map/ppermute | solution.py:66
  99.4 19.0 %collective-permute-done.4 = bf16[16,96,128]{2,1,0:T(8,128)(2,1)S(1)} collective-permute-done((bf16[16,96,128]{2,1,0:T(8,128)(2,1)S(1)}, bf16[16,96,128]{2,1,0:T(8,128)(2,1)S(1)}, u32[]{:S(2)}, u32[]{:S(2)}) %collective-permute-start.4) | collective-permute-done | bytes 393248 | tf_op jit(solution)/shard_map/ppermute | solution.py:66
  119.4 1.9 collective-permute-start.5
  126.7 2.1 copy.224
  128.8 11.5 %collective-permute-done.5 = bf16[32,96,128]{2,1,0:T(8,128)(2,1)} collective-permute-done((bf16[32,96,128]{2,1,0:T(8,128)(2,1)}, bf16[32,96,128]{2,1,0:T(8,128)(2,1)}, u32[]{:S(2)}, u32[]{:S(2)}) %collective-permute-start.5) | collective-permute-done | bytes 786464 | tf_op jit(solution)/shard_map/ppermute | solution.py:66
  142.1 7.1 %collective-permute-start.6 = (bf16[64,32,128]{2,1,0:T(8,128)(2,1)}, bf16[64,32,128]{2,1,0:T(8,128)(2,1)}, u32[]{:S(2)}, u32[]{:S(2)}) collective-permute-start(bf16[64,32,128]{2,1,0:T(8,128)(2,1)} %pad_maximum_fusion.17), channel_id=1, source_target_pairs={{0,256},{4,260},{8,264},{12,268},{16,272},{20,276},{24,280},{28,28... | collective-permute-start | bytes 1572872 | tf_op jit(solution)/shard_map/ppermute | solution.py:66
  154.8 2.2 copy.226
  157.0 14.6 %collective-permute-done.6 = bf16[64,32,128]{2,1,0:T(8,128)(2,1)} collective-permute-done((bf16[64,32,128]{2,1,0:T(8,128)(2,1)}, bf16[64,32,128]{2,1,0:T(8,128)(2,1)}, u32[]{:S(2)}, u32[]{:S(2)}) %collective-permute-start.6) | collective-permute-done | bytes 524320 | tf_op jit(solution)/shard_map/ppermute | solution.py:66
  192.4 2.3 fusion.146
  194.7 9.8 %psum.7 = f32[4,256]{1,0:T(4,128)S(1)} all-reduce(f32[4,256]{1,0:T(4,128)S(1)} %pad_maximum_fusion.34), channel_id=1, replica_groups=mesh['seq'=128,'head'=4] {'head'}, use_global_device_ids=true, to_apply=%region_24.25 | all-reduce | flops 1024 | bytes 8192 | tf_op jit(solution)/shard_map/psum | solution.py:184
  213.3 2.3 fusion.43
  220.3 3.1 collective-permute-start.9
  228.2 7.4 %collective-permute-start.10 = (bf16[2,768,128]{2,1,0:T(8,128)(2,1)}, bf16[2,768,128]{2,1,0:T(8,128)(2,1)S(1)}, u32[]{:S(2)}, u32[]{:S(2)}) collective-permute-start(bf16[2,768,128]{2,1,0:T(8,128)(2,1)} %pad_maximum_fusion.21), channel_id=1, source_target_pairs={{0,4},{4,0},{8,12},{12,8},{16,20},{20,16},{24,28},{28,24},{32,36},... | collective-permute-start | bytes 1179656 | tf_op jit(solution)/shard_map/ppermute | solution.py:66
  235.6 1.9 fusion.63
  245.1 2.1 fusion.31
  249.7 3.8 %collective-permute-start.13 = (bf16[4,224,128]{2,1,0:T(8,128)(2,1)S(1)}, bf16[4,224,128]{2,1,0:T(8,128)(2,1)S(1)}, u32[]{:S(2)}, u32[]{:S(2)}) collective-permute-start(bf16[4,224,128]{2,1,0:T(8,128)(2,1)S(1)} %pad_maximum_fusion.29), channel_id=1, source_target_pairs={{0,32},{4,36},{8,40},{12,44},{16,48},{20,52},{24,56},{28,60},{32,0... | collective-permute-start | bytes 688136 | tf_op jit(solution)/shard_map/ppermute | solution.py:66
  255.3 12.6 %collective-permute-done.13 = bf16[4,224,128]{2,1,0:T(8,128)(2,1)S(1)} collective-permute-done((bf16[4,224,128]{2,1,0:T(8,128)(2,1)S(1)}, bf16[4,224,128]{2,1,0:T(8,128)(2,1)S(1)}, u32[]{:S(2)}, u32[]{:S(2)}) %collective-permute-start.13) | collective-permute-done | bytes 229408 | tf_op jit(solution)/shard_map/ppermute | solution.py:66
  268.0 4.7 %collective-permute-start.14 = (bf16[8,224,128]{2,1,0:T(8,128)(2,1)S(1)}, bf16[8,224,128]{2,1,0:T(8,128)(2,1)S(1)}, u32[]{:S(2)}, u32[]{:S(2)}) collective-permute-start(bf16[8,224,128]{2,1,0:T(8,128)(2,1)S(1)} %pad_maximum_fusion.19), channel_id=1, source_target_pairs={{0,16},{4,20},{8,24},{12,28},{16,0},{20,4},{24,8},{28,12},{32,48},... | collective-permute-start | bytes 1376264 | tf_op jit(solution)/shard_map/ppermute | solution.py:66
  275.1 7.8 %collective-permute-done.14 = bf16[8,224,128]{2,1,0:T(8,128)(2,1)S(1)} collective-permute-done((bf16[8,224,128]{2,1,0:T(8,128)(2,1)S(1)}, bf16[8,224,128]{2,1,0:T(8,128)(2,1)S(1)}, u32[]{:S(2)}, u32[]{:S(2)}) %collective-permute-start.14) | collective-permute-done | bytes 458784 | tf_op jit(solution)/shard_map/ppermute | solution.py:66
  282.9 1.9 collective-permute-start.17
  288.3 14.1 %collective-permute-done.17 = bf16[16,80,128]{2,1,0:T(8,128)(2,1)} collective-permute-done((bf16[16,80,128]{2,1,0:T(8,128)(2,1)S(1)}, bf16[16,80,128]{2,1,0:T(8,128)(2,1)}, u32[]{:S(2)}, u32[]{:S(2)}) %collective-permute-start.17) | collective-permute-done | bytes 327712 | tf_op jit(solution)/shard_map/ppermute | solution.py:66
  302.5 1.9 pad_maximum_fusion.12
  304.4 2.1 collective-permute-start.18
  306.5 2.2 fusion.6
  308.7 2.3 fusion.45
  316.5 5.8 %collective-permute-done.18 = bf16[32,80,128]{2,1,0:T(8,128)(2,1)} collective-permute-done((bf16[32,80,128]{2,1,0:T(8,128)(2,1)}, bf16[32,80,128]{2,1,0:T(8,128)(2,1)}, u32[]{:S(2)}, u32[]{:S(2)}) %collective-permute-start.18) | collective-permute-done | bytes 655392 | tf_op jit(solution)/shard_map/ppermute | solution.py:66
  322.4 2.0 pad_maximum_fusion.16
  324.4 5.2 %collective-permute-start.20 = (bf16[64,32,128]{2,1,0:T(8,128)(2,1)}, bf16[64,32,128]{2,1,0:T(8,128)(2,1)}, u32[]{:S(2)}, u32[]{:S(2)}) collective-permute-start(bf16[64,32,128]{2,1,0:T(8,128)(2,1)} %get-tuple-element.33), channel_id=1, source_target_pairs={{0,256},{4,260},{8,264},{12,268},{16,272},{20,276},{24,280},{28,28... | collective-permute-start | bytes 1572872 | tf_op jit(solution)/shard_map/ppermute | solution.py:66
  331.3 2.0 copy.293
  340.5 15.0 %collective-permute-done.20 = bf16[64,32,128]{2,1,0:T(8,128)(2,1)} collective-permute-done((bf16[64,32,128]{2,1,0:T(8,128)(2,1)}, bf16[64,32,128]{2,1,0:T(8,128)(2,1)}, u32[]{:S(2)}, u32[]{:S(2)}) %collective-permute-start.20) | collective-permute-done | bytes 524320 | tf_op jit(solution)/shard_map/ppermute | solution.py:66
  355.5 2.2 pad_maximum_fusion.13
  363.4 2.2 fusion.61
  367.1 2.6 fusion.30
  (444 shorter events, 127.0 us)
Async XLA Ops:
  1.5 35.6 %copy-start.76 = (pred[32,2]{0,1:T(4,128)(4,1)}, pred[32,2]{0,1:T(4,128)(4,1)S(1)}, u32[]{:S(2)}) copy-start(pred[32,2]{0,1:T(4,128)(4,1)S(1)} %iota_compare_fusion.2) | copy-start | bytes 196
  5.6 21.7 %copy-start.54 = (bf16[8,2,128]{2,0,1:T(8,128)(2,1)}, bf16[8,2,128]{2,0,1:T(8,128)(2,1)S(1)}, u32[]{:S(2)}) copy-start(bf16[8,2,128]{2,0,1:T(8,128)(2,1)S(1)} %get-tuple-element.25) | copy-start | bytes 12292
  5.7 32.9 %copy-start.74 = (pred[16,2]{0,1:T(4,128)(4,1)}, pred[16,2]{0,1:T(4,128)(4,1)S(1)}, u32[]{:S(2)}) copy-start(pred[16,2]{0,1:T(4,128)(4,1)S(1)} %iota_compare_fusion.1) | copy-start | bytes 100
  7.0 20.2 %copy-start.62 = (bf16[16,2,128]{2,0,1:T(8,128)(2,1)}, bf16[16,2,128]{2,0,1:T(8,128)(2,1)S(1)}, u32[]{:S(2)}) copy-start(bf16[16,2,128]{2,0,1:T(8,128)(2,1)S(1)} %get-tuple-element.24) | copy-start | bytes 24580
  7.1 33.0 %copy-start.72 = (pred[4,2]{0,1:T(4,128)(4,1)}, pred[4,2]{0,1:T(4,128)(4,1)S(1)}, u32[]{:S(2)}) copy-start(pred[4,2]{0,1:T(4,128)(4,1)S(1)} %iota_compare_fusion) | copy-start | bytes 28
  7.7 18.5 %copy-start.31 = (bf16[64,2,128]{2,0,1:T(8,128)(2,1)}, bf16[64,2,128]{2,0,1:T(8,128)(2,1)S(1)}, u32[]{:S(2)}) copy-start(bf16[64,2,128]{2,0,1:T(8,128)(2,1)S(1)} %get-tuple-element.20) | copy-start | bytes 98308
  7.7 18.5 %copy-start.33 = (bf16[64,2,128]{2,0,1:T(8,128)(2,1)}, bf16[64,2,128]{2,0,1:T(8,128)(2,1)S(1)}, u32[]{:S(2)}) copy-start(bf16[64,2,128]{2,0,1:T(8,128)(2,1)S(1)} %get-tuple-element.19) | copy-start | bytes 98308
  7.8 18.5 %copy-start.38 = (bf16[64,2,128]{2,0,1:T(8,128)(2,1)}, bf16[64,2,128]{2,0,1:T(8,128)(2,1)S(1)}, u32[]{:S(2)}) copy-start(bf16[64,2,128]{2,0,1:T(8,128)(2,1)S(1)} %get-tuple-element.21) | copy-start | bytes 98308
  8.0 18.3 %collective-permute-start = (bf16[1,1376,128]{2,1,0:T(8,128)(2,1)S(1)}, bf16[1,1376,128]{2,1,0:T(8,128)(2,1)S(1)}, u32[]{:S(2)}, u32[]{:S(2)}) collective-permute-start(bf16[1,1376,128]{2,1,0:T(8,128)(2,1)S(1)} %bitcast.328), channel_id=1, source_target_pairs={{0,8},{4,12},{8,0},{12,4},{16,24},{20,28},{24,16},{28,20},{32,40},... | collective-permute-start | bytes 1056776 | tf_op jit(solution)/shard_map/ppermute | solution.py:66
  11.2 28.1 %copy-start.40 = (bf16[256,2,128]{2,1,0:T(2,128)(2,1)S(1)}, bf16[256,2,128]{2,1,0:T(2,128)(2,1)}, u32[]{:S(2)}) copy-start(bf16[256,2,128]{2,1,0:T(2,128)(2,1)} %param.13) | copy-start | bytes 393220
  11.2 11.5 %collective-permute-start.7 = (bf16[1,688,128]{2,1,0:T(8,128)(2,1)S(1)}, bf16[1,688,128]{2,1,0:T(8,128)(2,1)S(1)}, u32[]{:S(2)}, u32[]{:S(2)}) collective-permute-start(bf16[1,688,128]{2,1,0:T(8,128)(2,1)S(1)} %maximum_bitcast_fusion), channel_id=1, source_target_pairs={{0,8},{4,12},{8,0},{12,4},{16,24},{20,28},{24,16},{28,20},{32,40},... | collective-permute-start | bytes 528392 | tf_op jit(solution)/shard_map/ppermute | solution.py:66
  22.8 7.0 %collective-permute-start.8 = (bf16[2,688,128]{2,1,0:T(8,128)(2,1)S(1)}, bf16[2,688,128]{2,1,0:T(8,128)(2,1)S(1)}, u32[]{:S(2)}, u32[]{:S(2)}) collective-permute-start(bf16[2,688,128]{2,1,0:T(8,128)(2,1)S(1)} %pad_maximum_fusion.25), channel_id=1, source_target_pairs={{0,4},{4,0},{8,12},{12,8},{16,20},{20,16},{24,28},{28,24},{32,36},... | collective-permute-start | bytes 1056776 | tf_op jit(solution)/shard_map/ppermute | solution.py:66
  27.2 21.4 %collective-permute-start.1 = (bf16[2,1376,128]{2,1,0:T(8,128)(2,1)}, bf16[2,1376,128]{2,1,0:T(8,128)(2,1)S(1)}, u32[]{:S(2)}, u32[]{:S(2)}) collective-permute-start(bf16[2,1376,128]{2,1,0:T(8,128)(2,1)} %pad_maximum_fusion.10), channel_id=1, source_target_pairs={{0,4},{4,0},{8,12},{12,8},{16,20},{20,16},{24,28},{28,24},{32,36},... | collective-permute-start | bytes 2113544 | tf_op jit(solution)/shard_map/ppermute | solution.py:66
  29.8 14.1 %collective-permute-start.11 = (bf16[4,176,128]{2,1,0:T(8,128)(2,1)S(1)}, bf16[4,176,128]{2,1,0:T(8,128)(2,1)S(1)}, u32[]{:S(2)}, u32[]{:S(2)}) collective-permute-start(bf16[4,176,128]{2,1,0:T(8,128)(2,1)S(1)} %pad_maximum_fusion.31), channel_id=1, source_target_pairs={{0,32},{4,36},{8,40},{12,44},{16,48},{20,52},{24,56},{28,60},{32,0... | collective-permute-start | bytes 540680 | tf_op jit(solution)/shard_map/ppermute | solution.py:66
  37.9 207.2 %copy-start.46 = (pred[256,2]{0,1:T(4,128)(4,1)}, pred[256,2]{0,1:T(4,128)(4,1)S(1)}, u32[]{:S(2)}) copy-start(pred[256,2]{0,1:T(4,128)(4,1)S(1)} %broadcast_in_dim.631) | copy-start | bytes 1540
  38.7 153.7 %copy-start.48 = (pred[256,2]{0,1:T(4,128)(4,1)}, pred[256,2]{0,1:T(4,128)(4,1)S(1)}, u32[]{:S(2)}) copy-start(pred[256,2]{0,1:T(4,128)(4,1)S(1)} %broadcast_in_dim.625) | copy-start | bytes 1540
  44.0 12.0 %collective-permute-start.12 = (bf16[8,176,128]{2,1,0:T(8,128)(2,1)S(1)}, bf16[8,176,128]{2,1,0:T(8,128)(2,1)S(1)}, u32[]{:S(2)}, u32[]{:S(2)}) collective-permute-start(bf16[8,176,128]{2,1,0:T(8,128)(2,1)S(1)} %pad_maximum_fusion.24), channel_id=1, source_target_pairs={{0,16},{4,20},{8,24},{12,28},{16,0},{20,4},{24,8},{28,12},{32,48},... | collective-permute-start | bytes 1081352 | tf_op jit(solution)/shard_map/ppermute | solution.py:66
  48.9 22.4 %collective-permute-start.2 = (bf16[4,352,128]{2,1,0:T(8,128)(2,1)S(1)}, bf16[4,352,128]{2,1,0:T(8,128)(2,1)S(1)}, u32[]{:S(2)}, u32[]{:S(2)}) collective-permute-start(bf16[4,352,128]{2,1,0:T(8,128)(2,1)S(1)} %pad_maximum_fusion.23), channel_id=1, source_target_pairs={{0,32},{4,36},{8,40},{12,44},{16,48},{20,52},{24,56},{28,60},{32,0... | collective-permute-start | bytes 1081352 | tf_op jit(solution)/shard_map/ppermute | solution.py:66
  56.9 24.1 %copy-start.11 = (bf16[16,48,128]{2,1,0:T(8,128)(2,1)}, bf16[16,48,128]{2,1,0:T(8,128)(2,1)S(1)}, u32[]{:S(2)}) copy-start(bf16[16,48,128]{2,1,0:T(8,128)(2,1)S(1)} %pad_maximum_fusion.30) | copy-start | bytes 589828
  56.9 12.5 %collective-permute-start.15 = (bf16[16,48,128]{2,1,0:T(8,128)(2,1)S(1)}, bf16[16,48,128]{2,1,0:T(8,128)(2,1)S(1)}, u32[]{:S(2)}, u32[]{:S(2)}) collective-permute-start(bf16[16,48,128]{2,1,0:T(8,128)(2,1)S(1)} %pad_maximum_fusion.30), channel_id=1, source_target_pairs={{0,128},{4,132},{8,136},{12,140},{16,144},{20,148},{24,152},{28,15... | collective-permute-start | bytes 589832 | tf_op jit(solution)/shard_map/ppermute | solution.py:66
  69.4 11.6 %collective-permute-start.16 = (bf16[32,48,128]{2,1,0:T(8,128)(2,1)S(1)}, bf16[32,48,128]{2,1,0:T(8,128)(2,1)S(1)}, u32[]{:S(2)}, u32[]{:S(2)}) collective-permute-start(bf16[32,48,128]{2,1,0:T(8,128)(2,1)S(1)} %pad_maximum_fusion.22), channel_id=1, source_target_pairs={{0,64},{4,68},{8,72},{12,76},{16,80},{20,84},{24,88},{28,92},{32,9... | collective-permute-start | bytes 1179656 | tf_op jit(solution)/shard_map/ppermute | solution.py:66
  71.4 19.5 %collective-permute-start.3 = (bf16[8,352,128]{2,1,0:T(8,128)(2,1)S(1)}, bf16[8,352,128]{2,1,0:T(8,128)(2,1)S(1)}, u32[]{:S(2)}, u32[]{:S(2)}) collective-permute-start(bf16[8,352,128]{2,1,0:T(8,128)(2,1)S(1)} %pad_maximum_fusion.8), channel_id=1, source_target_pairs={{0,16},{4,20},{8,24},{12,28},{16,0},{20,4},{24,8},{28,12},{32,48},... | collective-permute-start | bytes 2162696 | tf_op jit(solution)/shard_map/ppermute | solution.py:66
  81.0 16.6 %collective-permute-start.19 = (bf16[64,16,128]{2,1,0:T(8,128)(2,1)S(1)}, bf16[64,16,128]{2,1,0:T(8,128)(2,1)S(1)}, u32[]{:S(2)}, u32[]{:S(2)}) collective-permute-start(bf16[64,16,128]{2,1,0:T(8,128)(2,1)S(1)} %pad_maximum_fusion.27), channel_id=1, source_target_pairs={{0,256},{4,260},{8,264},{12,268},{16,272},{20,276},{24,280},{28,28... | collective-permute-start | bytes 786440 | tf_op jit(solution)/shard_map/ppermute | solution.py:66
  91.0 27.4 %collective-permute-start.4 = (bf16[16,96,128]{2,1,0:T(8,128)(2,1)S(1)}, bf16[16,96,128]{2,1,0:T(8,128)(2,1)S(1)}, u32[]{:S(2)}, u32[]{:S(2)}) collective-permute-start(bf16[16,96,128]{2,1,0:T(8,128)(2,1)S(1)} %pad_maximum_fusion.20), channel_id=1, source_target_pairs={{0,128},{4,132},{8,136},{12,140},{16,144},{20,148},{24,152},{28,15... | collective-permute-start | bytes 1179656 | tf_op jit(solution)/shard_map/ppermute | solution.py:66
  99.4 23.9 %copy-start.34 = (bf16[64,2,128]{2,0,1:T(8,128)(2,1)S(1)}, bf16[64,2,128]{2,0,1:T(8,128)(2,1)}, u32[]{:S(2)}) copy-start(bf16[64,2,128]{2,0,1:T(8,128)(2,1)} %copy-done.33) | copy-start | bytes 98308
  99.4 23.8 %copy-start.37 = (pred[64,1024]{1,0:T(8,128)(4,1)S(1)}, pred[64,1024]{1,0:T(8,128)(4,1)}, u32[]{:S(2)}) copy-start(pred[64,1024]{1,0:T(8,128)(4,1)} %broadcast_compare_fusion.3) | copy-start | bytes 196612
  119.4 20.8 %collective-permute-start.5 = (bf16[32,96,128]{2,1,0:T(8,128)(2,1)}, bf16[32,96,128]{2,1,0:T(8,128)(2,1)}, u32[]{:S(2)}, u32[]{:S(2)}) collective-permute-start(bf16[32,96,128]{2,1,0:T(8,128)(2,1)} %pad_maximum_fusion.5), channel_id=1, source_target_pairs={{0,64},{4,68},{8,72},{12,76},{16,80},{20,84},{24,88},{28,92},{32,9... | collective-permute-start | bytes 2359304 | tf_op jit(solution)/shard_map/ppermute | solution.py:66
  126.7 22.5 %copy-start.4 = (bf16[16,96,128]{2,1,0:T(8,128)(2,1)S(1)}, bf16[16,96,128]{2,1,0:T(8,128)(2,1)}, u32[]{:S(2)}) copy-start(bf16[16,96,128]{2,1,0:T(8,128)(2,1)} %copy-done.3) | copy-start | bytes 1179652
  142.1 29.5 %collective-permute-start.6 = (bf16[64,32,128]{2,1,0:T(8,128)(2,1)}, bf16[64,32,128]{2,1,0:T(8,128)(2,1)}, u32[]{:S(2)}, u32[]{:S(2)}) collective-permute-start(bf16[64,32,128]{2,1,0:T(8,128)(2,1)} %pad_maximum_fusion.17), channel_id=1, source_target_pairs={{0,256},{4,260},{8,264},{12,268},{16,272},{20,276},{24,280},{28,28... | collective-permute-start | bytes 1572872 | tf_op jit(solution)/shard_map/ppermute | solution.py:66
  192.3 19.0 %copy-start.73 = (pred[4,2]{0,1:T(4,128)(4,1)S(1)}, pred[4,2]{0,1:T(4,128)(4,1)}, u32[]{:S(2)}) copy-start(pred[4,2]{0,1:T(4,128)(4,1)} %copy-done.72) | copy-start | bytes 28
  220.3 28.5 %copy-start.10 = (bf16[768,128]{1,0:T(8,128)(2,1)}, bf16[768,128]{1,0:T(8,128)(2,1)S(1)}, u32[]{:S(2)}) copy-start(bf16[768,128]{1,0:T(8,128)(2,1)S(1)} %constant_dynamic-update-slice_fusion.8) | copy-start | bytes 589828
  220.3 6.4 %collective-permute-start.9 = (bf16[1,768,128]{2,1,0:T(8,128)(2,1)S(1)}, bf16[1,768,128]{2,1,0:T(8,128)(2,1)S(1)}, u32[]{:S(2)}, u32[]{:S(2)}) collective-permute-start(bf16[1,768,128]{2,1,0:T(8,128)(2,1)S(1)} %bitcast.332), channel_id=1, source_target_pairs={{0,8},{4,12},{8,0},{12,4},{16,24},{20,28},{24,16},{28,20},{32,40},... | collective-permute-start | bytes 589832 | tf_op jit(solution)/shard_map/ppermute | solution.py:66
  225.0 20.1 %copy-start.21 = (bf16[256,2,128]{0,2,1:T(8,128)(2,1)S(1)}, bf16[256,2,128]{0,2,1:T(8,128)(2,1)}, u32[]{:S(2)}) copy-start(bf16[256,2,128]{0,2,1:T(8,128)(2,1)} %copy-done.20) | copy-start | bytes 393220
  225.0 20.0 %copy-start.49 = (pred[256,2]{0,1:T(4,128)(4,1)S(1)}, pred[256,2]{0,1:T(4,128)(4,1)}, u32[]{:S(2)}) copy-start(pred[256,2]{0,1:T(4,128)(4,1)} %copy-done.48) | copy-start | bytes 1540
  225.1 20.0 %copy-start.52 = (pred[256,2]{0,1:T(4,128)(4,1)S(1)}, pred[256,2]{0,1:T(4,128)(4,1)}, u32[]{:S(2)}) copy-start(pred[256,2]{0,1:T(4,128)(4,1)} %broadcast_in_dim.618) | copy-start | bytes 1540
  225.1 20.0 %copy-start.57 = (f32[256,2]{0,1:T(2,128)S(1)}, f32[256,2]{0,1:T(2,128)}, u32[]{:S(2)}) copy-start(f32[256,2]{0,1:T(2,128)} %copy-done.56) | copy-start | bytes 6148
  228.2 19.8 %collective-permute-start.10 = (bf16[2,768,128]{2,1,0:T(8,128)(2,1)}, bf16[2,768,128]{2,1,0:T(8,128)(2,1)S(1)}, u32[]{:S(2)}, u32[]{:S(2)}) collective-permute-start(bf16[2,768,128]{2,1,0:T(8,128)(2,1)} %pad_maximum_fusion.21), channel_id=1, source_target_pairs={{0,4},{4,0},{8,12},{12,8},{16,20},{20,16},{24,28},{28,24},{32,36},... | collective-permute-start | bytes 1179656 | tf_op jit(solution)/shard_map/ppermute | solution.py:66
  249.7 18.2 %collective-permute-start.13 = (bf16[4,224,128]{2,1,0:T(8,128)(2,1)S(1)}, bf16[4,224,128]{2,1,0:T(8,128)(2,1)S(1)}, u32[]{:S(2)}, u32[]{:S(2)}) collective-permute-start(bf16[4,224,128]{2,1,0:T(8,128)(2,1)S(1)} %pad_maximum_fusion.29), channel_id=1, source_target_pairs={{0,32},{4,36},{8,40},{12,44},{16,48},{20,52},{24,56},{28,60},{32,0... | collective-permute-start | bytes 688136 | tf_op jit(solution)/shard_map/ppermute | solution.py:66
  253.6 19.6 %copy-start.19 = (bf16[256,2,128]{2,1,0:T(2,128)(2,1)S(1)}, bf16[256,2,128]{2,1,0:T(2,128)(2,1)}, u32[]{:S(2)}) copy-start(bf16[256,2,128]{2,1,0:T(2,128)(2,1)} %param.11) | copy-start | bytes 393220
  268.0 14.9 %collective-permute-start.14 = (bf16[8,224,128]{2,1,0:T(8,128)(2,1)S(1)}, bf16[8,224,128]{2,1,0:T(8,128)(2,1)S(1)}, u32[]{:S(2)}, u32[]{:S(2)}) collective-permute-start(bf16[8,224,128]{2,1,0:T(8,128)(2,1)S(1)} %pad_maximum_fusion.19), channel_id=1, source_target_pairs={{0,16},{4,20},{8,24},{12,28},{16,0},{20,4},{24,8},{28,12},{32,48},... | collective-permute-start | bytes 1376264 | tf_op jit(solution)/shard_map/ppermute | solution.py:66
  282.9 19.5 %collective-permute-start.17 = (bf16[16,80,128]{2,1,0:T(8,128)(2,1)S(1)}, bf16[16,80,128]{2,1,0:T(8,128)(2,1)}, u32[]{:S(2)}, u32[]{:S(2)}) collective-permute-start(bf16[16,80,128]{2,1,0:T(8,128)(2,1)S(1)} %pad_maximum_fusion.26), channel_id=1, source_target_pairs={{0,128},{4,132},{8,136},{12,140},{16,144},{20,148},{24,152},{28,15... | collective-permute-start | bytes 983048 | tf_op jit(solution)/shard_map/ppermute | solution.py:66
  286.4 20.1 %copy-start.39 = (bf16[64,2,128]{2,0,1:T(8,128)(2,1)S(1)}, bf16[64,2,128]{2,0,1:T(8,128)(2,1)}, u32[]{:S(2)}) copy-start(bf16[64,2,128]{2,0,1:T(8,128)(2,1)} %copy-done.38) | copy-start | bytes 98308
  287.6 21.1 %copy-start.32 = (bf16[64,2,128]{2,0,1:T(8,128)(2,1)S(1)}, bf16[64,2,128]{2,0,1:T(8,128)(2,1)}, u32[]{:S(2)}) copy-start(bf16[64,2,128]{2,0,1:T(8,128)(2,1)} %copy-done.31) | copy-start | bytes 98308
  288.3 20.4 %copy-start.58 = (f32[2,1024]{1,0:T(2,128)S(1)}, f32[2,1024]{1,0:T(2,128)}, u32[]{:S(2)}) copy-start(f32[2,1024]{1,0:T(2,128)} %sub.438) | copy-start | bytes 24580
  304.4 18.0 %collective-permute-start.18 = (bf16[32,80,128]{2,1,0:T(8,128)(2,1)}, bf16[32,80,128]{2,1,0:T(8,128)(2,1)}, u32[]{:S(2)}, u32[]{:S(2)}) collective-permute-start(bf16[32,80,128]{2,1,0:T(8,128)(2,1)} %pad_maximum_fusion.12), channel_id=1, source_target_pairs={{0,64},{4,68},{8,72},{12,76},{16,80},{20,84},{24,88},{28,92},{32,9... | collective-permute-start | bytes 1966088 | tf_op jit(solution)/shard_map/ppermute | solution.py:66
  324.4 31.2 %collective-permute-start.20 = (bf16[64,32,128]{2,1,0:T(8,128)(2,1)}, bf16[64,32,128]{2,1,0:T(8,128)(2,1)}, u32[]{:S(2)}, u32[]{:S(2)}) collective-permute-start(bf16[64,32,128]{2,1,0:T(8,128)(2,1)} %get-tuple-element.33), channel_id=1, source_target_pairs={{0,256},{4,260},{8,264},{12,268},{16,272},{20,276},{24,280},{28,28... | collective-permute-start | bytes 1572872 | tf_op jit(solution)/shard_map/ppermute | solution.py:66
  340.5 19.7 %copy-start.69 = (bf16[8,2,128]{2,0,1:T(8,128)(2,1)S(1)}, bf16[8,2,128]{2,0,1:T(8,128)(2,1)}, u32[]{:S(2)}) copy-start(bf16[8,2,128]{2,0,1:T(8,128)(2,1)} %copy-done.68) | copy-start | bytes 12292
  340.5 19.7 %copy-start.80 = (pred[1024,8]{0,1:T(8,128)(4,1)S(1)}, pred[1024,8]{0,1:T(8,128)(4,1)}, u32[]{:S(2)}) copy-start(pred[1024,8]{0,1:T(8,128)(4,1)} %broadcast_compare_fusion.6) | copy-start | bytes 24580
  (63 other events, 472.5 us)
where the time goes:
time: 377 us; the launch traced here: 374 us
  waiting for transfers between devices  123 us (33%)
  starting transfers between devices  85.3 us (23%)
  local copies, waits for them, and re-layouts  70 us (19%)
  other arithmetic  46.2 us (12%)
  matrix products  37.5 us (10%)
  blocking collectives  9.81 us (3%)
    ppermute x21, waiting for transfers between devices, extend(): lax.ppermute(state, 'seq', [(source, source ^ offset) for source in range...  123 us
    ppermute x21, starting transfers between devices, extend(): lax.ppermute(state, 'seq', [(source, source ^ offset) for source in range...  85.3 us
    broadcast_in_dim x45, local copies, waits for them, and re-layouts, put_rows(): jnp.where(column == target, compact[:, None], jnp.asarray(filler, compact...  30.1 us
    concatenate x20, other arithmetic, extend(): state = jnp.concatenate([state, moved], axis=0)  13.2 us
    unnamed x205, local copies, waits for them, and re-layouts  12.9 us
    reduce_sum x12, other arithmetic, pick_rows(): return jnp.sum(zeroed, axis=1, dtype=source.dtype)  12.1 us
    psum x1, blocking collectives, shards(): lax.psum(jnp.stack([jnp.sum(attended, axis=(1, 2)), jnp.sum(attended * at...  9.81 us
    dot_general x4, matrix products, shards(): jnp.einsum('hqk,qhd->khd', score_grad, queries, preferred_element_type=jn...  8.41 us
  transfers between devices with their start and end apart: 21, of which 14 were waited for; matrix products, arithmetic and copies ran while one was open for 20% of the time, Pallas kernels for 0%

commit v1 on v0

--- a/solution.py
+++ b/solution.py
@@ -142,7 +142,10 @@
         spans,
         order,
     )
-    query_sets = extend([level["query_sel"].reshape(-1, lane) for level in levels], spans, order)
+    query_parts, key_sets = lax.optimization_barrier(
+        ([level["query_sel"].reshape(-1, lane) for level in levels], key_sets)
+    )
+    query_sets = extend(query_parts, spans, order)
 
     lse_total = jnp.full((tok_dev, heads_dev), neg_fill, jnp.float32)
     for level, key_set in zip(levels, key_sets):
@@ -226,6 +229,7 @@
         query_grad = query_grad + put_rows(
             grad_sel * score_scale, level["wanted"], level["stride"], 0.0
         )
+    back_sets, query_sets = lax.optimization_barrier((back_sets, query_sets))
     back_sets = extend(back_sets, spans, order)
 
     key_grad = jnp.zeros((tok_dev, heads_dev, head_size), jnp.float32)

time: 377 us -> 449 us (1.19)
  the two profiles are of different devices: /device:TPU:201 before, /device:TPU:6 now
where the time goes in v1:
time: 449 us; the launch traced here: 446 us
  waiting for transfers between devices  148 us (33%)
  starting transfers between devices  112 us (25%)
  local copies, waits for them, and re-layouts  82.3 us (18%)
  other arithmetic  50.5 us (11%)
  matrix products  37.2 us (8%)
  blocking collectives  13.7 us (3%)
    ppermute x21, waiting for transfers between devices, extend(): lax.ppermute(state, 'seq', [(source, source ^ offset) for source in range...  148 us
    ppermute x21, starting transfers between devices, extend(): lax.ppermute(state, 'seq', [(source, source ^ offset) for source in range...  112 us
    broadcast_in_dim x45, local copies, waits for them, and re-layouts, put_rows(): jnp.where(column == target, compact[:, None], jnp.asarray(filler, compact...  29.9 us
    unnamed x218, local copies, waits for them, and re-layouts  18.2 us
    concatenate x20, other arithmetic, extend(): state = jnp.concatenate([state, moved], axis=0)  15.5 us
    psum x1, blocking collectives, shards(): lax.psum(jnp.stack([jnp.sum(attended, axis=(1, 2)), jnp.sum(attended * at...  13.7 us
    reduce_sum x12, other arithmetic, pick_rows(): return jnp.sum(zeroed, axis=1, dtype=source.dtype)  12 us
    dot_general x4, matrix products, shards(): jnp.einsum('hqk,khd->qhd', score_grad, level['key_all'], preferred_elemen...  9.76 us
  transfers between devices with their start and end apart: 21, of which 19 were waited for; matrix products, arithmetic and copies ran while one was open for 19% of the time, Pallas kernels for 0%

profile of v1, /device:TPU:6, one launch (start us, length us, event | category | flops | bytes accessed | tf_op | source)
XLA Modules:
  0.0 446.2 jit_solution(4393063748798826100)
XLA Ops:
  8.8 2.7 collective-permute-start
  11.7 9.0 %collective-permute-done = bf16[1,1376,128]{2,1,0:T(8,128)(2,1)S(1)} collective-permute-done((bf16[1,1376,128]{2,1,0:T(8,128)(2,1)S(1)}, bf16[1,1376,128]{2,1,0:T(8,128)(2,1)S(1)}, u32[]{:S(2)}, u32[]{:S(2)}) %collective-permute-start) | collective-permute-done | bytes 352288 | tf_op jit(solution)/shard_map/ppermute | solution.py:66
  24.9 7.9 %collective-permute-start.2 = (bf16[4,352,128]{2,1,0:T(8,128)(2,1)S(1)}, bf16[4,352,128]{2,1,0:T(8,128)(2,1)S(1)}, u32[]{:S(2)}, u32[]{:S(2)}) collective-permute-start(bf16[4,352,128]{2,1,0:T(8,128)(2,1)S(1)} %pad_maximum_fusion.23), channel_id=1, source_target_pairs={{0,32},{4,36},{8,40},{12,44},{16,48},{20,52},{24,56},{28,60},{32,0... | collective-permute-start | bytes 1081352 | tf_op jit(solution)/shard_map/ppermute | solution.py:66
  32.8 12.3 %collective-permute-done.2 = bf16[4,352,128]{2,1,0:T(8,128)(2,1)S(1)} collective-permute-done((bf16[4,352,128]{2,1,0:T(8,128)(2,1)S(1)}, bf16[4,352,128]{2,1,0:T(8,128)(2,1)S(1)}, u32[]{:S(2)}, u32[]{:S(2)}) %collective-permute-start.2) | collective-permute-done | bytes 360480 | tf_op jit(solution)/shard_map/ppermute | solution.py:66
  46.0 6.1 %collective-permute-start.3 = (bf16[8,352,128]{2,1,0:T(8,128)(2,1)}, bf16[8,352,128]{2,1,0:T(8,128)(2,1)S(1)}, u32[]{:S(2)}, u32[]{:S(2)}) collective-permute-start(bf16[8,352,128]{2,1,0:T(8,128)(2,1)} %pad_maximum_fusion.8), channel_id=1, source_target_pairs={{0,16},{4,20},{8,24},{12,28},{16,0},{20,4},{24,8},{28,12},{32,48},... | collective-permute-start | bytes 2162696 | tf_op jit(solution)/shard_map/ppermute | solution.py:66
  54.2 13.5 %collective-permute-done.3 = bf16[8,352,128]{2,1,0:T(8,128)(2,1)S(1)} collective-permute-done((bf16[8,352,128]{2,1,0:T(8,128)(2,1)}, bf16[8,352,128]{2,1,0:T(8,128)(2,1)S(1)}, u32[]{:S(2)}, u32[]{:S(2)}) %collective-permute-start.3) | collective-permute-done | bytes 720928 | tf_op jit(solution)/shard_map/ppermute | solution.py:66
  67.7 5.4 %collective-permute-start.4 = (bf16[16,96,128]{2,1,0:T(8,128)(2,1)S(1)}, bf16[16,96,128]{2,1,0:T(8,128)(2,1)S(1)}, u32[]{:S(2)}, u32[]{:S(2)}) collective-permute-start(bf16[16,96,128]{2,1,0:T(8,128)(2,1)S(1)} %pad_maximum_fusion.20), channel_id=1, source_target_pairs={{0,128},{4,132},{8,136},{12,140},{16,144},{20,148},{24,152},{28,15... | collective-permute-start | bytes 1179656 | tf_op jit(solution)/shard_map/ppermute | solution.py:66
  79.5 9.7 %collective-permute-done.4 = bf16[16,96,128]{2,1,0:T(8,128)(2,1)S(1)} collective-permute-done((bf16[16,96,128]{2,1,0:T(8,128)(2,1)S(1)}, bf16[16,96,128]{2,1,0:T(8,128)(2,1)S(1)}, u32[]{:S(2)}, u32[]{:S(2)}) %collective-permute-start.4) | collective-permute-done | bytes 393248 | tf_op jit(solution)/shard_map/ppermute | solution.py:66
  89.3 2.6 collective-permute-start.5
  94.5 15.1 %collective-permute-done.5 = bf16[32,96,128]{2,1,0:T(8,128)(2,1)S(1)} collective-permute-done((bf16[32,96,128]{2,1,0:T(8,128)(2,1)S(1)}, bf16[32,96,128]{2,1,0:T(8,128)(2,1)S(1)}, u32[]{:S(2)}, u32[]{:S(2)}) %collective-permute-start.5) | collective-permute-done | bytes 786464 | tf_op jit(solution)/shard_map/ppermute | solution.py:66
  109.7 9.6 %collective-permute-start.6 = (bf16[64,32,128]{2,1,0:T(8,128)(2,1)S(1)}, bf16[64,32,128]{2,1,0:T(8,128)(2,1)S(1)}, u32[]{:S(2)}, u32[]{:S(2)}) collective-permute-start(bf16[64,32,128]{2,1,0:T(8,128)(2,1)S(1)} %pad_maximum_fusion.17), channel_id=1, source_target_pairs={{0,256},{4,260},{8,264},{12,268},{16,272},{20,276},{24,280},{28,28... | collective-permute-start | bytes 1572872 | tf_op jit(solution)/shard_map/ppermute | solution.py:66
  121.0 8.5 %collective-permute-done.6 = bf16[64,32,128]{2,1,0:T(8,128)(2,1)S(1)} collective-permute-done((bf16[64,32,128]{2,1,0:T(8,128)(2,1)S(1)}, bf16[64,32,128]{2,1,0:T(8,128)(2,1)S(1)}, u32[]{:S(2)}, u32[]{:S(2)}) %collective-permute-start.6) | collective-permute-done | bytes 524320 | tf_op jit(solution)/shard_map/ppermute | solution.py:66
  164.3 2.4 fusion.146
  166.6 13.7 %psum.7 = f32[4,256]{1,0:T(4,128)S(1)} all-reduce(f32[4,256]{1,0:T(4,128)S(1)} %pad_maximum_fusion.38), channel_id=1, replica_groups=mesh['seq'=128,'head'=4] {'head'}, use_global_device_ids=true, to_apply=%region_24.25 | all-reduce | flops 1024 | bytes 8192 | tf_op jit(solution)/shard_map/psum | solution.py:187
  186.8 2.7 collective-permute-start.7
  191.6 2.5 collective-permute-done.7
  199.6 10.6 %collective-permute-start.9 = (bf16[4,176,128]{2,1,0:T(8,128)(2,1)S(1)}, bf16[4,176,128]{2,1,0:T(8,128)(2,1)}, u32[]{:S(2)}, u32[]{:S(2)}) collective-permute-start(bf16[4,176,128]{2,1,0:T(8,128)(2,1)S(1)} %pad_maximum_fusion.31), channel_id=1, source_target_pairs={{0,32},{4,36},{8,40},{12,44},{16,48},{20,52},{24,56},{28,60},{32,0... | collective-permute-start | bytes 540680 | tf_op jit(solution)/shard_map/ppermute | solution.py:66
  212.0 5.7 %collective-permute-done.9 = bf16[4,176,128]{2,1,0:T(8,128)(2,1)} collective-permute-done((bf16[4,176,128]{2,1,0:T(8,128)(2,1)S(1)}, bf16[4,176,128]{2,1,0:T(8,128)(2,1)}, u32[]{:S(2)}, u32[]{:S(2)}) %collective-permute-start.9) | collective-permute-done | bytes 180256 | tf_op jit(solution)/shard_map/ppermute | solution.py:66
  219.4 3.0 collective-permute-start.10
  228.0 5.3 %collective-permute-done.10 = bf16[8,176,128]{2,1,0:T(8,128)(2,1)} collective-permute-done((bf16[8,176,128]{2,1,0:T(8,128)(2,1)}, bf16[8,176,128]{2,1,0:T(8,128)(2,1)}, u32[]{:S(2)}, u32[]{:S(2)}) %collective-permute-start.10) | collective-permute-done | bytes 360480 | tf_op jit(solution)/shard_map/ppermute | solution.py:66
  234.2 12.9 %collective-permute-start.11 = (bf16[16,48,128]{2,1,0:T(8,128)(2,1)S(1)}, bf16[16,48,128]{2,1,0:T(8,128)(2,1)S(1)}, u32[]{:S(2)}, u32[]{:S(2)}) collective-permute-start(bf16[16,48,128]{2,1,0:T(8,128)(2,1)S(1)} %pad_maximum_fusion.30), channel_id=1, source_target_pairs={{0,128},{4,132},{8,136},{12,140},{16,144},{20,148},{24,152},{28,15... | collective-permute-start | bytes 589832 | tf_op jit(solution)/shard_map/ppermute | solution.py:66
  249.9 5.2 %collective-permute-done.11 = bf16[16,48,128]{2,1,0:T(8,128)(2,1)S(1)} collective-permute-done((bf16[16,48,128]{2,1,0:T(8,128)(2,1)S(1)}, bf16[16,48,128]{2,1,0:T(8,128)(2,1)S(1)}, u32[]{:S(2)}, u32[]{:S(2)}) %collective-permute-start.11) | collective-permute-done | bytes 196640 | tf_op jit(solution)/shard_map/ppermute | solution.py:66
  256.6 2.6 collective-permute-start.12
  259.2 2.3 fusion.43
  263.6 5.1 %collective-permute-done.12 = bf16[32,48,128]{2,1,0:T(8,128)(2,1)} collective-permute-done((bf16[32,48,128]{2,1,0:T(8,128)(2,1)}, bf16[32,48,128]{2,1,0:T(8,128)(2,1)}, u32[]{:S(2)}, u32[]{:S(2)}) %collective-permute-start.12) | collective-permute-done | bytes 393248 | tf_op jit(solution)/shard_map/ppermute | solution.py:66
  269.7 9.1 %collective-permute-start.13 = (bf16[64,16,128]{2,1,0:T(8,128)(2,1)S(1)}, bf16[64,16,128]{2,1,0:T(8,128)(2,1)S(1)}, u32[]{:S(2)}, u32[]{:S(2)}) collective-permute-start(bf16[64,16,128]{2,1,0:T(8,128)(2,1)S(1)} %pad_maximum_fusion.28), channel_id=1, source_target_pairs={{0,256},{4,260},{8,264},{12,268},{16,272},{20,276},{24,280},{28,28... | collective-permute-start | bytes 786440 | tf_op jit(solution)/shard_map/ppermute | solution.py:66
  282.7 3.3 collective-permute-done.13
  286.9 2.8 collective-permute-start.14
  289.8 2.2 fusion.57
  292.0 2.5 collective-permute-done.14
  297.2 2.5 fusion.63
  309.5 2.8 fusion.31
  314.0 2.0 copy.253
  317.7 6.7 %collective-permute-start.16 = (bf16[4,224,128]{2,1,0:T(8,128)(2,1)S(1)}, bf16[4,224,128]{2,1,0:T(8,128)(2,1)S(1)}, u32[]{:S(2)}, u32[]{:S(2)}) collective-permute-start(bf16[4,224,128]{2,1,0:T(8,128)(2,1)S(1)} %pad_maximum_fusion.29), channel_id=1, source_target_pairs={{0,32},{4,36},{8,40},{12,44},{16,48},{20,52},{24,56},{28,60},{32,0... | collective-permute-start | bytes 688136 | tf_op jit(solution)/shard_map/ppermute | solution.py:66
  326.0 10.4 %collective-permute-done.16 = bf16[4,224,128]{2,1,0:T(8,128)(2,1)S(1)} collective-permute-done((bf16[4,224,128]{2,1,0:T(8,128)(2,1)S(1)}, bf16[4,224,128]{2,1,0:T(8,128)(2,1)S(1)}, u32[]{:S(2)}, u32[]{:S(2)}) %collective-permute-start.16) | collective-permute-done | bytes 229408 | tf_op jit(solution)/shard_map/ppermute | solution.py:66
  336.5 3.4 collective-permute-start.17
  342.4 9.6 %collective-permute-done.17 = bf16[8,224,128]{2,1,0:T(8,128)(2,1)S(1)} collective-permute-done((bf16[8,224,128]{2,1,0:T(8,128)(2,1)S(1)}, bf16[8,224,128]{2,1,0:T(8,128)(2,1)S(1)}, u32[]{:S(2)}, u32[]{:S(2)}) %collective-permute-start.17) | collective-permute-done | bytes 458784 | tf_op jit(solution)/shard_map/ppermute | solution.py:66
  352.0 9.0 %collective-permute-start.18 = (bf16[16,80,128]{2,1,0:T(8,128)(2,1)S(1)}, bf16[16,80,128]{2,1,0:T(8,128)(2,1)}, u32[]{:S(2)}, u32[]{:S(2)}) collective-permute-start(bf16[16,80,128]{2,1,0:T(8,128)(2,1)S(1)} %pad_maximum_fusion.26), channel_id=1, source_target_pairs={{0,128},{4,132},{8,136},{12,140},{16,144},{20,148},{24,152},{28,15... | collective-permute-start | bytes 983048 | tf_op jit(solution)/shard_map/ppermute | solution.py:66
  364.5 9.5 %collective-permute-done.18 = bf16[16,80,128]{2,1,0:T(8,128)(2,1)} collective-permute-done((bf16[16,80,128]{2,1,0:T(8,128)(2,1)S(1)}, bf16[16,80,128]{2,1,0:T(8,128)(2,1)}, u32[]{:S(2)}, u32[]{:S(2)}) %collective-permute-start.18) | collective-permute-done | bytes 327712 | tf_op jit(solution)/shard_map/ppermute | solution.py:66
  377.8 2.2 fusion.6
  380.0 2.3 fusion.45
  387.9 6.9 %collective-permute-done.19 = bf16[32,80,128]{2,1,0:T(8,128)(2,1)} collective-permute-done((bf16[32,80,128]{2,1,0:T(8,128)(2,1)}, bf16[32,80,128]{2,1,0:T(8,128)(2,1)}, u32[]{:S(2)}, u32[]{:S(2)}) %collective-permute-start.19) | collective-permute-done | bytes 655392 | tf_op jit(solution)/shard_map/ppermute | solution.py:66
  394.7 2.0 pad_maximum_fusion.16
  396.7 7.5 %collective-permute-start.20 = (bf16[64,32,128]{2,1,0:T(8,128)(2,1)}, bf16[64,32,128]{2,1,0:T(8,128)(2,1)}, u32[]{:S(2)}, u32[]{:S(2)}) collective-permute-start(bf16[64,32,128]{2,1,0:T(8,128)(2,1)} %get-tuple-element.65), channel_id=1, source_target_pairs={{0,256},{4,260},{8,264},{12,268},{16,272},{20,276},{24,280},{28,28... | collective-permute-start | bytes 1572872 | tf_op jit(solution)/shard_map/ppermute | solution.py:66
  415.2 12.2 %collective-permute-done.20 = bf16[64,32,128]{2,1,0:T(8,128)(2,1)} collective-permute-done((bf16[64,32,128]{2,1,0:T(8,128)(2,1)}, bf16[64,32,128]{2,1,0:T(8,128)(2,1)}, u32[]{:S(2)}, u32[]{:S(2)}) %collective-permute-start.20) | collective-permute-done | bytes 524320 | tf_op jit(solution)/shard_map/ppermute | solution.py:66
  427.3 2.2 pad_maximum_fusion.13
  435.2 2.2 fusion.61
  439.0 2.6 fusion.30
  (467 shorter events, 151.5 us)
Async XLA Ops:
  2.4 76.2 %copy-start.83 = (pred[4,2]{0,1:T(4,128)(4,1)}, pred[4,2]{0,1:T(4,128)(4,1)S(1)}, u32[]{:S(2)}) copy-start(pred[4,2]{0,1:T(4,128)(4,1)S(1)} %iota_compare_fusion.2) | copy-start | bytes 28
  3.3 19.5 %copy-start.97 = (s32[16]{0:T(128)S(1)}, s32[16]{0:T(128)}, u32[]{:S(2)}) copy-start(s32[16]{0:T(128)} %constant.135.clone) | copy-start | bytes 196
  4.4 70.3 %copy-start.84 = (pred[16,2]{0,1:T(4,128)(4,1)}, pred[16,2]{0,1:T(4,128)(4,1)S(1)}, u32[]{:S(2)}) copy-start(pred[16,2]{0,1:T(4,128)(4,1)S(1)} %iota_compare_fusion.1) | copy-start | bytes 100
  5.8 67.4 %copy-start.85 = (pred[32,2]{0,1:T(4,128)(4,1)}, pred[32,2]{0,1:T(4,128)(4,1)S(1)}, u32[]{:S(2)}) copy-start(pred[32,2]{0,1:T(4,128)(4,1)S(1)} %iota_compare_fusion) | copy-start | bytes 196
  8.3 24.5 %copy-start.96 = (s32[4]{0:T(128)S(1)}, s32[4]{0:T(128)}, u32[]{:S(2)}) copy-start(s32[4]{0:T(128)} %constant.134.clone) | copy-start | bytes 52
  8.8 11.9 %collective-permute-start = (bf16[1,1376,128]{2,1,0:T(8,128)(2,1)S(1)}, bf16[1,1376,128]{2,1,0:T(8,128)(2,1)S(1)}, u32[]{:S(2)}, u32[]{:S(2)}) collective-permute-start(bf16[1,1376,128]{2,1,0:T(8,128)(2,1)S(1)} %bitcast.329), channel_id=1, source_target_pairs={{0,8},{4,12},{8,0},{12,4},{16,24},{20,28},{24,16},{28,20},{32,40},... | collective-permute-start | bytes 1056776 | tf_op jit(solution)/shard_map/ppermute | solution.py:66
  20.8 4.1 collective-permute-start.1
  24.8 29.4 %copy-start.12 = (bf16[2,1376,128]{2,1,0:T(8,128)(2,1)}, bf16[2,1376,128]{2,1,0:T(8,128)(2,1)S(1)}, u32[]{:S(2)}) copy-start(bf16[2,1376,128]{2,1,0:T(8,128)(2,1)S(1)} %collective-permute-done.1) | copy-start | bytes 2113540
  24.9 53.0 %copy-start.40 = (bf16[256,2,128]{2,1,0:T(2,128)(2,1)S(1)}, bf16[256,2,128]{2,1,0:T(2,128)(2,1)}, u32[]{:S(2)}) copy-start(bf16[256,2,128]{2,1,0:T(2,128)(2,1)} %param.13) | copy-start | bytes 393220
  24.9 20.2 %collective-permute-start.2 = (bf16[4,352,128]{2,1,0:T(8,128)(2,1)S(1)}, bf16[4,352,128]{2,1,0:T(8,128)(2,1)S(1)}, u32[]{:S(2)}, u32[]{:S(2)}) collective-permute-start(bf16[4,352,128]{2,1,0:T(8,128)(2,1)S(1)} %pad_maximum_fusion.23), channel_id=1, source_target_pairs={{0,32},{4,36},{8,40},{12,44},{16,48},{20,52},{24,56},{28,60},{32,0... | collective-permute-start | bytes 1081352 | tf_op jit(solution)/shard_map/ppermute | solution.py:66
  46.0 21.7 %collective-permute-start.3 = (bf16[8,352,128]{2,1,0:T(8,128)(2,1)}, bf16[8,352,128]{2,1,0:T(8,128)(2,1)S(1)}, u32[]{:S(2)}, u32[]{:S(2)}) collective-permute-start(bf16[8,352,128]{2,1,0:T(8,128)(2,1)} %pad_maximum_fusion.8), channel_id=1, source_target_pairs={{0,16},{4,20},{8,24},{12,28},{16,0},{20,4},{24,8},{28,12},{32,48},... | collective-permute-start | bytes 2162696 | tf_op jit(solution)/shard_map/ppermute | solution.py:66
  67.7 21.5 %collective-permute-start.4 = (bf16[16,96,128]{2,1,0:T(8,128)(2,1)S(1)}, bf16[16,96,128]{2,1,0:T(8,128)(2,1)S(1)}, u32[]{:S(2)}, u32[]{:S(2)}) collective-permute-start(bf16[16,96,128]{2,1,0:T(8,128)(2,1)S(1)} %pad_maximum_fusion.20), channel_id=1, source_target_pairs={{0,128},{4,132},{8,136},{12,140},{16,144},{20,148},{24,152},{28,15... | collective-permute-start | bytes 1179656 | tf_op jit(solution)/shard_map/ppermute | solution.py:66
  74.0 90.2 %copy-start.52 = (pred[256,2]{0,1:T(4,128)(4,1)}, pred[256,2]{0,1:T(4,128)(4,1)S(1)}, u32[]{:S(2)}) copy-start(pred[256,2]{0,1:T(4,128)(4,1)S(1)} %broadcast_in_dim.631) | copy-start | bytes 1540
  79.5 39.8 %copy-start.13 = (bf16[2,1376,128]{2,1,0:T(8,128)(2,1)S(1)}, bf16[2,1376,128]{2,1,0:T(8,128)(2,1)}, u32[]{:S(2)}) copy-start(bf16[2,1376,128]{2,1,0:T(8,128)(2,1)} %copy-done.12) | copy-start | bytes 2113540
  89.3 20.5 %copy-start.7 = (bf16[16,96,128]{2,1,0:T(8,128)(2,1)}, bf16[16,96,128]{2,1,0:T(8,128)(2,1)S(1)}, u32[]{:S(2)}) copy-start(bf16[16,96,128]{2,1,0:T(8,128)(2,1)S(1)} %collective-permute-done.4) | copy-start | bytes 1179652
  89.3 20.3 %collective-permute-start.5 = (bf16[32,96,128]{2,1,0:T(8,128)(2,1)S(1)}, bf16[32,96,128]{2,1,0:T(8,128)(2,1)S(1)}, u32[]{:S(2)}, u32[]{:S(2)}) collective-permute-start(bf16[32,96,128]{2,1,0:T(8,128)(2,1)S(1)} %pad_maximum_fusion.5), channel_id=1, source_target_pairs={{0,64},{4,68},{8,72},{12,76},{16,80},{20,84},{24,88},{28,92},{32,9... | collective-permute-start | bytes 2359304 | tf_op jit(solution)/shard_map/ppermute | solution.py:66
  109.7 19.8 %collective-permute-start.6 = (bf16[64,32,128]{2,1,0:T(8,128)(2,1)S(1)}, bf16[64,32,128]{2,1,0:T(8,128)(2,1)S(1)}, u32[]{:S(2)}, u32[]{:S(2)}) collective-permute-start(bf16[64,32,128]{2,1,0:T(8,128)(2,1)S(1)} %pad_maximum_fusion.17), channel_id=1, source_target_pairs={{0,256},{4,260},{8,264},{12,268},{16,272},{20,276},{24,280},{28,28... | collective-permute-start | bytes 1572872 | tf_op jit(solution)/shard_map/ppermute | solution.py:66
  146.0 18.3 %copy-start.61 = (f32[256,2]{0,1:T(2,128)}, f32[256,2]{0,1:T(2,128)S(1)}, u32[]{:S(2)}) copy-start(f32[256,2]{0,1:T(2,128)S(1)} %get-tuple-element.62) | copy-start | bytes 6148
  164.3 21.6 %copy-start.72 = (f32[16,2]{0,1:T(2,128)S(1)}, f32[16,2]{0,1:T(2,128)}, u32[]{:S(2)}) copy-start(f32[16,2]{0,1:T(2,128)} %copy-done.71) | copy-start | bytes 388
  164.3 21.8 %copy-start.42 = (bf16[64,2,128]{2,1,0:T(2,128)(2,1)S(1)}, bf16[64,2,128]{2,1,0:T(2,128)(2,1)}, u32[]{:S(2)}) copy-start(bf16[64,2,128]{2,1,0:T(2,128)(2,1)} %copy.200) | copy-start | bytes 98308
  181.6 29.3 %copy-start.43 = (f32[256,2]{0,1:T(2,128)}, f32[256,2]{0,1:T(2,128)S(1)}, u32[]{:S(2)}) copy-start(f32[256,2]{0,1:T(2,128)S(1)} %get-tuple-element.60) | copy-start | bytes 6148
  186.8 41.3 %copy-start.14 = (bf16[1,688,128]{2,1,0:T(8,128)(2,1)}, bf16[1,688,128]{2,1,0:T(8,128)(2,1)S(1)}, u32[]{:S(2)}) copy-start(bf16[1,688,128]{2,1,0:T(8,128)(2,1)S(1)} %maximum_bitcast_fusion.1) | copy-start | bytes 528388
  186.8 7.3 %collective-permute-start.7 = (bf16[1,688,128]{2,1,0:T(8,128)(2,1)S(1)}, bf16[1,688,128]{2,1,0:T(8,128)(2,1)S(1)}, u32[]{:S(2)}, u32[]{:S(2)}) collective-permute-start(bf16[1,688,128]{2,1,0:T(8,128)(2,1)S(1)} %maximum_bitcast_fusion.1), channel_id=1, source_target_pairs={{0,8},{4,12},{8,0},{12,4},{16,24},{20,28},{24,16},{28,20},{32,40},... | collective-permute-start | bytes 528392 | tf_op jit(solution)/shard_map/ppermute | solution.py:66
  194.2 4.7 %collective-permute-start.8 = (bf16[2,688,128]{2,1,0:T(8,128)(2,1)S(1)}, bf16[2,688,128]{2,1,0:T(8,128)(2,1)S(1)}, u32[]{:S(2)}, u32[]{:S(2)}) collective-permute-start(bf16[2,688,128]{2,1,0:T(8,128)(2,1)S(1)} %pad_maximum_fusion.25), channel_id=1, source_target_pairs={{0,4},{4,0},{8,12},{12,8},{16,20},{20,16},{24,28},{28,24},{32,36},... | collective-permute-start | bytes 1056776 | tf_op jit(solution)/shard_map/ppermute | solution.py:66
  197.8 30.2 %copy-start.81 = (bf16[8,2,128]{2,0,1:T(8,128)(2,1)}, bf16[8,2,128]{2,0,1:T(8,128)(2,1)S(1)}, u32[]{:S(2)}) copy-start(bf16[8,2,128]{2,0,1:T(8,128)(2,1)S(1)} %select_reduce_fusion) | copy-start | bytes 12292
  198.8 29.2 %copy-start.45 = (bf16[16,2,128]{2,0,1:T(8,128)(2,1)}, bf16[16,2,128]{2,0,1:T(8,128)(2,1)S(1)}, u32[]{:S(2)}) copy-start(bf16[16,2,128]{2,0,1:T(8,128)(2,1)S(1)} %select_reduce_fusion.1) | copy-start | bytes 24580
  199.6 18.1 %collective-permute-start.9 = (bf16[4,176,128]{2,1,0:T(8,128)(2,1)S(1)}, bf16[4,176,128]{2,1,0:T(8,128)(2,1)}, u32[]{:S(2)}, u32[]{:S(2)}) collective-permute-start(bf16[4,176,128]{2,1,0:T(8,128)(2,1)S(1)} %pad_maximum_fusion.31), channel_id=1, source_target_pairs={{0,32},{4,36},{8,40},{12,44},{16,48},{20,52},{24,56},{28,60},{32,0... | collective-permute-start | bytes 540680 | tf_op jit(solution)/shard_map/ppermute | solution.py:66
  219.4 13.9 %collective-permute-start.10 = (bf16[8,176,128]{2,1,0:T(8,128)(2,1)}, bf16[8,176,128]{2,1,0:T(8,128)(2,1)}, u32[]{:S(2)}, u32[]{:S(2)}) collective-permute-start(bf16[8,176,128]{2,1,0:T(8,128)(2,1)} %pad_maximum_fusion.24), channel_id=1, source_target_pairs={{0,16},{4,20},{8,24},{12,28},{16,0},{20,4},{24,8},{28,12},{32,48},... | collective-permute-start | bytes 1081352 | tf_op jit(solution)/shard_map/ppermute | solution.py:66
  234.2 20.9 %collective-permute-start.11 = (bf16[16,48,128]{2,1,0:T(8,128)(2,1)S(1)}, bf16[16,48,128]{2,1,0:T(8,128)(2,1)S(1)}, u32[]{:S(2)}, u32[]{:S(2)}) collective-permute-start(bf16[16,48,128]{2,1,0:T(8,128)(2,1)S(1)} %pad_maximum_fusion.30), channel_id=1, source_target_pairs={{0,128},{4,132},{8,136},{12,140},{16,144},{20,148},{24,152},{28,15... | collective-permute-start | bytes 589832 | tf_op jit(solution)/shard_map/ppermute | solution.py:66
  256.6 12.1 %collective-permute-start.12 = (bf16[32,48,128]{2,1,0:T(8,128)(2,1)}, bf16[32,48,128]{2,1,0:T(8,128)(2,1)}, u32[]{:S(2)}, u32[]{:S(2)}) collective-permute-start(bf16[32,48,128]{2,1,0:T(8,128)(2,1)} %pad_maximum_fusion.21), channel_id=1, source_target_pairs={{0,64},{4,68},{8,72},{12,76},{16,80},{20,84},{24,88},{28,92},{32,9... | collective-permute-start | bytes 1179656 | tf_op jit(solution)/shard_map/ppermute | solution.py:66
  269.7 16.4 %collective-permute-start.13 = (bf16[64,16,128]{2,1,0:T(8,128)(2,1)S(1)}, bf16[64,16,128]{2,1,0:T(8,128)(2,1)S(1)}, u32[]{:S(2)}, u32[]{:S(2)}) collective-permute-start(bf16[64,16,128]{2,1,0:T(8,128)(2,1)S(1)} %pad_maximum_fusion.28), channel_id=1, source_target_pairs={{0,256},{4,260},{8,264},{12,268},{16,272},{20,276},{24,280},{28,28... | collective-permute-start | bytes 786440 | tf_op jit(solution)/shard_map/ppermute | solution.py:66
  286.9 7.6 %collective-permute-start.14 = (bf16[1,768,128]{2,1,0:T(8,128)(2,1)S(1)}, bf16[1,768,128]{2,1,0:T(8,128)(2,1)S(1)}, u32[]{:S(2)}, u32[]{:S(2)}) collective-permute-start(bf16[1,768,128]{2,1,0:T(8,128)(2,1)S(1)} %maximum_bitcast_fusion), channel_id=1, source_target_pairs={{0,8},{4,12},{8,0},{12,4},{16,24},{20,28},{24,16},{28,20},{32,40},... | collective-permute-start | bytes 589832 | tf_op jit(solution)/shard_map/ppermute | solution.py:66
  292.0 17.5 %copy-start.24 = (bf16[256,2,128]{0,2,1:T(8,128)(2,1)S(1)}, bf16[256,2,128]{0,2,1:T(8,128)(2,1)}, u32[]{:S(2)}) copy-start(bf16[256,2,128]{0,2,1:T(8,128)(2,1)} %copy-done.23) | copy-start | bytes 393220
  292.0 17.5 %copy-start.44 = (f32[256,2]{0,1:T(2,128)S(1)}, f32[256,2]{0,1:T(2,128)}, u32[]{:S(2)}) copy-start(f32[256,2]{0,1:T(2,128)} %copy-done.43) | copy-start | bytes 6148
  292.0 17.5 %copy-start.53 = (pred[256,2]{0,1:T(4,128)(4,1)S(1)}, pred[256,2]{0,1:T(4,128)(4,1)}, u32[]{:S(2)}) copy-start(pred[256,2]{0,1:T(4,128)(4,1)} %copy-done.52) | copy-start | bytes 1540
  292.0 17.5 %copy-start.56 = (pred[256,2]{0,1:T(4,128)(4,1)S(1)}, pred[256,2]{0,1:T(4,128)(4,1)}, u32[]{:S(2)}) copy-start(pred[256,2]{0,1:T(4,128)(4,1)} %broadcast_in_dim.625) | copy-start | bytes 1540
  292.0 17.5 %copy-start.59 = (pred[256,2]{0,1:T(4,128)(4,1)S(1)}, pred[256,2]{0,1:T(4,128)(4,1)}, u32[]{:S(2)}) copy-start(pred[256,2]{0,1:T(4,128)(4,1)} %broadcast_in_dim.618) | copy-start | bytes 1540
  295.3 20.7 %collective-permute-start.15 = (bf16[2,768,128]{2,1,0:T(8,128)(2,1)}, bf16[2,768,128]{2,1,0:T(8,128)(2,1)S(1)}, u32[]{:S(2)}, u32[]{:S(2)}) collective-permute-start(bf16[2,768,128]{2,1,0:T(8,128)(2,1)} %pad_maximum_fusion.22), channel_id=1, source_target_pairs={{0,4},{4,0},{8,12},{12,8},{16,20},{20,16},{24,28},{28,24},{32,36},... | collective-permute-start | bytes 1179656 | tf_op jit(solution)/shard_map/ppermute | solution.py:66
  317.7 18.8 %collective-permute-start.16 = (bf16[4,224,128]{2,1,0:T(8,128)(2,1)S(1)}, bf16[4,224,128]{2,1,0:T(8,128)(2,1)S(1)}, u32[]{:S(2)}, u32[]{:S(2)}) collective-permute-start(bf16[4,224,128]{2,1,0:T(8,128)(2,1)S(1)} %pad_maximum_fusion.29), channel_id=1, source_target_pairs={{0,32},{4,36},{8,40},{12,44},{16,48},{20,52},{24,56},{28,60},{32,0... | collective-permute-start | bytes 688136 | tf_op jit(solution)/shard_map/ppermute | solution.py:66
  336.5 15.5 %collective-permute-start.17 = (bf16[8,224,128]{2,1,0:T(8,128)(2,1)S(1)}, bf16[8,224,128]{2,1,0:T(8,128)(2,1)S(1)}, u32[]{:S(2)}, u32[]{:S(2)}) collective-permute-start(bf16[8,224,128]{2,1,0:T(8,128)(2,1)S(1)} %pad_maximum_fusion.19), channel_id=1, source_target_pairs={{0,16},{4,20},{8,24},{12,28},{16,0},{20,4},{24,8},{28,12},{32,48},... | collective-permute-start | bytes 1376264 | tf_op jit(solution)/shard_map/ppermute | solution.py:66
  352.0 22.0 %collective-permute-start.18 = (bf16[16,80,128]{2,1,0:T(8,128)(2,1)S(1)}, bf16[16,80,128]{2,1,0:T(8,128)(2,1)}, u32[]{:S(2)}, u32[]{:S(2)}) collective-permute-start(bf16[16,80,128]{2,1,0:T(8,128)(2,1)S(1)} %pad_maximum_fusion.26), channel_id=1, source_target_pairs={{0,128},{4,132},{8,136},{12,140},{16,144},{20,148},{24,152},{28,15... | collective-permute-start | bytes 983048 | tf_op jit(solution)/shard_map/ppermute | solution.py:66
  363.7 16.3 %copy-start.35 = (bf16[64,2,128]{2,0,1:T(8,128)(2,1)S(1)}, bf16[64,2,128]{2,0,1:T(8,128)(2,1)}, u32[]{:S(2)}) copy-start(bf16[64,2,128]{2,0,1:T(8,128)(2,1)} %copy-done.34) | copy-start | bytes 98308
  375.9 18.9 %collective-permute-start.19 = (bf16[32,80,128]{2,1,0:T(8,128)(2,1)}, bf16[32,80,128]{2,1,0:T(8,128)(2,1)}, u32[]{:S(2)}, u32[]{:S(2)}) collective-permute-start(bf16[32,80,128]{2,1,0:T(8,128)(2,1)} %pad_maximum_fusion.12), channel_id=1, source_target_pairs={{0,64},{4,68},{8,72},{12,76},{16,80},{20,84},{24,88},{28,92},{32,9... | collective-permute-start | bytes 1966088 | tf_op jit(solution)/shard_map/ppermute | solution.py:66
  387.9 21.1 %copy-start.67 = (bf16[16,2,128]{2,0,1:T(8,128)(2,1)S(1)}, bf16[16,2,128]{2,0,1:T(8,128)(2,1)}, u32[]{:S(2)}) copy-start(bf16[16,2,128]{2,0,1:T(8,128)(2,1)} %copy-done.66) | copy-start | bytes 24580
  387.9 21.1 %copy-start.82 = (pred[1024,16]{0,1:T(8,128)(4,1)S(1)}, pred[1024,16]{0,1:T(8,128)(4,1)}, u32[]{:S(2)}) copy-start(pred[1024,16]{0,1:T(8,128)(4,1)} %broadcast_compare_fusion.4) | copy-start | bytes 49156
  396.7 30.6 %collective-permute-start.20 = (bf16[64,32,128]{2,1,0:T(8,128)(2,1)}, bf16[64,32,128]{2,1,0:T(8,128)(2,1)}, u32[]{:S(2)}, u32[]{:S(2)}) collective-permute-start(bf16[64,32,128]{2,1,0:T(8,128)(2,1)} %get-tuple-element.65), channel_id=1, source_target_pairs={{0,256},{4,260},{8,264},{12,268},{16,272},{20,276},{24,280},{28,28... | collective-permute-start | bytes 1572872 | tf_op jit(solution)/shard_map/ppermute | solution.py:66
  415.2 16.9 %copy-start.78 = (bf16[8,2,128]{2,0,1:T(8,128)(2,1)S(1)}, bf16[8,2,128]{2,0,1:T(8,128)(2,1)}, u32[]{:S(2)}) copy-start(bf16[8,2,128]{2,0,1:T(8,128)(2,1)} %copy-done.77) | copy-start | bytes 12292
  415.2 16.9 %copy-start.92 = (pred[1024,8]{0,1:T(8,128)(4,1)S(1)}, pred[1024,8]{0,1:T(8,128)(4,1)}, u32[]{:S(2)}) copy-start(pred[1024,8]{0,1:T(8,128)(4,1)} %broadcast_compare_fusion.6) | copy-start | bytes 24580
  (75 other events, 375.8 us)

commit v2 on v0

--- a/solution.py
+++ b/solution.py
@@ -128,29 +128,16 @@
     for level in levels:
         level["owner"] = level["spot"] ^ jnp.asarray(spread(order, level["span"]))
 
-    key_sets = extend(
-        [
-            jnp.concatenate(
-                [
-                    level["key_sel"].reshape(-1, lane),
-                    level["value_sel"].reshape(-1, lane),
-                ],
-                axis=0,
-            )
-            for level in levels
-        ],
-        spans,
-        order,
-    )
+    key_sets = extend([level["key_sel"].reshape(-1, lane) for level in levels], spans, order)
+    value_sets = extend([level["value_sel"].reshape(-1, lane) for level in levels], spans, order)
     query_sets = extend([level["query_sel"].reshape(-1, lane) for level in levels], spans, order)
 
     lse_total = jnp.full((tok_dev, heads_dev), neg_fill, jnp.float32)
-    for level, key_set in zip(levels, key_sets):
+    for level, key_set, value_set in zip(levels, key_sets, value_sets):
         span, rows = level["span"], level["rows"]
-        paired = key_set.reshape(span, 2, rows, heads_dev, head_size)
-        keys = paired[:, 0].reshape(span * rows, heads_dev, head_size)
+        keys = key_set.reshape(span * rows, heads_dev, head_size)
         level["key_all"] = keys
-        level["value_all"] = paired[:, 1].reshape(span * rows, heads_dev, head_size)
+        level["value_all"] = value_set.reshape(span * rows, heads_dev, head_size)
         raw = (
             jnp.einsum("qhd,khd->hqk", level["query_sel"], keys, preferred_element_type=jnp.float32)
             * score_scale
@@ -206,14 +193,14 @@
 
     query_grad = jnp.zeros((tok_dev, heads_dev, head_size), jnp.float32)
     back_sets = []
+    other_sets = []
     for level in levels:
         dout_sel = pick_rows(d_attended, level["wanted"], level["stride"])
         delta_sel = pick_rows(row_delta, level["wanted"], level["stride"])
         back_sets.append(
-            jnp.concatenate(
-                [dout_sel.reshape(-1, lane), pack_stats(level["lse_sel"], delta_sel)], axis=0
-            )
-        )
+            jnp.concatenate([dout_sel[:, 0], pack_stats(level["lse_sel"], delta_sel)], axis=0)
+        )
+        other_sets.append(dout_sel[:, 1:].reshape(-1, lane))
         weight_grad = jnp.einsum(
             "qhd,khd->hqk", dout_sel, level["value_all"], preferred_element_type=jnp.float32
         )
@@ -227,17 +214,22 @@
             grad_sel * score_scale, level["wanted"], level["stride"], 0.0
         )
     back_sets = extend(back_sets, spans, order)
+    other_sets = extend(other_sets, spans, order)
 
     key_grad = jnp.zeros((tok_dev, heads_dev, head_size), jnp.float32)
     value_grad = jnp.zeros((tok_dev, heads_dev, head_size), jnp.float32)
-    for level, query_set, back_set in zip(levels, query_sets, back_sets):
+    for level, query_set, back_set, other_set in zip(levels, query_sets, back_sets, other_sets):
         span, rows = level["span"], level["rows"]
         queries = query_set.reshape(span * rows, heads_dev, head_size)
         back_slots = back_set.reshape(span, -1, lane)
-        dout_all = back_slots[:, : rows * heads_dev].reshape(span * rows, heads_dev, head_size)
-        lse_all, delta_all = unpack_stats(
-            back_slots[:, rows * heads_dev :], span, rows, heads_dev
-        )
+        dout_all = jnp.concatenate(
+            [
+                back_slots[:, :rows].reshape(span, rows, 1, head_size),
+                other_set.reshape(span, rows, heads_dev - 1, head_size),
+            ],
+            axis=2,
+        ).reshape(span * rows, heads_dev, head_size)
+        lse_all, delta_all = unpack_stats(back_slots[:, rows:], span, rows, heads_dev)
         raw = (
             jnp.einsum(
                 "qhd,khd->hqk", queries, level["key_sel"], preferred_element_type=jnp.float32

time: 377 us -> 417 us (1.11)
  the two profiles are of different devices: /device:TPU:201 before, /device:TPU:6 now
where the time goes in v2:
time: 417 us; the launch traced here: 413 us
  starting transfers between devices  154 us (37%)
  local copies, waits for them, and re-layouts  84.7 us (20%)
  other arithmetic  68.7 us (16%)
  waiting for transfers between devices  58.6 us (14%)
  matrix products  34.4 us (8%)
  blocking collectives  9.4 us (2%)
    ppermute x35, starting transfers between devices, extend(): lax.ppermute(state, 'seq', [(source, source ^ offset) for source in range...  154 us
    ppermute x35, waiting for transfers between devices, extend(): lax.ppermute(state, 'seq', [(source, source ^ offset) for source in range...  58.6 us
    concatenate x34, other arithmetic, extend(): state = jnp.concatenate([state, moved], axis=0)  29.3 us
    broadcast_in_dim x45, local copies, waits for them, and re-layouts, put_rows(): jnp.where(column == target, compact[:, None], jnp.asarray(filler, compact...  28.4 us
    unnamed x207, local copies, waits for them, and re-layouts  19.7 us
    reduce_sum x12, other arithmetic, pick_rows(): return jnp.sum(zeroed, axis=1, dtype=source.dtype)  12 us
    slice x14, local copies, waits for them, and re-layouts, extend(): finished[index] = state[:, start:start + sizes[index]]  11.3 us
    psum x1, blocking collectives, shards(): lax.psum(jnp.stack([jnp.sum(attended, axis=(1, 2)), jnp.sum(attended * at...  9.4 us
  transfers between devices with their start and end apart: 35, of which 10 were waited for; matrix products, arithmetic and copies ran while one was open for 39% of the time, Pallas kernels for 0%

profile of v2, /device:TPU:6, one launch (start us, length us, event | category | flops | bytes accessed | tf_op | source)
XLA Modules:
  0.0 412.6 jit_solution(5350876698163633734)
XLA Ops:
  7.9 2.7 collective-permute-start
  10.7 3.1 collective-permute-start.7
  14.0 2.7 collective-permute-start.14
  29.0 2.4 collective-permute-start.1
  34.8 7.7 %collective-permute-start.9 = (bf16[4,176,128]{2,1,0:T(8,128)(2,1)S(1)}, bf16[4,176,128]{2,1,0:T(8,128)(2,1)S(1)}, u32[]{:S(2)}, u32[]{:S(2)}) collective-permute-start(bf16[4,176,128]{2,1,0:T(8,128)(2,1)S(1)} %pad_maximum_fusion.60), channel_id=1, source_target_pairs={{0,32},{4,36},{8,40},{12,44},{16,48},{20,52},{24,56},{28,60},{32,0... | collective-permute-start | bytes 540680 | tf_op jit(solution)/shard_map/ppermute | solution.py:66
  42.6 2.0 collective-permute-start.2
  51.3 2.0 copy.285
  54.2 7.7 %collective-permute-start.20 = (bf16[4,176,128]{2,1,0:T(8,128)(2,1)S(1)}, bf16[4,176,128]{2,1,0:T(8,128)(2,1)S(1)}, u32[]{:S(2)}, u32[]{:S(2)}) collective-permute-start(bf16[4,176,128]{2,1,0:T(8,128)(2,1)S(1)} %pad_maximum_fusion.59), channel_id=1, source_target_pairs={{0,32},{4,36},{8,40},{12,44},{16,48},{20,52},{24,56},{28,60},{32,0... | collective-permute-start | bytes 540680 | tf_op jit(solution)/shard_map/ppermute | solution.py:66
  62.0 3.0 collective-permute-start.10
  66.0 4.3 %collective-permute-start.3 = (bf16[8,176,128]{2,1,0:T(8,128)(2,1)S(1)}, bf16[8,176,128]{2,1,0:T(8,128)(2,1)S(1)}, u32[]{:S(2)}, u32[]{:S(2)}) collective-permute-start(bf16[8,176,128]{2,1,0:T(8,128)(2,1)S(1)} %pad_maximum_fusion.28), channel_id=1, source_target_pairs={{0,16},{4,20},{8,24},{12,28},{16,0},{20,4},{24,8},{28,12},{32,48},... | collective-permute-start | bytes 1081352 | tf_op jit(solution)/shard_map/ppermute | solution.py:66
  71.3 5.9 %collective-permute-start.21 = (bf16[8,176,128]{2,1,0:T(8,128)(2,1)S(1)}, bf16[8,176,128]{2,1,0:T(8,128)(2,1)S(1)}, u32[]{:S(2)}, u32[]{:S(2)}) collective-permute-start(bf16[8,176,128]{2,1,0:T(8,128)(2,1)S(1)} %pad_maximum_fusion.30), channel_id=1, source_target_pairs={{0,16},{4,20},{8,24},{12,28},{16,0},{20,4},{24,8},{28,12},{32,48},... | collective-permute-start | bytes 1081352 | tf_op jit(solution)/shard_map/ppermute | solution.py:66
  77.2 5.6 %collective-permute-start.11 = (bf16[16,48,128]{2,1,0:T(8,128)(2,1)S(1)}, bf16[16,48,128]{2,1,0:T(8,128)(2,1)S(1)}, u32[]{:S(2)}, u32[]{:S(2)}) collective-permute-start(bf16[16,48,128]{2,1,0:T(8,128)(2,1)S(1)} %pad_maximum_fusion.55), channel_id=1, source_target_pairs={{0,128},{4,132},{8,136},{12,140},{16,144},{20,148},{24,152},{28,15... | collective-permute-start | bytes 589832 | tf_op jit(solution)/shard_map/ppermute | solution.py:66
  85.3 6.1 %collective-permute-start.4 = (bf16[16,48,128]{2,1,0:T(8,128)(2,1)S(1)}, bf16[16,48,128]{2,1,0:T(8,128)(2,1)S(1)}, u32[]{:S(2)}, u32[]{:S(2)}) collective-permute-start(bf16[16,48,128]{2,1,0:T(8,128)(2,1)S(1)} %pad_maximum_fusion.56), channel_id=1, source_target_pairs={{0,128},{4,132},{8,136},{12,140},{16,144},{20,148},{24,152},{28,15... | collective-permute-start | bytes 589832 | tf_op jit(solution)/shard_map/ppermute | solution.py:66
  93.2 3.8 collective-permute-start.26
  97.8 4.3 %collective-permute-start.12 = (bf16[32,48,128]{2,1,0:T(8,128)(2,1)}, bf16[32,48,128]{2,1,0:T(8,128)(2,1)}, u32[]{:S(2)}, u32[]{:S(2)}) collective-permute-start(bf16[32,48,128]{2,1,0:T(8,128)(2,1)} %pad_maximum_fusion.24), channel_id=1, source_target_pairs={{0,64},{4,68},{8,72},{12,76},{16,80},{20,84},{24,88},{28,92},{32,9... | collective-permute-start | bytes 1179656 | tf_op jit(solution)/shard_map/ppermute | solution.py:66
  103.7 3.3 collective-permute-start.5
  108.8 1.9 slice.305
  114.5 2.5 collective-permute-start.27
  118.6 10.0 %collective-permute-start.13 = (bf16[64,16,128]{2,1,0:T(8,128)(2,1)}, bf16[64,16,128]{2,1,0:T(8,128)(2,1)}, u32[]{:S(2)}, u32[]{:S(2)}) collective-permute-start(bf16[64,16,128]{2,1,0:T(8,128)(2,1)} %pad_maximum_fusion.50), channel_id=1, source_target_pairs={{0,256},{4,260},{8,264},{12,268},{16,272},{20,276},{24,280},{28,28... | collective-permute-start | bytes 786440 | tf_op jit(solution)/shard_map/ppermute | solution.py:66
  129.6 3.8 collective-permute-start.6
  135.9 2.0 pad_maximum_fusion.2
  140.1 3.3 collective-permute-done.27
  145.2 8.7 %collective-permute-start.32 = (bf16[64,16,128]{2,1,0:T(8,128)(2,1)}, bf16[64,16,128]{2,1,0:T(8,128)(2,1)}, u32[]{:S(2)}, u32[]{:S(2)}) collective-permute-start(bf16[64,16,128]{2,1,0:T(8,128)(2,1)} %pad_maximum_fusion.47), channel_id=1, source_target_pairs={{0,256},{4,260},{8,264},{12,268},{16,272},{20,276},{24,280},{28,28... | collective-permute-start | bytes 786440 | tf_op jit(solution)/shard_map/ppermute | solution.py:66
  173.6 2.3 fusion.158
  175.9 9.4 %psum.7 = f32[4,256]{1,0:T(4,128)S(1)} all-reduce(f32[4,256]{1,0:T(4,128)S(1)} %pad_maximum_fusion.66), channel_id=1, replica_groups=mesh['seq'=128,'head'=4] {'head'}, use_global_device_ids=true, to_apply=%region_24.25 | all-reduce | flops 1024 | bytes 8192 | tf_op jit(solution)/shard_map/psum | solution.py:171
  195.3 2.2 fusion.63
  202.0 2.1 fusion.57
  222.0 3.1 collective-permute-start.16
  231.0 2.7 collective-permute-start.18
  233.7 2.6 fusion.31
  238.8 1.9 collective-permute-start.19
  245.2 2.4 collective-permute-start.17
  249.8 3.0 collective-permute-start.24
  254.9 6.8 %collective-permute-start.22 = (bf16[4,136,128]{1,2,0:T(8,128)(2,1)S(1)}, bf16[4,136,128]{1,2,0:T(8,128)(2,1)S(1)}, u32[]{:S(2)}, u32[]{:S(2)}) collective-permute-start(bf16[4,136,128]{1,2,0:T(8,128)(2,1)S(1)} %slice.329), channel_id=1, source_target_pairs={{0,32},{4,36},{8,40},{12,44},{16,48},{20,52},{24,56},{28,60},{32,0... | collective-permute-start | bytes 417800 | tf_op jit(solution)/shard_map/ppermute | solution.py:66
  262.4 5.4 %collective-permute-start.25 = (bf16[8,88,128]{1,2,0:T(8,128)(2,1)S(1)}, bf16[8,88,128]{1,2,0:T(8,128)(2,1)S(1)}, u32[]{:S(2)}, u32[]{:S(2)}) collective-permute-start(bf16[8,88,128]{1,2,0:T(8,128)(2,1)S(1)} %pad_maximum_fusion.53), channel_id=1, source_target_pairs={{0,16},{4,20},{8,24},{12,28},{16,0},{20,4},{24,8},{28,12},{32,48},... | collective-permute-start | bytes 540680 | tf_op jit(solution)/shard_map/ppermute | solution.py:66
  268.4 6.0 %collective-permute-done.22 = bf16[4,136,128]{1,2,0:T(8,128)(2,1)S(1)} collective-permute-done((bf16[4,136,128]{1,2,0:T(8,128)(2,1)S(1)}, bf16[4,136,128]{1,2,0:T(8,128)(2,1)S(1)}, u32[]{:S(2)}, u32[]{:S(2)}) %collective-permute-start.22) | collective-permute-done | bytes 139296 | tf_op jit(solution)/shard_map/ppermute | solution.py:66
  275.3 6.7 %collective-permute-start.23 = (bf16[8,136,128]{1,2,0:T(8,128)(2,1)}, bf16[8,136,128]{1,2,0:T(8,128)(2,1)}, u32[]{:S(2)}, u32[]{:S(2)}) collective-permute-start(bf16[8,136,128]{1,2,0:T(8,128)(2,1)} %pad_maximum_fusion.14), channel_id=1, source_target_pairs={{0,16},{4,20},{8,24},{12,28},{16,0},{20,4},{24,8},{28,12},{32,48},... | collective-permute-start | bytes 835592 | tf_op jit(solution)/shard_map/ppermute | solution.py:66
  282.1 15.2 %collective-permute-start.30 = (bf16[16,24,128]{1,2,0:T(8,128)(2,1)S(1)}, bf16[16,24,128]{1,2,0:T(8,128)(2,1)}, u32[]{:S(2)}, u32[]{:S(2)}) collective-permute-start(bf16[16,24,128]{1,2,0:T(8,128)(2,1)S(1)} %bitcast.305), channel_id=1, source_target_pairs={{0,128},{4,132},{8,136},{12,140},{16,144},{20,148},{24,152},{28,15... | collective-permute-start | bytes 294920 | tf_op jit(solution)/shard_map/ppermute | solution.py:66
  300.3 1.9 copy.290
  302.3 13.7 %collective-permute-done.30 = bf16[16,24,128]{1,2,0:T(8,128)(2,1)} collective-permute-done((bf16[16,24,128]{1,2,0:T(8,128)(2,1)S(1)}, bf16[16,24,128]{1,2,0:T(8,128)(2,1)}, u32[]{:S(2)}, u32[]{:S(2)}) %collective-permute-start.30) | collective-permute-done | bytes 98336 | tf_op jit(solution)/shard_map/ppermute | solution.py:66
  322.5 5.1 %collective-permute-start.28 = (bf16[16,56,128]{1,2,0:T(8,128)(2,1)}, bf16[16,56,128]{1,2,0:T(8,128)(2,1)}, u32[]{:S(2)}, u32[]{:S(2)}) collective-permute-start(bf16[16,56,128]{1,2,0:T(8,128)(2,1)} %slice.340), channel_id=1, source_target_pairs={{0,128},{4,132},{8,136},{12,140},{16,144},{20,148},{24,152},{28,15... | collective-permute-start | bytes 688136 | tf_op jit(solution)/shard_map/ppermute | solution.py:66
  330.6 2.3 fusion.6
  332.8 2.3 fusion.45
  337.3 1.9 collective-permute-start.34
  339.2 17.1 %collective-permute-done.28 = bf16[16,56,128]{1,2,0:T(8,128)(2,1)} collective-permute-done((bf16[16,56,128]{1,2,0:T(8,128)(2,1)}, bf16[16,56,128]{1,2,0:T(8,128)(2,1)}, u32[]{:S(2)}, u32[]{:S(2)}) %collective-permute-start.28) | collective-permute-done | bytes 229408 | tf_op jit(solution)/shard_map/ppermute | solution.py:66
  372.8 2.1 collective-permute-start.33
  383.8 12.3 %collective-permute-done.33 = bf16[64,24,128]{2,1,0:T(8,128)(2,1)} collective-permute-done((bf16[64,24,128]{2,1,0:T(8,128)(2,1)S(1)}, bf16[64,24,128]{2,1,0:T(8,128)(2,1)}, u32[]{:S(2)}, u32[]{:S(2)}) %collective-permute-start.33) | collective-permute-done | bytes 393248 | tf_op jit(solution)/shard_map/ppermute | solution.py:66
  405.2 2.0 fusion.30
  (505 shorter events, 178.3 us)
Async XLA Ops:
  2.5 23.8 %copy-start.76 = (pred[4,2]{0,1:T(4,128)(4,1)}, pred[4,2]{0,1:T(4,128)(4,1)S(1)}, u32[]{:S(2)}) copy-start(pred[4,2]{0,1:T(4,128)(4,1)S(1)} %iota_compare_fusion) | copy-start | bytes 28
  3.4 22.7 %copy-start.44 = (bf16[256,2,128]{2,1,0:T(2,128)(2,1)S(1)}, bf16[256,2,128]{2,1,0:T(2,128)(2,1)}, u32[]{:S(2)}) copy-start(bf16[256,2,128]{2,1,0:T(2,128)(2,1)} %param.13) | copy-start | bytes 393220
  6.5 22.5 %copy-start.56 = (bf16[16,2,128]{2,0,1:T(8,128)(2,1)}, bf16[16,2,128]{2,0,1:T(8,128)(2,1)S(1)}, u32[]{:S(2)}) copy-start(bf16[16,2,128]{2,0,1:T(8,128)(2,1)S(1)} %get-tuple-element.24) | copy-start | bytes 24580
  7.9 21.1 %collective-permute-start = (bf16[1,688,128]{2,1,0:T(8,128)(2,1)S(1)}, bf16[1,688,128]{2,1,0:T(8,128)(2,1)S(1)}, u32[]{:S(2)}, u32[]{:S(2)}) collective-permute-start(bf16[1,688,128]{2,1,0:T(8,128)(2,1)S(1)} %maximum_bitcast_fusion.1), channel_id=1, source_target_pairs={{0,8},{4,12},{8,0},{12,4},{16,24},{20,28},{24,16},{28,20},{32,40},... | collective-permute-start | bytes 528392 | tf_op jit(solution)/shard_map/ppermute | solution.py:66
  10.7 16.2 %collective-permute-start.7 = (bf16[1,688,128]{2,1,0:T(8,128)(2,1)S(1)}, bf16[1,688,128]{2,1,0:T(8,128)(2,1)S(1)}, u32[]{:S(2)}, u32[]{:S(2)}) collective-permute-start(bf16[1,688,128]{2,1,0:T(8,128)(2,1)S(1)} %maximum_bitcast_fusion.2), channel_id=1, source_target_pairs={{0,8},{4,12},{8,0},{12,4},{16,24},{20,28},{24,16},{28,20},{32,40},... | collective-permute-start | bytes 528392 | tf_op jit(solution)/shard_map/ppermute | solution.py:66
  14.0 18.1 %collective-permute-start.14 = (bf16[1,688,128]{2,1,0:T(8,128)(2,1)S(1)}, bf16[1,688,128]{2,1,0:T(8,128)(2,1)S(1)}, u32[]{:S(2)}, u32[]{:S(2)}) collective-permute-start(bf16[1,688,128]{2,1,0:T(8,128)(2,1)S(1)} %maximum_bitcast_fusion.3), channel_id=1, source_target_pairs={{0,8},{4,12},{8,0},{12,4},{16,24},{20,28},{24,16},{28,20},{32,40},... | collective-permute-start | bytes 528392 | tf_op jit(solution)/shard_map/ppermute | solution.py:66
  27.0 7.8 %collective-permute-start.8 = (bf16[2,688,128]{2,1,0:T(8,128)(2,1)S(1)}, bf16[2,688,128]{2,1,0:T(8,128)(2,1)S(1)}, u32[]{:S(2)}, u32[]{:S(2)}) collective-permute-start(bf16[2,688,128]{2,1,0:T(8,128)(2,1)S(1)} %pad_maximum_fusion.32), channel_id=1, source_target_pairs={{0,4},{4,0},{8,12},{12,8},{16,20},{20,16},{24,28},{28,24},{32,36},... | collective-permute-start | bytes 1056776 | tf_op jit(solution)/shard_map/ppermute | solution.py:66
  29.0 13.6 %collective-permute-start.1 = (bf16[2,688,128]{2,1,0:T(8,128)(2,1)S(1)}, bf16[2,688,128]{2,1,0:T(8,128)(2,1)S(1)}, u32[]{:S(2)}, u32[]{:S(2)}) collective-permute-start(bf16[2,688,128]{2,1,0:T(8,128)(2,1)S(1)} %pad_maximum_fusion.31), channel_id=1, source_target_pairs={{0,4},{4,0},{8,12},{12,8},{16,20},{20,16},{24,28},{28,24},{32,36},... | collective-permute-start | bytes 1056776 | tf_op jit(solution)/shard_map/ppermute | solution.py:66
  32.9 15.7 %collective-permute-start.15 = (bf16[2,688,128]{2,1,0:T(8,128)(2,1)}, bf16[2,688,128]{2,1,0:T(8,128)(2,1)}, u32[]{:S(2)}, u32[]{:S(2)}) collective-permute-start(bf16[2,688,128]{2,1,0:T(8,128)(2,1)} %pad_maximum_fusion.33), channel_id=1, source_target_pairs={{0,4},{4,0},{8,12},{12,8},{16,20},{20,16},{24,28},{28,24},{32,36},... | collective-permute-start | bytes 1056776 | tf_op jit(solution)/shard_map/ppermute | solution.py:66
  34.8 27.1 %collective-permute-start.9 = (bf16[4,176,128]{2,1,0:T(8,128)(2,1)S(1)}, bf16[4,176,128]{2,1,0:T(8,128)(2,1)S(1)}, u32[]{:S(2)}, u32[]{:S(2)}) collective-permute-start(bf16[4,176,128]{2,1,0:T(8,128)(2,1)S(1)} %pad_maximum_fusion.60), channel_id=1, source_target_pairs={{0,32},{4,36},{8,40},{12,44},{16,48},{20,52},{24,56},{28,60},{32,0... | collective-permute-start | bytes 540680 | tf_op jit(solution)/shard_map/ppermute | solution.py:66
  42.6 22.5 %collective-permute-start.2 = (bf16[4,176,128]{2,1,0:T(8,128)(2,1)S(1)}, bf16[4,176,128]{2,1,0:T(8,128)(2,1)}, u32[]{:S(2)}, u32[]{:S(2)}) collective-permute-start(bf16[4,176,128]{2,1,0:T(8,128)(2,1)S(1)} %pad_maximum_fusion.61), channel_id=1, source_target_pairs={{0,32},{4,36},{8,40},{12,44},{16,48},{20,52},{24,56},{28,60},{32,0... | collective-permute-start | bytes 540680 | tf_op jit(solution)/shard_map/ppermute | solution.py:66
  48.5 21.8 %copy-start.67 = (f32[2,256]{1,0:T(2,128)}, f32[2,256]{1,0:T(2,128)S(1)}, u32[]{:S(2)}) copy-start(f32[2,256]{1,0:T(2,128)S(1)} %get-tuple-element.81) | copy-start | bytes 6148
  54.2 17.0 %collective-permute-start.20 = (bf16[4,176,128]{2,1,0:T(8,128)(2,1)S(1)}, bf16[4,176,128]{2,1,0:T(8,128)(2,1)S(1)}, u32[]{:S(2)}, u32[]{:S(2)}) collective-permute-start(bf16[4,176,128]{2,1,0:T(8,128)(2,1)S(1)} %pad_maximum_fusion.59), channel_id=1, source_target_pairs={{0,32},{4,36},{8,40},{12,44},{16,48},{20,52},{24,56},{28,60},{32,0... | collective-permute-start | bytes 540680 | tf_op jit(solution)/shard_map/ppermute | solution.py:66
  62.0 15.2 %collective-permute-start.10 = (bf16[8,176,128]{2,1,0:T(8,128)(2,1)S(1)}, bf16[8,176,128]{2,1,0:T(8,128)(2,1)S(1)}, u32[]{:S(2)}, u32[]{:S(2)}) collective-permute-start(bf16[8,176,128]{2,1,0:T(8,128)(2,1)S(1)} %pad_maximum_fusion.29), channel_id=1, source_target_pairs={{0,16},{4,20},{8,24},{12,28},{16,0},{20,4},{24,8},{28,12},{32,48},... | collective-permute-start | bytes 1081352 | tf_op jit(solution)/shard_map/ppermute | solution.py:66
  66.0 18.4 %collective-permute-start.3 = (bf16[8,176,128]{2,1,0:T(8,128)(2,1)S(1)}, bf16[8,176,128]{2,1,0:T(8,128)(2,1)S(1)}, u32[]{:S(2)}, u32[]{:S(2)}) collective-permute-start(bf16[8,176,128]{2,1,0:T(8,128)(2,1)S(1)} %pad_maximum_fusion.28), channel_id=1, source_target_pairs={{0,16},{4,20},{8,24},{12,28},{16,0},{20,4},{24,8},{28,12},{32,48},... | collective-permute-start | bytes 1081352 | tf_op jit(solution)/shard_map/ppermute | solution.py:66
  71.2 21.9 %copy-start.19 = (bf16[4,176,128]{2,1,0:T(8,128)(2,1)}, bf16[4,176,128]{2,1,0:T(8,128)(2,1)S(1)}, u32[]{:S(2)}) copy-start(bf16[4,176,128]{2,1,0:T(8,128)(2,1)S(1)} %collective-permute-done.20) | copy-start | bytes 540676
  71.3 21.2 %copy-start.42 = (bf16[64,2,128]{2,0,1:T(8,128)(2,1)S(1)}, bf16[64,2,128]{2,0,1:T(8,128)(2,1)}, u32[]{:S(2)}) copy-start(bf16[64,2,128]{2,0,1:T(8,128)(2,1)} %copy-done.41) | copy-start | bytes 98308
  71.3 21.8 %collective-permute-start.21 = (bf16[8,176,128]{2,1,0:T(8,128)(2,1)S(1)}, bf16[8,176,128]{2,1,0:T(8,128)(2,1)S(1)}, u32[]{:S(2)}, u32[]{:S(2)}) collective-permute-start(bf16[8,176,128]{2,1,0:T(8,128)(2,1)S(1)} %pad_maximum_fusion.30), channel_id=1, source_target_pairs={{0,16},{4,20},{8,24},{12,28},{16,0},{20,4},{24,8},{28,12},{32,48},... | collective-permute-start | bytes 1081352 | tf_op jit(solution)/shard_map/ppermute | solution.py:66
  77.2 19.7 %collective-permute-start.11 = (bf16[16,48,128]{2,1,0:T(8,128)(2,1)S(1)}, bf16[16,48,128]{2,1,0:T(8,128)(2,1)S(1)}, u32[]{:S(2)}, u32[]{:S(2)}) collective-permute-start(bf16[16,48,128]{2,1,0:T(8,128)(2,1)S(1)} %pad_maximum_fusion.55), channel_id=1, source_target_pairs={{0,128},{4,132},{8,136},{12,140},{16,144},{20,148},{24,152},{28,15... | collective-permute-start | bytes 589832 | tf_op jit(solution)/shard_map/ppermute | solution.py:66
  85.3 17.6 %collective-permute-start.4 = (bf16[16,48,128]{2,1,0:T(8,128)(2,1)S(1)}, bf16[16,48,128]{2,1,0:T(8,128)(2,1)S(1)}, u32[]{:S(2)}, u32[]{:S(2)}) collective-permute-start(bf16[16,48,128]{2,1,0:T(8,128)(2,1)S(1)} %pad_maximum_fusion.56), channel_id=1, source_target_pairs={{0,128},{4,132},{8,136},{12,140},{16,144},{20,148},{24,152},{28,15... | collective-permute-start | bytes 589832 | tf_op jit(solution)/shard_map/ppermute | solution.py:66
  93.2 19.6 %collective-permute-start.26 = (bf16[16,48,128]{2,1,0:T(8,128)(2,1)S(1)}, bf16[16,48,128]{2,1,0:T(8,128)(2,1)}, u32[]{:S(2)}, u32[]{:S(2)}) collective-permute-start(bf16[16,48,128]{2,1,0:T(8,128)(2,1)S(1)} %pad_maximum_fusion.54), channel_id=1, source_target_pairs={{0,128},{4,132},{8,136},{12,140},{16,144},{20,148},{24,152},{28,15... | collective-permute-start | bytes 589832 | tf_op jit(solution)/shard_map/ppermute | solution.py:66
  97.8 19.2 %collective-permute-start.12 = (bf16[32,48,128]{2,1,0:T(8,128)(2,1)}, bf16[32,48,128]{2,1,0:T(8,128)(2,1)}, u32[]{:S(2)}, u32[]{:S(2)}) collective-permute-start(bf16[32,48,128]{2,1,0:T(8,128)(2,1)} %pad_maximum_fusion.24), channel_id=1, source_target_pairs={{0,64},{4,68},{8,72},{12,76},{16,80},{20,84},{24,88},{28,92},{32,9... | collective-permute-start | bytes 1179656 | tf_op jit(solution)/shard_map/ppermute | solution.py:66
  103.7 24.9 %collective-permute-start.5 = (bf16[32,48,128]{2,1,0:T(8,128)(2,1)}, bf16[32,48,128]{2,1,0:T(8,128)(2,1)}, u32[]{:S(2)}, u32[]{:S(2)}) collective-permute-start(bf16[32,48,128]{2,1,0:T(8,128)(2,1)} %pad_maximum_fusion.23), channel_id=1, source_target_pairs={{0,64},{4,68},{8,72},{12,76},{16,80},{20,84},{24,88},{28,92},{32,9... | collective-permute-start | bytes 1179656 | tf_op jit(solution)/shard_map/ppermute | solution.py:66
  114.5 29.0 %collective-permute-start.27 = (bf16[32,48,128]{2,1,0:T(8,128)(2,1)}, bf16[32,48,128]{2,1,0:T(8,128)(2,1)}, u32[]{:S(2)}, u32[]{:S(2)}) collective-permute-start(bf16[32,48,128]{2,1,0:T(8,128)(2,1)} %pad_maximum_fusion.26), channel_id=1, source_target_pairs={{0,64},{4,68},{8,72},{12,76},{16,80},{20,84},{24,88},{28,92},{32,9... | collective-permute-start | bytes 1179656 | tf_op jit(solution)/shard_map/ppermute | solution.py:66
  118.6 43.9 %collective-permute-start.13 = (bf16[64,16,128]{2,1,0:T(8,128)(2,1)}, bf16[64,16,128]{2,1,0:T(8,128)(2,1)}, u32[]{:S(2)}, u32[]{:S(2)}) collective-permute-start(bf16[64,16,128]{2,1,0:T(8,128)(2,1)} %pad_maximum_fusion.50), channel_id=1, source_target_pairs={{0,256},{4,260},{8,264},{12,268},{16,272},{20,276},{24,280},{28,28... | collective-permute-start | bytes 786440 | tf_op jit(solution)/shard_map/ppermute | solution.py:66
  129.6 26.3 %collective-permute-start.6 = (bf16[64,16,128]{2,1,0:T(8,128)(2,1)S(1)}, bf16[64,16,128]{2,1,0:T(8,128)(2,1)}, u32[]{:S(2)}, u32[]{:S(2)}) collective-permute-start(bf16[64,16,128]{2,1,0:T(8,128)(2,1)S(1)} %pad_maximum_fusion.51), channel_id=1, source_target_pairs={{0,256},{4,260},{8,264},{12,268},{16,272},{20,276},{24,280},{28,28... | collective-permute-start | bytes 786440 | tf_op jit(solution)/shard_map/ppermute | solution.py:66
  145.2 95.5 %collective-permute-start.32 = (bf16[64,16,128]{2,1,0:T(8,128)(2,1)}, bf16[64,16,128]{2,1,0:T(8,128)(2,1)}, u32[]{:S(2)}, u32[]{:S(2)}) collective-permute-start(bf16[64,16,128]{2,1,0:T(8,128)(2,1)} %pad_maximum_fusion.47), channel_id=1, source_target_pairs={{0,256},{4,260},{8,264},{12,268},{16,272},{20,276},{24,280},{28,28... | collective-permute-start | bytes 786440 | tf_op jit(solution)/shard_map/ppermute | solution.py:66
  175.9 26.2 %copy-start.10 = (bf16[64,32,128]{2,1,0:T(8,128)(2,1)S(1)}, bf16[64,32,128]{2,1,0:T(8,128)(2,1)}, u32[]{:S(2)}) copy-start(bf16[64,32,128]{2,1,0:T(8,128)(2,1)} %copy-done.9) | copy-start | bytes 1572868
  205.7 28.0 %copy-start.5 = (bf16[1024,2,128]{0,2,1:T(8,128)(2,1)S(1)}, bf16[1024,2,128]{0,2,1:T(8,128)(2,1)}, u32[]{:S(2)}) copy-start(bf16[1024,2,128]{0,2,1:T(8,128)(2,1)} %copy.252) | copy-start | bytes 1572868
  205.7 28.0 %copy-start.59 = (pred[256,2]{0,1:T(4,128)(4,1)S(1)}, pred[256,2]{0,1:T(4,128)(4,1)}, u32[]{:S(2)}) copy-start(pred[256,2]{0,1:T(4,128)(4,1)} %broadcast_in_dim.637) | copy-start | bytes 1540
  222.0 22.3 %collective-permute-start.16 = (bf16[1,424,128]{1,2,0:T(8,128)(2,1)S(1)}, bf16[1,424,128]{1,2,0:T(8,128)(2,1)}, u32[]{:S(2)}, u32[]{:S(2)}) collective-permute-start(bf16[1,424,128]{1,2,0:T(8,128)(2,1)S(1)} %bitcast.327), channel_id=1, source_target_pairs={{0,8},{4,12},{8,0},{12,4},{16,24},{20,28},{24,16},{28,20},{32,40},... | collective-permute-start | bytes 325640 | tf_op jit(solution)/shard_map/ppermute | solution.py:66
  231.0 6.8 %collective-permute-start.18 = (bf16[1,344,128]{1,2,0:T(8,128)(2,1)}, bf16[1,344,128]{1,2,0:T(8,128)(2,1)}, u32[]{:S(2)}, u32[]{:S(2)}) collective-permute-start(bf16[1,344,128]{1,2,0:T(8,128)(2,1)} %maximum_bitcast_fusion.4), channel_id=1, source_target_pairs={{0,8},{4,12},{8,0},{12,4},{16,24},{20,28},{24,16},{28,20},{32,40},... | collective-permute-start | bytes 264200 | tf_op jit(solution)/shard_map/ppermute | solution.py:66
  238.8 8.9 %collective-permute-start.19 = (bf16[2,344,128]{1,2,0:T(8,128)(2,1)S(1)}, bf16[2,344,128]{1,2,0:T(8,128)(2,1)S(1)}, u32[]{:S(2)}, u32[]{:S(2)}) collective-permute-start(bf16[2,344,128]{1,2,0:T(8,128)(2,1)S(1)} %pad_maximum_fusion.57), channel_id=1, source_target_pairs={{0,4},{4,0},{8,12},{12,8},{16,20},{20,16},{24,28},{28,24},{32,36},... | collective-permute-start | bytes 528392 | tf_op jit(solution)/shard_map/ppermute | solution.py:66
  245.2 7.5 %collective-permute-start.17 = (bf16[2,424,128]{1,2,0:T(8,128)(2,1)S(1)}, bf16[2,424,128]{1,2,0:T(8,128)(2,1)S(1)}, u32[]{:S(2)}, u32[]{:S(2)}) collective-permute-start(bf16[2,424,128]{1,2,0:T(8,128)(2,1)S(1)} %pad_maximum_fusion.52), channel_id=1, source_target_pairs={{0,4},{4,0},{8,12},{12,8},{16,20},{20,16},{24,28},{28,24},{32,36},... | collective-permute-start | bytes 651272 | tf_op jit(solution)/shard_map/ppermute | solution.py:66
  249.8 12.5 %collective-permute-start.24 = (bf16[4,88,128]{1,2,0:T(8,128)(2,1)S(1)}, bf16[4,88,128]{1,2,0:T(8,128)(2,1)S(1)}, u32[]{:S(2)}, u32[]{:S(2)}) collective-permute-start(bf16[4,88,128]{1,2,0:T(8,128)(2,1)S(1)} %pad_maximum_fusion.63), channel_id=1, source_target_pairs={{0,32},{4,36},{8,40},{12,44},{16,48},{20,52},{24,56},{28,60},{32,0... | collective-permute-start | bytes 270344 | tf_op jit(solution)/shard_map/ppermute | solution.py:66
  253.8 43.5 %copy-start.4 = (bf16[1024,2,128]{0,2,1:T(8,128)(2,1)S(1)}, bf16[1024,2,128]{0,2,1:T(8,128)(2,1)}, u32[]{:S(2)}) copy-start(bf16[1024,2,128]{0,2,1:T(8,128)(2,1)} %copy.285) | copy-start | bytes 1572868
  253.8 43.5 %copy-start.35 = (pred[1024,256]{1,0:T(8,128)(4,1)S(1)}, pred[1024,256]{1,0:T(8,128)(4,1)}, u32[]{:S(2)}) copy-start(pred[1024,256]{1,0:T(8,128)(4,1)} %broadcast_compare_fusion) | copy-start | bytes 786436
  254.9 19.4 %collective-permute-start.22 = (bf16[4,136,128]{1,2,0:T(8,128)(2,1)S(1)}, bf16[4,136,128]{1,2,0:T(8,128)(2,1)S(1)}, u32[]{:S(2)}, u32[]{:S(2)}) collective-permute-start(bf16[4,136,128]{1,2,0:T(8,128)(2,1)S(1)} %slice.329), channel_id=1, source_target_pairs={{0,32},{4,36},{8,40},{12,44},{16,48},{20,52},{24,56},{28,60},{32,0... | collective-permute-start | bytes 417800 | tf_op jit(solution)/shard_map/ppermute | solution.py:66
  262.4 19.6 %collective-permute-start.25 = (bf16[8,88,128]{1,2,0:T(8,128)(2,1)S(1)}, bf16[8,88,128]{1,2,0:T(8,128)(2,1)S(1)}, u32[]{:S(2)}, u32[]{:S(2)}) collective-permute-start(bf16[8,88,128]{1,2,0:T(8,128)(2,1)S(1)} %pad_maximum_fusion.53), channel_id=1, source_target_pairs={{0,16},{4,20},{8,24},{12,28},{16,0},{20,4},{24,8},{28,12},{32,48},... | collective-permute-start | bytes 540680 | tf_op jit(solution)/shard_map/ppermute | solution.py:66
  275.3 44.6 %collective-permute-start.23 = (bf16[8,136,128]{1,2,0:T(8,128)(2,1)}, bf16[8,136,128]{1,2,0:T(8,128)(2,1)}, u32[]{:S(2)}, u32[]{:S(2)}) collective-permute-start(bf16[8,136,128]{1,2,0:T(8,128)(2,1)} %pad_maximum_fusion.14), channel_id=1, source_target_pairs={{0,16},{4,20},{8,24},{12,28},{16,0},{20,4},{24,8},{28,12},{32,48},... | collective-permute-start | bytes 835592 | tf_op jit(solution)/shard_map/ppermute | solution.py:66
  282.1 33.8 %collective-permute-start.30 = (bf16[16,24,128]{1,2,0:T(8,128)(2,1)S(1)}, bf16[16,24,128]{1,2,0:T(8,128)(2,1)}, u32[]{:S(2)}, u32[]{:S(2)}) collective-permute-start(bf16[16,24,128]{1,2,0:T(8,128)(2,1)S(1)} %bitcast.305), channel_id=1, source_target_pairs={{0,128},{4,132},{8,136},{12,140},{16,144},{20,148},{24,152},{28,15... | collective-permute-start | bytes 294920 | tf_op jit(solution)/shard_map/ppermute | solution.py:66
  299.3 21.8 %copy-start.21 = (bf16[16,24,128]{2,1,0:T(8,128)(2,1)}, bf16[16,24,128]{2,1,0:T(8,128)(2,1)S(1)}, u32[]{:S(2)}) copy-start(bf16[16,24,128]{2,1,0:T(8,128)(2,1)S(1)} %copy.303) | copy-start | bytes 294916
  317.9 18.5 %collective-permute-start.31 = (bf16[32,24,128]{2,1,0:T(8,128)(2,1)}, bf16[32,24,128]{2,1,0:T(8,128)(2,1)}, u32[]{:S(2)}, u32[]{:S(2)}) collective-permute-start(bf16[32,24,128]{2,1,0:T(8,128)(2,1)} %pad_maximum_fusion.58), channel_id=1, source_target_pairs={{0,64},{4,68},{8,72},{12,76},{16,80},{20,84},{24,88},{28,92},{32,9... | collective-permute-start | bytes 589832 | tf_op jit(solution)/shard_map/ppermute | solution.py:66
  322.5 33.9 %collective-permute-start.28 = (bf16[16,56,128]{1,2,0:T(8,128)(2,1)}, bf16[16,56,128]{1,2,0:T(8,128)(2,1)}, u32[]{:S(2)}, u32[]{:S(2)}) collective-permute-start(bf16[16,56,128]{1,2,0:T(8,128)(2,1)} %slice.340), channel_id=1, source_target_pairs={{0,128},{4,132},{8,136},{12,140},{16,144},{20,148},{24,152},{28,15... | collective-permute-start | bytes 688136 | tf_op jit(solution)/shard_map/ppermute | solution.py:66
  337.3 31.2 %collective-permute-start.34 = (bf16[64,8,128]{2,1,0:T(8,128)(2,1)S(1)}, bf16[64,8,128]{2,1,0:T(8,128)(2,1)}, u32[]{:S(2)}, u32[]{:S(2)}) collective-permute-start(bf16[64,8,128]{2,1,0:T(8,128)(2,1)S(1)} %pad_maximum_fusion.62), channel_id=1, source_target_pairs={{0,256},{4,260},{8,264},{12,268},{16,272},{20,276},{24,280},{28,28... | collective-permute-start | bytes 393224 | tf_op jit(solution)/shard_map/ppermute | solution.py:66
  339.2 22.5 %copy-start.47 = (f32[64,2,128]{2,0,1:T(8,128)S(1)}, f32[64,2,128]{2,0,1:T(8,128)}, u32[]{:S(2)}) copy-start(f32[64,2,128]{2,0,1:T(8,128)} %fusion.45) | copy-start | bytes 196612
  358.4 13.4 %collective-permute-start.29 = (bf16[32,56,128]{2,1,0:T(8,128)(2,1)}, bf16[32,56,128]{2,1,0:T(8,128)(2,1)}, u32[]{:S(2)}, u32[]{:S(2)}) collective-permute-start(bf16[32,56,128]{2,1,0:T(8,128)(2,1)} %pad_maximum_fusion.20), channel_id=1, source_target_pairs={{0,64},{4,68},{8,72},{12,76},{16,80},{20,84},{24,88},{28,92},{32,9... | collective-permute-start | bytes 1376264 | tf_op jit(solution)/shard_map/ppermute | solution.py:66
  372.8 23.3 %collective-permute-start.33 = (bf16[64,24,128]{2,1,0:T(8,128)(2,1)S(1)}, bf16[64,24,128]{2,1,0:T(8,128)(2,1)}, u32[]{:S(2)}, u32[]{:S(2)}) collective-permute-start(bf16[64,24,128]{2,1,0:T(8,128)(2,1)S(1)} %pad_maximum_fusion.21), channel_id=1, source_target_pairs={{0,256},{4,260},{8,264},{12,268},{16,272},{20,276},{24,280},{28,28... | collective-permute-start | bytes 1179656 | tf_op jit(solution)/shard_map/ppermute | solution.py:66
  (81 other events, 821.0 us)

commit v3 on v0

--- a/solution.py
+++ b/solution.py
@@ -134,6 +134,7 @@
                 [
                     level["key_sel"].reshape(-1, lane),
                     level["value_sel"].reshape(-1, lane),
+                    level["query_sel"].reshape(-1, lane),
                 ],
                 axis=0,
             )
@@ -142,15 +143,15 @@
         spans,
         order,
     )
-    query_sets = extend([level["query_sel"].reshape(-1, lane) for level in levels], spans, order)
 
     lse_total = jnp.full((tok_dev, heads_dev), neg_fill, jnp.float32)
     for level, key_set in zip(levels, key_sets):
         span, rows = level["span"], level["rows"]
-        paired = key_set.reshape(span, 2, rows, heads_dev, head_size)
+        paired = key_set.reshape(span, 3, rows, heads_dev, head_size)
         keys = paired[:, 0].reshape(span * rows, heads_dev, head_size)
         level["key_all"] = keys
         level["value_all"] = paired[:, 1].reshape(span * rows, heads_dev, head_size)
+        level["query_all"] = paired[:, 2].reshape(span * rows, heads_dev, head_size)
         raw = (
             jnp.einsum("qhd,khd->hqk", level["query_sel"], keys, preferred_element_type=jnp.float32)
             * score_scale
@@ -230,9 +231,9 @@
 
     key_grad = jnp.zeros((tok_dev, heads_dev, head_size), jnp.float32)
     value_grad = jnp.zeros((tok_dev, heads_dev, head_size), jnp.float32)
-    for level, query_set, back_set in zip(levels, query_sets, back_sets):
+    for level, back_set in zip(levels, back_sets):
         span, rows = level["span"], level["rows"]
-        queries = query_set.reshape(span * rows, heads_dev, head_size)
+        queries = level["query_all"]
         back_slots = back_set.reshape(span, -1, lane)
         dout_all = back_slots[:, : rows * heads_dev].reshape(span * rows, heads_dev, head_size)
         lse_all, delta_all = unpack_stats(

time: 377 us -> 442 us (1.17)
  the two profiles are of different devices: /device:TPU:201 before, /device:TPU:10 now
where the time goes in v3:
time: 442 us; the launch traced here: 439 us
  waiting for transfers between devices  165 us (37%)
  local copies, waits for them, and re-layouts  94.5 us (21%)
  starting transfers between devices  75.8 us (17%)
  other arithmetic  54.2 us (12%)
  matrix products  34.8 us (8%)
  blocking collectives  12.8 us (3%)
    ppermute x14, waiting for transfers between devices, extend(): lax.ppermute(state, 'seq', [(source, source ^ offset) for source in range...  165 us
    ppermute x14, starting transfers between devices, extend(): lax.ppermute(state, 'seq', [(source, source ^ offset) for source in range...  75.8 us
    broadcast_in_dim x45, local copies, waits for them, and re-layouts, put_rows(): jnp.where(column == target, compact[:, None], jnp.asarray(filler, compact...  35.6 us
    unnamed x169, local copies, waits for them, and re-layouts  22.4 us
    concatenate x13, other arithmetic, extend(): state = jnp.concatenate([state, moved], axis=0)  16.6 us
    reduce_sum x12, other arithmetic, pick_rows(): return jnp.sum(zeroed, axis=1, dtype=source.dtype)  13.3 us
    psum x1, blocking collectives, shards(): lax.psum(jnp.stack([jnp.sum(attended, axis=(1, 2)), jnp.sum(attended * at...  12.8 us
  transfers between devices with their start and end apart: 14, of which 13 were waited for; matrix products, arithmetic and copies ran while one was open for 14% of the time, Pallas kernels for 0%

profile of v3, /device:TPU:10, one launch (start us, length us, event | category | flops | bytes accessed | tf_op | source)
XLA Modules:
  0.0 439.3 jit_solution(18076645483011351043)
XLA Ops:
  9.4 2.4 collective-permute-start
  12.1 12.9 %collective-permute-done = bf16[1,2064,128]{2,1,0:T(8,128)(2,1)S(1)} collective-permute-done((bf16[1,2064,128]{2,1,0:T(8,128)(2,1)S(1)}, bf16[1,2064,128]{2,1,0:T(8,128)(2,1)S(1)}, u32[]{:S(2)}, u32[]{:S(2)}) %collective-permute-start) | collective-permute-done | bytes 528416 | tf_op jit(solution)/shard_map/ppermute | solution.py:66
  25.1 1.9 collective-permute-start.1
  30.9 6.8 %collective-permute-start.2 = (bf16[4,528,128]{2,1,0:T(8,128)(2,1)S(1)}, bf16[4,528,128]{2,1,0:T(8,128)(2,1)S(1)}, u32[]{:S(2)}, u32[]{:S(2)}) collective-permute-start(bf16[4,528,128]{2,1,0:T(8,128)(2,1)S(1)} %pad_maximum_fusion.12), channel_id=1, source_target_pairs={{0,32},{4,36},{8,40},{12,44},{16,48},{20,52},{24,56},{28,60},{32,0... | collective-permute-start | bytes 1622024 | tf_op jit(solution)/shard_map/ppermute | solution.py:66
  38.5 24.1 %collective-permute-done.2 = bf16[4,528,128]{2,1,0:T(8,128)(2,1)S(1)} collective-permute-done((bf16[4,528,128]{2,1,0:T(8,128)(2,1)S(1)}, bf16[4,528,128]{2,1,0:T(8,128)(2,1)S(1)}, u32[]{:S(2)}, u32[]{:S(2)}) %collective-permute-start.2) | collective-permute-done | bytes 540704 | tf_op jit(solution)/shard_map/ppermute | solution.py:66
  63.7 4.0 collective-permute-start.3
  74.3 17.0 %collective-permute-done.3 = bf16[8,528,128]{2,1,0:T(8,128)(2,1)} collective-permute-done((bf16[8,528,128]{2,1,0:T(8,128)(2,1)}, bf16[8,528,128]{2,1,0:T(8,128)(2,1)}, u32[]{:S(2)}, u32[]{:S(2)}) %collective-permute-start.3) | collective-permute-done | bytes 1081376 | tf_op jit(solution)/shard_map/ppermute | solution.py:66
  92.3 6.1 %collective-permute-start.4 = (bf16[16,144,128]{2,1,0:T(8,128)(2,1)S(1)}, bf16[16,144,128]{2,1,0:T(8,128)(2,1)}, u32[]{:S(2)}, u32[]{:S(2)}) collective-permute-start(bf16[16,144,128]{2,1,0:T(8,128)(2,1)S(1)} %pad_maximum_fusion.11), channel_id=1, source_target_pairs={{0,128},{4,132},{8,136},{12,140},{16,144},{20,148},{24,152},{28,15... | collective-permute-start | bytes 1769480 | tf_op jit(solution)/shard_map/ppermute | solution.py:66
  105.5 16.2 %collective-permute-done.4 = bf16[16,144,128]{2,1,0:T(8,128)(2,1)} collective-permute-done((bf16[16,144,128]{2,1,0:T(8,128)(2,1)S(1)}, bf16[16,144,128]{2,1,0:T(8,128)(2,1)}, u32[]{:S(2)}, u32[]{:S(2)}) %collective-permute-start.4) | collective-permute-done | bytes 589856 | tf_op jit(solution)/shard_map/ppermute | solution.py:66
  121.7 2.2 pad_maximum_fusion.4
  123.9 2.5 collective-permute-start.5
  133.5 19.3 %collective-permute-done.5 = bf16[32,144,128]{2,1,0:T(8,128)(2,1)} collective-permute-done((bf16[32,144,128]{2,1,0:T(8,128)(2,1)}, bf16[32,144,128]{2,1,0:T(8,128)(2,1)}, u32[]{:S(2)}, u32[]{:S(2)}) %collective-permute-start.5) | collective-permute-done | bytes 1179680 | tf_op jit(solution)/shard_map/ppermute | solution.py:66
  155.3 2.0 pad_maximum_fusion.8
  157.3 9.7 %collective-permute-start.6 = (bf16[64,48,128]{2,1,0:T(8,128)(2,1)}, bf16[64,48,128]{2,1,0:T(8,128)(2,1)}, u32[]{:S(2)}, u32[]{:S(2)}) collective-permute-start(bf16[64,48,128]{2,1,0:T(8,128)(2,1)} %pad_maximum_fusion.8), channel_id=1, source_target_pairs={{0,256},{4,260},{8,264},{12,268},{16,272},{20,276},{24,280},{28,28... | collective-permute-start | bytes 2359304 | tf_op jit(solution)/shard_map/ppermute | solution.py:66
  172.0 11.1 %collective-permute-done.6 = bf16[64,48,128]{2,1,0:T(8,128)(2,1)} collective-permute-done((bf16[64,48,128]{2,1,0:T(8,128)(2,1)}, bf16[64,48,128]{2,1,0:T(8,128)(2,1)}, u32[]{:S(2)}, u32[]{:S(2)}) %collective-permute-start.6) | collective-permute-done | bytes 786464 | tf_op jit(solution)/shard_map/ppermute | solution.py:66
  200.9 1.8 copy.222
  204.7 1.8 copy.224
  211.3 2.4 fusion.144
  213.7 12.8 %psum.7 = f32[4,256]{1,0:T(4,128)S(1)} all-reduce(f32[4,256]{1,0:T(4,128)S(1)} %pad_maximum_fusion.24), channel_id=1, replica_groups=mesh['seq'=128,'head'=4] {'head'}, use_global_device_ids=true, to_apply=%region_24.25 | all-reduce | flops 1024 | bytes 8192 | tf_op jit(solution)/shard_map/psum | solution.py:185
  250.9 2.3 fusion.43
  258.2 8.7 %collective-permute-start.7 = (bf16[1,768,128]{2,1,0:T(8,128)(2,1)S(1)}, bf16[1,768,128]{2,1,0:T(8,128)(2,1)S(1)}, u32[]{:S(2)}, u32[]{:S(2)}) collective-permute-start(bf16[1,768,128]{2,1,0:T(8,128)(2,1)S(1)} %bitcast.344), channel_id=1, source_target_pairs={{0,8},{4,12},{8,0},{12,4},{16,24},{20,28},{24,16},{28,20},{32,40},... | collective-permute-start | bytes 589832 | tf_op jit(solution)/shard_map/ppermute | solution.py:66
  268.5 2.0 collective-permute-done.7
  272.0 1.9 collective-permute-start.8
  273.9 1.9 fusion.63
  277.4 1.8 copy.234
  279.9 1.8 copy.236
  282.5 1.8 copy.238
  284.3 2.8 fusion.31
  290.4 1.9 collective-permute-start.9
  293.9 15.2 %collective-permute-done.9 = bf16[4,224,128]{2,1,0:T(8,128)(2,1)S(1)} collective-permute-done((bf16[4,224,128]{2,1,0:T(8,128)(2,1)S(1)}, bf16[4,224,128]{2,1,0:T(8,128)(2,1)S(1)}, u32[]{:S(2)}, u32[]{:S(2)}) %collective-permute-start.9) | collective-permute-done | bytes 229408 | tf_op jit(solution)/shard_map/ppermute | solution.py:66
  309.1 1.9 collective-permute-start.10
  313.3 11.6 %collective-permute-done.10 = bf16[8,224,128]{2,1,0:T(8,128)(2,1)S(1)} collective-permute-done((bf16[8,224,128]{2,1,0:T(8,128)(2,1)S(1)}, bf16[8,224,128]{2,1,0:T(8,128)(2,1)S(1)}, u32[]{:S(2)}, u32[]{:S(2)}) %collective-permute-start.10) | collective-permute-done | bytes 458784 | tf_op jit(solution)/shard_map/ppermute | solution.py:66
  326.8 16.4 %collective-permute-start.11 = (bf16[16,80,128]{2,1,0:T(8,128)(2,1)S(1)}, bf16[16,80,128]{2,1,0:T(8,128)(2,1)}, u32[]{:S(2)}, u32[]{:S(2)}) collective-permute-start(bf16[16,80,128]{2,1,0:T(8,128)(2,1)S(1)} %pad_maximum_fusion.19), channel_id=1, source_target_pairs={{0,128},{4,132},{8,136},{12,140},{16,144},{20,148},{24,152},{28,15... | collective-permute-start | bytes 983048 | tf_op jit(solution)/shard_map/ppermute | solution.py:66
  344.7 12.6 %collective-permute-done.11 = bf16[16,80,128]{2,1,0:T(8,128)(2,1)} collective-permute-done((bf16[16,80,128]{2,1,0:T(8,128)(2,1)S(1)}, bf16[16,80,128]{2,1,0:T(8,128)(2,1)}, u32[]{:S(2)}, u32[]{:S(2)}) %collective-permute-start.11) | collective-permute-done | bytes 327712 | tf_op jit(solution)/shard_map/ppermute | solution.py:66
  357.3 1.9 pad_maximum_fusion.10
  359.2 2.7 collective-permute-start.12
  365.6 2.3 fusion.45
  369.6 7.3 %collective-permute-done.12 = bf16[32,80,128]{2,1,0:T(8,128)(2,1)} collective-permute-done((bf16[32,80,128]{2,1,0:T(8,128)(2,1)}, bf16[32,80,128]{2,1,0:T(8,128)(2,1)}, u32[]{:S(2)}, u32[]{:S(2)}) %collective-permute-start.12) | collective-permute-done | bytes 655392 | tf_op jit(solution)/shard_map/ppermute | solution.py:66
  378.6 2.1 copy.285
  383.6 2.2 pad_maximum_fusion.16
  385.8 8.8 %collective-permute-start.13 = (bf16[64,32,128]{2,1,0:T(8,128)(2,1)}, bf16[64,32,128]{2,1,0:T(8,128)(2,1)}, u32[]{:S(2)}, u32[]{:S(2)}) collective-permute-start(bf16[64,32,128]{2,1,0:T(8,128)(2,1)} %get-tuple-element.45), channel_id=1, source_target_pairs={{0,256},{4,260},{8,264},{12,268},{16,272},{20,276},{24,280},{28,28... | collective-permute-start | bytes 1572872 | tf_op jit(solution)/shard_map/ppermute | solution.py:66
  401.7 14.9 %collective-permute-done.13 = bf16[64,32,128]{2,1,0:T(8,128)(2,1)} collective-permute-done((bf16[64,32,128]{2,1,0:T(8,128)(2,1)}, bf16[64,32,128]{2,1,0:T(8,128)(2,1)}, u32[]{:S(2)}, u32[]{:S(2)}) %collective-permute-start.13) | collective-permute-done | bytes 524320 | tf_op jit(solution)/shard_map/ppermute | solution.py:66
  416.6 2.2 pad_maximum_fusion.13
  424.1 1.8 convolution_bitcast_fusion.6
  425.9 2.1 fusion.61
  431.0 1.9 copy.264
  432.8 2.0 fusion.29
  436.5 2.0 fusion.30
  (382 shorter events, 141.7 us)
Async XLA Ops:
  0.6 11.3 %copy-start.69 = (s32[128]{0:T(128)S(1)}, s32[128]{0:T(128)}, u32[]{:S(2)}) copy-start(s32[128]{0:T(128)} %constant.137.clone) | copy-start | bytes 1540
  0.6 11.3 %copy-start.68 = (s32[64]{0:T(128)S(1)}, s32[64]{0:T(128)}, u32[]{:S(2)}) copy-start(s32[64]{0:T(128)} %constant.136.clone) | copy-start | bytes 772
  0.7 11.3 %copy-start.67 = (s32[16]{0:T(128)S(1)}, s32[16]{0:T(128)}, u32[]{:S(2)}) copy-start(s32[16]{0:T(128)} %constant.135.clone) | copy-start | bytes 196
  1.5 68.6 %copy-start.58 = (pred[4,2]{0,1:T(4,128)(4,1)}, pred[4,2]{0,1:T(4,128)(4,1)S(1)}, u32[]{:S(2)}) copy-start(pred[4,2]{0,1:T(4,128)(4,1)S(1)} %iota_compare_fusion) | copy-start | bytes 28
  1.6 67.0 %copy-start.59 = (pred[16,2]{0,1:T(4,128)(4,1)}, pred[16,2]{0,1:T(4,128)(4,1)S(1)}, u32[]{:S(2)}) copy-start(pred[16,2]{0,1:T(4,128)(4,1)S(1)} %iota_compare_fusion.1) | copy-start | bytes 100
  1.6 66.1 %copy-start.60 = (pred[32,2]{0,1:T(4,128)(4,1)}, pred[32,2]{0,1:T(4,128)(4,1)S(1)}, u32[]{:S(2)}) copy-start(pred[32,2]{0,1:T(4,128)(4,1)S(1)} %iota_compare_fusion.2) | copy-start | bytes 196
  7.6 19.5 %copy-start.66 = (s32[4]{0:T(128)S(1)}, s32[4]{0:T(128)}, u32[]{:S(2)}) copy-start(s32[4]{0:T(128)} %constant.134.clone) | copy-start | bytes 52
  8.8 22.0 %copy-start.28 = (bf16[64,2,128]{2,0,1:T(8,128)(2,1)}, bf16[64,2,128]{2,0,1:T(8,128)(2,1)S(1)}, u32[]{:S(2)}) copy-start(bf16[64,2,128]{2,0,1:T(8,128)(2,1)S(1)} %get-tuple-element.20) | copy-start | bytes 98308
  9.4 15.6 %collective-permute-start = (bf16[1,2064,128]{2,1,0:T(8,128)(2,1)S(1)}, bf16[1,2064,128]{2,1,0:T(8,128)(2,1)S(1)}, u32[]{:S(2)}, u32[]{:S(2)}) collective-permute-start(bf16[1,2064,128]{2,1,0:T(8,128)(2,1)S(1)} %bitcast.323), channel_id=1, source_target_pairs={{0,8},{4,12},{8,0},{12,4},{16,24},{20,28},{24,16},{28,20},{32,40},... | collective-permute-start | bytes 1585160 | tf_op jit(solution)/shard_map/ppermute | solution.py:66
  25.1 4.7 %collective-permute-start.1 = (bf16[2,2064,128]{2,1,0:T(8,128)(2,1)S(1)}, bf16[2,2064,128]{2,1,0:T(8,128)(2,1)}, u32[]{:S(2)}, u32[]{:S(2)}) collective-permute-start(bf16[2,2064,128]{2,1,0:T(8,128)(2,1)S(1)} %pad_maximum_fusion.6), channel_id=1, source_target_pairs={{0,4},{4,0},{8,12},{12,8},{16,20},{20,16},{24,28},{28,24},{32,36},... | collective-permute-start | bytes 3170312 | tf_op jit(solution)/shard_map/ppermute | solution.py:66
  28.8 41.5 %copy-start.39 = (bf16[256,2,128]{2,1,0:T(2,128)(2,1)S(1)}, bf16[256,2,128]{2,1,0:T(2,128)(2,1)}, u32[]{:S(2)}) copy-start(bf16[256,2,128]{2,1,0:T(2,128)(2,1)} %param.13) | copy-start | bytes 393220
  30.9 31.7 %collective-permute-start.2 = (bf16[4,528,128]{2,1,0:T(8,128)(2,1)S(1)}, bf16[4,528,128]{2,1,0:T(8,128)(2,1)S(1)}, u32[]{:S(2)}, u32[]{:S(2)}) collective-permute-start(bf16[4,528,128]{2,1,0:T(8,128)(2,1)S(1)} %pad_maximum_fusion.12), channel_id=1, source_target_pairs={{0,32},{4,36},{8,40},{12,44},{16,48},{20,52},{24,56},{28,60},{32,0... | collective-permute-start | bytes 1622024 | tf_op jit(solution)/shard_map/ppermute | solution.py:66
  62.6 29.7 %copy-start = (bf16[4,528,128]{2,1,0:T(8,128)(2,1)}, bf16[4,528,128]{2,1,0:T(8,128)(2,1)S(1)}, u32[]{:S(2)}) copy-start(bf16[4,528,128]{2,1,0:T(8,128)(2,1)S(1)} %collective-permute-done.2) | copy-start | bytes 1622020
  63.7 27.5 %collective-permute-start.3 = (bf16[8,528,128]{2,1,0:T(8,128)(2,1)}, bf16[8,528,128]{2,1,0:T(8,128)(2,1)}, u32[]{:S(2)}, u32[]{:S(2)}) collective-permute-start(bf16[8,528,128]{2,1,0:T(8,128)(2,1)} %pad_maximum_fusion.5), channel_id=1, source_target_pairs={{0,16},{4,20},{8,24},{12,28},{16,0},{20,4},{24,8},{28,12},{32,48},... | collective-permute-start | bytes 3244040 | tf_op jit(solution)/shard_map/ppermute | solution.py:66
  68.6 142.7 %copy-start.43 = (pred[256,2]{0,1:T(4,128)(4,1)}, pred[256,2]{0,1:T(4,128)(4,1)S(1)}, u32[]{:S(2)}) copy-start(pred[256,2]{0,1:T(4,128)(4,1)S(1)} %broadcast_in_dim.622) | copy-start | bytes 1540
  70.2 118.0 %copy-start.46 = (pred[256,2]{0,1:T(4,128)(4,1)}, pred[256,2]{0,1:T(4,128)(4,1)S(1)}, u32[]{:S(2)}) copy-start(pred[256,2]{0,1:T(4,128)(4,1)S(1)} %broadcast_in_dim.615) | copy-start | bytes 1540
  92.3 29.5 %collective-permute-start.4 = (bf16[16,144,128]{2,1,0:T(8,128)(2,1)S(1)}, bf16[16,144,128]{2,1,0:T(8,128)(2,1)}, u32[]{:S(2)}, u32[]{:S(2)}) collective-permute-start(bf16[16,144,128]{2,1,0:T(8,128)(2,1)S(1)} %pad_maximum_fusion.11), channel_id=1, source_target_pairs={{0,128},{4,132},{8,136},{12,140},{16,144},{20,148},{24,152},{28,15... | collective-permute-start | bytes 1769480 | tf_op jit(solution)/shard_map/ppermute | solution.py:66
  105.5 21.2 %copy-start.1 = (bf16[4,528,128]{2,1,0:T(8,128)(2,1)S(1)}, bf16[4,528,128]{2,1,0:T(8,128)(2,1)}, u32[]{:S(2)}) copy-start(bf16[4,528,128]{2,1,0:T(8,128)(2,1)} %copy-done) | copy-start | bytes 1622020
  123.9 29.0 %collective-permute-start.5 = (bf16[32,144,128]{2,1,0:T(8,128)(2,1)}, bf16[32,144,128]{2,1,0:T(8,128)(2,1)}, u32[]{:S(2)}, u32[]{:S(2)}) collective-permute-start(bf16[32,144,128]{2,1,0:T(8,128)(2,1)} %pad_maximum_fusion.4), channel_id=1, source_target_pairs={{0,64},{4,68},{8,72},{12,76},{16,80},{20,84},{24,88},{28,92},{32,9... | collective-permute-start | bytes 3538952 | tf_op jit(solution)/shard_map/ppermute | solution.py:66
  133.3 21.2 %copy-start.61 = (f32[64,2]{0,1:T(2,128)}, f32[64,2]{0,1:T(2,128)S(1)}, u32[]{:S(2)}) copy-start(f32[64,2]{0,1:T(2,128)S(1)} %add_bitcast_fusion.3) | copy-start | bytes 1540
  157.3 25.8 %collective-permute-start.6 = (bf16[64,48,128]{2,1,0:T(8,128)(2,1)}, bf16[64,48,128]{2,1,0:T(8,128)(2,1)}, u32[]{:S(2)}, u32[]{:S(2)}) collective-permute-start(bf16[64,48,128]{2,1,0:T(8,128)(2,1)} %pad_maximum_fusion.8), channel_id=1, source_target_pairs={{0,256},{4,260},{8,264},{12,268},{16,272},{20,276},{24,280},{28,28... | collective-permute-start | bytes 2359304 | tf_op jit(solution)/shard_map/ppermute | solution.py:66
  170.9 31.8 %copy-start.21 = (f32[2,16,1024]{2,1,0:T(8,128)}, f32[2,16,1024]{2,1,0:T(8,128)S(1)}, u32[]{:S(2)}) copy-start(f32[2,16,1024]{2,1,0:T(8,128)S(1)} %get-tuple-element.84) | copy-start | bytes 393220
  171.1 13.9 %copy-start.57 = (f32[16,2]{0,1:T(2,128)}, f32[16,2]{0,1:T(2,128)S(1)}, u32[]{:S(2)}) copy-start(f32[16,2]{0,1:T(2,128)S(1)} %add_bitcast_fusion.2) | copy-start | bytes 388
  185.1 14.1 %copy-start.6 = (bf16[16,1,64,2,128]{4,2,0,3,1:T(8,128)(2,1)S(1)}, bf16[16,1,64,2,128]{4,2,0,3,1:T(8,128)(2,1)}, u32[]{:S(2)}) copy-start(bf16[16,1,64,2,128]{4,2,0,3,1:T(8,128)(2,1)} %copy.221) | copy-start | bytes 1572868
  200.1 11.2 %copy-start.2 = (bf16[1024,2,128]{0,2,1:T(8,128)(2,1)S(1)}, bf16[1024,2,128]{0,2,1:T(8,128)(2,1)}, u32[]{:S(2)}) copy-start(bf16[1024,2,128]{0,2,1:T(8,128)(2,1)} %copy.282) | copy-start | bytes 1572868
  200.1 11.2 %copy-start.25 = (bf16[256,2,128]{0,2,1:T(8,128)(2,1)S(1)}, bf16[256,2,128]{0,2,1:T(8,128)(2,1)}, u32[]{:S(2)}) copy-start(bf16[256,2,128]{0,2,1:T(8,128)(2,1)} %copy.227) | copy-start | bytes 393220
  227.7 25.5 %copy-start.22 = (bf16[256,2,128]{0,2,1:T(8,128)(2,1)}, bf16[256,2,128]{0,2,1:T(8,128)(2,1)S(1)}, u32[]{:S(2)}) copy-start(bf16[256,2,128]{0,2,1:T(8,128)(2,1)S(1)} %get-tuple-element.29) | copy-start | bytes 393220
  258.2 31.4 %copy-start.14 = (bf16[768,128]{1,0:T(8,128)(2,1)}, bf16[768,128]{1,0:T(8,128)(2,1)S(1)}, u32[]{:S(2)}) copy-start(bf16[768,128]{1,0:T(8,128)(2,1)S(1)} %constant_dynamic-update-slice_fusion.12) | copy-start | bytes 589828
  258.2 12.3 %collective-permute-start.7 = (bf16[1,768,128]{2,1,0:T(8,128)(2,1)S(1)}, bf16[1,768,128]{2,1,0:T(8,128)(2,1)S(1)}, u32[]{:S(2)}, u32[]{:S(2)}) collective-permute-start(bf16[1,768,128]{2,1,0:T(8,128)(2,1)S(1)} %bitcast.344), channel_id=1, source_target_pairs={{0,8},{4,12},{8,0},{12,4},{16,24},{20,28},{24,16},{28,20},{32,40},... | collective-permute-start | bytes 589832 | tf_op jit(solution)/shard_map/ppermute | solution.py:66
  268.5 15.7 %copy-start.23 = (bf16[256,2,128]{0,2,1:T(8,128)(2,1)S(1)}, bf16[256,2,128]{0,2,1:T(8,128)(2,1)}, u32[]{:S(2)}) copy-start(bf16[256,2,128]{0,2,1:T(8,128)(2,1)} %copy-done.22) | copy-start | bytes 393220
  268.5 15.7 %copy-start.44 = (pred[256,2]{0,1:T(4,128)(4,1)S(1)}, pred[256,2]{0,1:T(4,128)(4,1)}, u32[]{:S(2)}) copy-start(pred[256,2]{0,1:T(4,128)(4,1)} %copy-done.43) | copy-start | bytes 1540
  268.5 15.7 %copy-start.47 = (pred[256,2]{0,1:T(4,128)(4,1)S(1)}, pred[256,2]{0,1:T(4,128)(4,1)}, u32[]{:S(2)}) copy-start(pred[256,2]{0,1:T(4,128)(4,1)} %copy-done.46) | copy-start | bytes 1540
  268.5 15.7 %copy-start.49 = (f32[256,2]{0,1:T(2,128)S(1)}, f32[256,2]{0,1:T(2,128)}, u32[]{:S(2)}) copy-start(f32[256,2]{0,1:T(2,128)} %get-tuple-element.30) | copy-start | bytes 6148
  272.0 16.8 %collective-permute-start.8 = (bf16[2,768,128]{2,1,0:T(8,128)(2,1)}, bf16[2,768,128]{2,1,0:T(8,128)(2,1)S(1)}, u32[]{:S(2)}, u32[]{:S(2)}) collective-permute-start(bf16[2,768,128]{2,1,0:T(8,128)(2,1)} %pad_maximum_fusion.18), channel_id=1, source_target_pairs={{0,4},{4,0},{8,12},{12,8},{16,20},{20,16},{24,28},{28,24},{32,36},... | collective-permute-start | bytes 1179656 | tf_op jit(solution)/shard_map/ppermute | solution.py:66
  290.4 18.7 %collective-permute-start.9 = (bf16[4,224,128]{2,1,0:T(8,128)(2,1)S(1)}, bf16[4,224,128]{2,1,0:T(8,128)(2,1)S(1)}, u32[]{:S(2)}, u32[]{:S(2)}) collective-permute-start(bf16[4,224,128]{2,1,0:T(8,128)(2,1)S(1)} %pad_maximum_fusion.21), channel_id=1, source_target_pairs={{0,32},{4,36},{8,40},{12,44},{16,48},{20,52},{24,56},{28,60},{32,0... | collective-permute-start | bytes 688136 | tf_op jit(solution)/shard_map/ppermute | solution.py:66
  292.4 19.3 %copy-start.37 = (pred[1024,256]{1,0:T(8,128)(4,1)S(1)}, pred[1024,256]{1,0:T(8,128)(4,1)}, u32[]{:S(2)}) copy-start(pred[1024,256]{1,0:T(8,128)(4,1)} %broadcast_compare_fusion) | copy-start | bytes 786436
  309.1 15.8 %collective-permute-start.10 = (bf16[8,224,128]{2,1,0:T(8,128)(2,1)S(1)}, bf16[8,224,128]{2,1,0:T(8,128)(2,1)S(1)}, u32[]{:S(2)}, u32[]{:S(2)}) collective-permute-start(bf16[8,224,128]{2,1,0:T(8,128)(2,1)S(1)} %pad_maximum_fusion.17), channel_id=1, source_target_pairs={{0,16},{4,20},{8,24},{12,28},{16,0},{20,4},{24,8},{28,12},{32,48},... | collective-permute-start | bytes 1376264 | tf_op jit(solution)/shard_map/ppermute | solution.py:66
  326.8 30.5 %collective-permute-start.11 = (bf16[16,80,128]{2,1,0:T(8,128)(2,1)S(1)}, bf16[16,80,128]{2,1,0:T(8,128)(2,1)}, u32[]{:S(2)}, u32[]{:S(2)}) collective-permute-start(bf16[16,80,128]{2,1,0:T(8,128)(2,1)S(1)} %pad_maximum_fusion.19), channel_id=1, source_target_pairs={{0,128},{4,132},{8,136},{12,140},{16,144},{20,148},{24,152},{28,15... | collective-permute-start | bytes 983048 | tf_op jit(solution)/shard_map/ppermute | solution.py:66
  343.4 18.5 %copy-start.4 = (bf16[16,1,64,2,128]{4,2,0,3,1:T(8,128)(2,1)S(1)}, bf16[16,1,64,2,128]{4,2,0,3,1:T(8,128)(2,1)}, u32[]{:S(2)}) copy-start(bf16[16,1,64,2,128]{4,2,0,3,1:T(8,128)(2,1)} %copy.248) | copy-start | bytes 1572868
  343.4 18.6 %copy-start.31 = (bf16[64,2,128]{2,0,1:T(8,128)(2,1)S(1)}, bf16[64,2,128]{2,0,1:T(8,128)(2,1)}, u32[]{:S(2)}) copy-start(bf16[64,2,128]{2,0,1:T(8,128)(2,1)} %copy-done.30) | copy-start | bytes 98308
  343.4 18.6 %copy-start.35 = (pred[1024,64]{0,1:T(8,128)(4,1)S(1)}, pred[1024,64]{0,1:T(8,128)(4,1)}, u32[]{:S(2)}) copy-start(pred[1024,64]{0,1:T(8,128)(4,1)} %broadcast_compare_fusion.2) | copy-start | bytes 196612
  344.7 17.7 %copy-start.8 = (bf16[16,128,128]{2,1,0:T(8,128)(2,1)}, bf16[16,128,128]{2,1,0:T(8,128)(2,1)S(1)}, u32[]{:S(2)}) copy-start(bf16[16,128,128]{2,1,0:T(8,128)(2,1)S(1)} %slice.274) | copy-start | bytes 1572868
  344.7 21.0 %copy-start.5 = (bf16[16,1,64,2,128]{4,2,0,3,1:T(8,128)(2,1)S(1)}, bf16[16,1,64,2,128]{4,2,0,3,1:T(8,128)(2,1)}, u32[]{:S(2)}) copy-start(bf16[16,1,64,2,128]{4,2,0,3,1:T(8,128)(2,1)} %copy.248) | copy-start | bytes 1572868
  344.7 21.0 %copy-start.29 = (bf16[64,2,128]{2,0,1:T(8,128)(2,1)S(1)}, bf16[64,2,128]{2,0,1:T(8,128)(2,1)}, u32[]{:S(2)}) copy-start(bf16[64,2,128]{2,0,1:T(8,128)(2,1)} %copy-done.28) | copy-start | bytes 98308
  359.2 17.7 %collective-permute-start.12 = (bf16[32,80,128]{2,1,0:T(8,128)(2,1)}, bf16[32,80,128]{2,1,0:T(8,128)(2,1)}, u32[]{:S(2)}, u32[]{:S(2)}) collective-permute-start(bf16[32,80,128]{2,1,0:T(8,128)(2,1)} %pad_maximum_fusion.10), channel_id=1, source_target_pairs={{0,64},{4,68},{8,72},{12,76},{16,80},{20,84},{24,88},{28,92},{32,9... | collective-permute-start | bytes 1966088 | tf_op jit(solution)/shard_map/ppermute | solution.py:66
  378.6 16.0 %copy-start.3 = (bf16[64,1,16,2,128]{4,2,0,3,1:T(8,128)(2,1)S(1)}, bf16[64,1,16,2,128]{4,2,0,3,1:T(8,128)(2,1)}, u32[]{:S(2)}) copy-start(bf16[64,1,16,2,128]{4,2,0,3,1:T(8,128)(2,1)} %copy.253) | copy-start | bytes 1572868
  383.6 11.9 %copy-start.42 = (f32[1,2,64,16]{2,3,1,0:T(8,128)S(1)}, f32[1,2,64,16]{2,3,1,0:T(8,128)}, u32[]{:S(2)}) copy-start(f32[1,2,64,16]{2,3,1,0:T(8,128)} %get-tuple-element.50) | copy-start | bytes 24580
  385.8 30.9 %collective-permute-start.13 = (bf16[64,32,128]{2,1,0:T(8,128)(2,1)}, bf16[64,32,128]{2,1,0:T(8,128)(2,1)}, u32[]{:S(2)}, u32[]{:S(2)}) collective-permute-start(bf16[64,32,128]{2,1,0:T(8,128)(2,1)} %get-tuple-element.45), channel_id=1, source_target_pairs={{0,256},{4,260},{8,264},{12,268},{16,272},{20,276},{24,280},{28,28... | collective-permute-start | bytes 1572872 | tf_op jit(solution)/shard_map/ppermute | solution.py:66
  (36 other events, 136.5 us)

commit v4 on v0

--- a/solution.py
+++ b/solution.py
@@ -49,7 +49,7 @@
     return table
 
 
-def extend(parts, spans, order):
+def extend(parts, spans, order, toward):
     count = lax.axis_size("seq")
     live = sorted(range(len(parts)), key=lambda index: -spans[index])
     sizes = [part.shape[0] for part in parts]
@@ -63,7 +63,10 @@
             state = state[:, :start]
         if not live:
             break
-        moved = lax.ppermute(state, "seq", [(source, source ^ offset) for source in range(count)])
+        pairs = [(source, source ^ offset) for source in range(count)]
+        if all(spans[index] <= 2 * state.shape[0] for index in live):
+            pairs = [pair for pair in pairs if (pair[1] > pair[0]) == (toward > 0)]
+        moved = lax.ppermute(state, "seq", pairs)
         state = jnp.concatenate([state, moved], axis=0)
     return [finished[index] for index in range(len(parts))]
 
@@ -141,8 +144,11 @@
         ],
         spans,
         order,
-    )
-    query_sets = extend([level["query_sel"].reshape(-1, lane) for level in levels], spans, order)
+        1,
+    )
+    query_sets = extend(
+        [level["query_sel"].reshape(-1, lane) for level in levels], spans, order, -1
+    )
 
     lse_total = jnp.full((tok_dev, heads_dev), neg_fill, jnp.float32)
     for level, key_set in zip(levels, key_sets):
@@ -226,7 +232,7 @@
         query_grad = query_grad + put_rows(
             grad_sel * score_scale, level["wanted"], level["stride"], 0.0
         )
-    back_sets = extend(back_sets, spans, order)
+    back_sets = extend(back_sets, spans, order, -1)
 
     key_grad = jnp.zeros((tok_dev, heads_dev, head_size), jnp.float32)
     value_grad = jnp.zeros((tok_dev, heads_dev, head_size), jnp.float32)

time: 377 us -> 371 us (0.984)
  the two profiles are of different devices: /device:TPU:201 before, /device:TPU:74 now
where the time goes in v4:
time: 371 us; the launch traced here: 369 us
  waiting for transfers between devices  123 us (33%)
  starting transfers between devices  76.5 us (21%)
  local copies, waits for them, and re-layouts  70 us (19%)
  other arithmetic  46.2 us (12%)
  matrix products  37.5 us (10%)
  blocking collectives  13.3 us (4%)
    ppermute x21, waiting for transfers between devices, extend(): moved = lax.ppermute(state, 'seq', pairs)  123 us
    ppermute x21, starting transfers between devices, extend(): moved = lax.ppermute(state, 'seq', pairs)  76.5 us
    broadcast_in_dim x45, local copies, waits for them, and re-layouts, put_rows(): jnp.where(column == target, compact[:, None], jnp.asarray(filler, compact...  30.1 us
    psum x1, blocking collectives, shards(): lax.psum(jnp.stack([jnp.sum(attended, axis=(1, 2)), jnp.sum(attended * at...  13.3 us
    concatenate x20, other arithmetic, extend(): state = jnp.concatenate([state, moved], axis=0)  13.2 us
    unnamed x205, local copies, waits for them, and re-layouts  12.9 us
    reduce_sum x12, other arithmetic, pick_rows(): return jnp.sum(zeroed, axis=1, dtype=source.dtype)  12.1 us
    dot_general x4, matrix products, shards(): jnp.einsum('hqk,qhd->khd', score_grad, queries, preferred_element_type=jn...  8.41 us
  transfers between devices with their start and end apart: 21, of which 16 were waited for; matrix products, arithmetic and copies ran while one was open for 21% of the time, Pallas kernels for 0%

profile of v4, /device:TPU:74, one launch (start us, length us, event | category | flops | bytes accessed | tf_op | source)
XLA Modules:
  0.0 368.6 jit_solution(18264421656202876044)
XLA Ops:
  8.0 2.4 collective-permute-start
  10.6 3.5 collective-permute-start.7
  19.5 4.2 %collective-permute-done.7 = bf16[1,688,128]{2,1,0:T(8,128)(2,1)S(1)} collective-permute-done((bf16[1,688,128]{2,1,0:T(8,128)(2,1)S(1)}, bf16[1,688,128]{2,1,0:T(8,128)(2,1)S(1)}, u32[]{:S(2)}, u32[]{:S(2)}) %collective-permute-start.7) | collective-permute-done | bytes 176160 | tf_op jit(solution)/shard_map/ppermute | solution.py:69
  23.7 1.9 collective-permute-start.8
  26.6 2.4 collective-permute-start.1
  29.7 6.8 %collective-permute-start.11 = (bf16[4,176,128]{2,1,0:T(8,128)(2,1)S(1)}, bf16[4,176,128]{2,1,0:T(8,128)(2,1)S(1)}, u32[]{:S(2)}, u32[]{:S(2)}) collective-permute-start(bf16[4,176,128]{2,1,0:T(8,128)(2,1)S(1)} %pad_maximum_fusion.31), channel_id=1, source_target_pairs={{0,32},{4,36},{8,40},{12,44},{16,48},{20,52},{24,56},{28,60},{32,0... | collective-permute-start | bytes 540680 | tf_op jit(solution)/shard_map/ppermute | solution.py:69
  42.2 2.4 collective-permute-done.11
  44.7 4.0 %collective-permute-start.12 = (bf16[8,176,128]{2,1,0:T(8,128)(2,1)S(1)}, bf16[8,176,128]{2,1,0:T(8,128)(2,1)S(1)}, u32[]{:S(2)}, u32[]{:S(2)}) collective-permute-start(bf16[8,176,128]{2,1,0:T(8,128)(2,1)S(1)} %pad_maximum_fusion.24), channel_id=1, source_target_pairs={{0,16},{4,20},{8,24},{12,28},{16,0},{20,4},{24,8},{28,12},{32,48},... | collective-permute-start | bytes 1081352 | tf_op jit(solution)/shard_map/ppermute | solution.py:69
  49.0 7.0 %collective-permute-start.2 = (bf16[4,352,128]{2,1,0:T(8,128)(2,1)S(1)}, bf16[4,352,128]{2,1,0:T(8,128)(2,1)S(1)}, u32[]{:S(2)}, u32[]{:S(2)}) collective-permute-start(bf16[4,352,128]{2,1,0:T(8,128)(2,1)S(1)} %pad_maximum_fusion.23), channel_id=1, source_target_pairs={{0,32},{4,36},{8,40},{12,44},{16,48},{20,52},{24,56},{28,60},{32,0... | collective-permute-start | bytes 1081352 | tf_op jit(solution)/shard_map/ppermute | solution.py:69
  58.4 6.1 %collective-permute-start.15 = (bf16[16,48,128]{2,1,0:T(8,128)(2,1)S(1)}, bf16[16,48,128]{2,1,0:T(8,128)(2,1)S(1)}, u32[]{:S(2)}, u32[]{:S(2)}) collective-permute-start(bf16[16,48,128]{2,1,0:T(8,128)(2,1)S(1)} %pad_maximum_fusion.30), channel_id=1, source_target_pairs={{0,128},{4,132},{8,136},{12,140},{16,144},{20,148},{24,152},{28,15... | collective-permute-start | bytes 589832 | tf_op jit(solution)/shard_map/ppermute | solution.py:69
  66.5 3.7 %collective-permute-done.15 = bf16[16,48,128]{2,1,0:T(8,128)(2,1)S(1)} collective-permute-done((bf16[16,48,128]{2,1,0:T(8,128)(2,1)S(1)}, bf16[16,48,128]{2,1,0:T(8,128)(2,1)S(1)}, u32[]{:S(2)}, u32[]{:S(2)}) %collective-permute-start.15) | collective-permute-done | bytes 196640 | tf_op jit(solution)/shard_map/ppermute | solution.py:69
  70.3 3.2 collective-permute-start.16
  73.6 4.0 %collective-permute-start.3 = (bf16[8,352,128]{2,1,0:T(8,128)(2,1)S(1)}, bf16[8,352,128]{2,1,0:T(8,128)(2,1)S(1)}, u32[]{:S(2)}, u32[]{:S(2)}) collective-permute-start(bf16[8,352,128]{2,1,0:T(8,128)(2,1)S(1)} %pad_maximum_fusion.8), channel_id=1, source_target_pairs={{0,16},{4,20},{8,24},{12,28},{16,0},{20,4},{24,8},{28,12},{32,48},... | collective-permute-start | bytes 2162696 | tf_op jit(solution)/shard_map/ppermute | solution.py:69
  80.1 2.4 collective-permute-done.16
  84.9 8.1 %collective-permute-done.3 = bf16[8,352,128]{2,1,0:T(8,128)(2,1)S(1)} collective-permute-done((bf16[8,352,128]{2,1,0:T(8,128)(2,1)S(1)}, bf16[8,352,128]{2,1,0:T(8,128)(2,1)S(1)}, u32[]{:S(2)}, u32[]{:S(2)}) %collective-permute-start.3) | collective-permute-done | bytes 720928 | tf_op jit(solution)/shard_map/ppermute | solution.py:69
  93.1 5.3 %collective-permute-start.4 = (bf16[16,96,128]{2,1,0:T(8,128)(2,1)S(1)}, bf16[16,96,128]{2,1,0:T(8,128)(2,1)S(1)}, u32[]{:S(2)}, u32[]{:S(2)}) collective-permute-start(bf16[16,96,128]{2,1,0:T(8,128)(2,1)S(1)} %pad_maximum_fusion.20), channel_id=1, source_target_pairs={{0,128},{4,132},{8,136},{12,140},{16,144},{20,148},{24,152},{28,15... | collective-permute-start | bytes 1179656 | tf_op jit(solution)/shard_map/ppermute | solution.py:69
  99.3 2.8 collective-permute-done.19
  103.9 14.1 %collective-permute-done.4 = bf16[16,96,128]{2,1,0:T(8,128)(2,1)S(1)} collective-permute-done((bf16[16,96,128]{2,1,0:T(8,128)(2,1)S(1)}, bf16[16,96,128]{2,1,0:T(8,128)(2,1)S(1)}, u32[]{:S(2)}, u32[]{:S(2)}) %collective-permute-start.4) | collective-permute-done | bytes 393248 | tf_op jit(solution)/shard_map/ppermute | solution.py:69
  119.0 2.2 collective-permute-start.5
  126.5 2.1 copy.224
  128.6 12.0 %collective-permute-done.5 = bf16[32,96,128]{2,1,0:T(8,128)(2,1)} collective-permute-done((bf16[32,96,128]{2,1,0:T(8,128)(2,1)}, bf16[32,96,128]{2,1,0:T(8,128)(2,1)}, u32[]{:S(2)}, u32[]{:S(2)}) %collective-permute-start.5) | collective-permute-done | bytes 786464 | tf_op jit(solution)/shard_map/ppermute | solution.py:69
  142.5 6.3 %collective-permute-start.6 = (bf16[64,32,128]{2,1,0:T(8,128)(2,1)}, bf16[64,32,128]{2,1,0:T(8,128)(2,1)}, u32[]{:S(2)}, u32[]{:S(2)}) collective-permute-start(bf16[64,32,128]{2,1,0:T(8,128)(2,1)} %pad_maximum_fusion.17), channel_id=1, source_target_pairs={{0,256},{4,260},{8,264},{12,268},{16,272},{20,276},{24,280},{28,28... | collective-permute-start | bytes 1572872 | tf_op jit(solution)/shard_map/ppermute | solution.py:69
  154.4 2.2 copy.226
  156.5 13.8 %collective-permute-done.6 = bf16[64,32,128]{2,1,0:T(8,128)(2,1)} collective-permute-done((bf16[64,32,128]{2,1,0:T(8,128)(2,1)}, bf16[64,32,128]{2,1,0:T(8,128)(2,1)}, u32[]{:S(2)}, u32[]{:S(2)}) %collective-permute-start.6) | collective-permute-done | bytes 524320 | tf_op jit(solution)/shard_map/ppermute | solution.py:69
  191.1 2.3 fusion.146
  193.4 13.3 %psum.7 = f32[4,256]{1,0:T(4,128)S(1)} all-reduce(f32[4,256]{1,0:T(4,128)S(1)} %pad_maximum_fusion.34), channel_id=1, replica_groups=mesh['seq'=128,'head'=4] {'head'}, use_global_device_ids=true, to_apply=%region_24.25 | all-reduce | flops 1024 | bytes 8192 | tf_op jit(solution)/shard_map/psum | solution.py:190
  215.4 2.3 fusion.43
  222.5 2.4 collective-permute-start.9
  226.6 3.5 collective-permute-done.9
  231.5 1.9 collective-permute-start.10
  233.4 1.9 fusion.63
  243.0 2.1 fusion.31
  247.6 4.1 %collective-permute-start.13 = (bf16[4,224,128]{2,1,0:T(8,128)(2,1)S(1)}, bf16[4,224,128]{2,1,0:T(8,128)(2,1)S(1)}, u32[]{:S(2)}, u32[]{:S(2)}) collective-permute-start(bf16[4,224,128]{2,1,0:T(8,128)(2,1)S(1)} %pad_maximum_fusion.29), channel_id=1, source_target_pairs={{0,32},{4,36},{8,40},{12,44},{16,48},{20,52},{24,56},{28,60},{32,0... | collective-permute-start | bytes 688136 | tf_op jit(solution)/shard_map/ppermute | solution.py:69
  253.4 12.9 %collective-permute-done.13 = bf16[4,224,128]{2,1,0:T(8,128)(2,1)S(1)} collective-permute-done((bf16[4,224,128]{2,1,0:T(8,128)(2,1)S(1)}, bf16[4,224,128]{2,1,0:T(8,128)(2,1)S(1)}, u32[]{:S(2)}, u32[]{:S(2)}) %collective-permute-start.13) | collective-permute-done | bytes 229408 | tf_op jit(solution)/shard_map/ppermute | solution.py:69
  266.4 4.0 %collective-permute-start.14 = (bf16[8,224,128]{2,1,0:T(8,128)(2,1)S(1)}, bf16[8,224,128]{2,1,0:T(8,128)(2,1)S(1)}, u32[]{:S(2)}, u32[]{:S(2)}) collective-permute-start(bf16[8,224,128]{2,1,0:T(8,128)(2,1)S(1)} %pad_maximum_fusion.19), channel_id=1, source_target_pairs={{0,16},{4,20},{8,24},{12,28},{16,0},{20,4},{24,8},{28,12},{32,48},... | collective-permute-start | bytes 1376264 | tf_op jit(solution)/shard_map/ppermute | solution.py:69
  272.9 9.3 %collective-permute-done.14 = bf16[8,224,128]{2,1,0:T(8,128)(2,1)S(1)} collective-permute-done((bf16[8,224,128]{2,1,0:T(8,128)(2,1)S(1)}, bf16[8,224,128]{2,1,0:T(8,128)(2,1)S(1)}, u32[]{:S(2)}, u32[]{:S(2)}) %collective-permute-start.14) | collective-permute-done | bytes 458784 | tf_op jit(solution)/shard_map/ppermute | solution.py:69
  282.2 1.9 collective-permute-start.17
  287.6 10.1 %collective-permute-done.17 = bf16[16,80,128]{2,1,0:T(8,128)(2,1)} collective-permute-done((bf16[16,80,128]{2,1,0:T(8,128)(2,1)S(1)}, bf16[16,80,128]{2,1,0:T(8,128)(2,1)}, u32[]{:S(2)}, u32[]{:S(2)}) %collective-permute-start.17) | collective-permute-done | bytes 327712 | tf_op jit(solution)/shard_map/ppermute | solution.py:69
  299.6 4.1 %collective-permute-start.18 = (bf16[32,80,128]{2,1,0:T(8,128)(2,1)}, bf16[32,80,128]{2,1,0:T(8,128)(2,1)}, u32[]{:S(2)}, u32[]{:S(2)}) collective-permute-start(bf16[32,80,128]{2,1,0:T(8,128)(2,1)} %pad_maximum_fusion.12), channel_id=1, source_target_pairs={{0,64},{4,68},{8,72},{12,76},{16,80},{20,84},{24,88},{28,92},{32,9... | collective-permute-start | bytes 1966088 | tf_op jit(solution)/shard_map/ppermute | solution.py:69
  303.7 2.2 fusion.6
  305.9 2.3 fusion.45
  313.7 4.1 %collective-permute-done.18 = bf16[32,80,128]{2,1,0:T(8,128)(2,1)} collective-permute-done((bf16[32,80,128]{2,1,0:T(8,128)(2,1)}, bf16[32,80,128]{2,1,0:T(8,128)(2,1)}, u32[]{:S(2)}, u32[]{:S(2)}) %collective-permute-start.18) | collective-permute-done | bytes 655392 | tf_op jit(solution)/shard_map/ppermute | solution.py:69
  317.8 2.0 pad_maximum_fusion.16
  322.8 2.0 copy.293
  332.1 17.7 %collective-permute-done.20 = bf16[64,32,128]{2,1,0:T(8,128)(2,1)} collective-permute-done((bf16[64,32,128]{2,1,0:T(8,128)(2,1)}, bf16[64,32,128]{2,1,0:T(8,128)(2,1)}, u32[]{:S(2)}, u32[]{:S(2)}) %collective-permute-start.20) | collective-permute-done | bytes 524320 | tf_op jit(solution)/shard_map/ppermute | solution.py:69
  349.8 2.2 pad_maximum_fusion.13
  357.7 2.2 fusion.61
  361.4 2.6 fusion.30
  (444 shorter events, 129.7 us)
Async XLA Ops:
  1.5 35.7 %copy-start.76 = (pred[32,2]{0,1:T(4,128)(4,1)}, pred[32,2]{0,1:T(4,128)(4,1)S(1)}, u32[]{:S(2)}) copy-start(pred[32,2]{0,1:T(4,128)(4,1)S(1)} %iota_compare_fusion.2) | copy-start | bytes 196
  5.6 21.0 %copy-start.54 = (bf16[8,2,128]{2,0,1:T(8,128)(2,1)}, bf16[8,2,128]{2,0,1:T(8,128)(2,1)S(1)}, u32[]{:S(2)}) copy-start(bf16[8,2,128]{2,0,1:T(8,128)(2,1)S(1)} %get-tuple-element.25) | copy-start | bytes 12292
  5.7 33.0 %copy-start.74 = (pred[16,2]{0,1:T(4,128)(4,1)}, pred[16,2]{0,1:T(4,128)(4,1)S(1)}, u32[]{:S(2)}) copy-start(pred[16,2]{0,1:T(4,128)(4,1)S(1)} %iota_compare_fusion.1) | copy-start | bytes 100
  7.0 19.6 %copy-start.62 = (bf16[16,2,128]{2,0,1:T(8,128)(2,1)}, bf16[16,2,128]{2,0,1:T(8,128)(2,1)S(1)}, u32[]{:S(2)}) copy-start(bf16[16,2,128]{2,0,1:T(8,128)(2,1)S(1)} %get-tuple-element.24) | copy-start | bytes 24580
  7.1 33.1 %copy-start.72 = (pred[4,2]{0,1:T(4,128)(4,1)}, pred[4,2]{0,1:T(4,128)(4,1)S(1)}, u32[]{:S(2)}) copy-start(pred[4,2]{0,1:T(4,128)(4,1)S(1)} %iota_compare_fusion) | copy-start | bytes 28
  7.7 17.9 %copy-start.31 = (bf16[64,2,128]{2,0,1:T(8,128)(2,1)}, bf16[64,2,128]{2,0,1:T(8,128)(2,1)S(1)}, u32[]{:S(2)}) copy-start(bf16[64,2,128]{2,0,1:T(8,128)(2,1)S(1)} %get-tuple-element.20) | copy-start | bytes 98308
  7.7 17.9 %copy-start.33 = (bf16[64,2,128]{2,0,1:T(8,128)(2,1)}, bf16[64,2,128]{2,0,1:T(8,128)(2,1)S(1)}, u32[]{:S(2)}) copy-start(bf16[64,2,128]{2,0,1:T(8,128)(2,1)S(1)} %get-tuple-element.19) | copy-start | bytes 98308
  7.8 17.9 %copy-start.38 = (bf16[64,2,128]{2,0,1:T(8,128)(2,1)}, bf16[64,2,128]{2,0,1:T(8,128)(2,1)S(1)}, u32[]{:S(2)}) copy-start(bf16[64,2,128]{2,0,1:T(8,128)(2,1)S(1)} %get-tuple-element.21) | copy-start | bytes 98308
  8.0 17.6 %collective-permute-start = (bf16[1,1376,128]{2,1,0:T(8,128)(2,1)S(1)}, bf16[1,1376,128]{2,1,0:T(8,128)(2,1)S(1)}, u32[]{:S(2)}, u32[]{:S(2)}) collective-permute-start(bf16[1,1376,128]{2,1,0:T(8,128)(2,1)S(1)} %bitcast.328), channel_id=1, source_target_pairs={{0,8},{4,12},{8,0},{12,4},{16,24},{20,28},{24,16},{28,20},{32,40},... | collective-permute-start | bytes 1056776 | tf_op jit(solution)/shard_map/ppermute | solution.py:69
  10.6 28.9 %copy-start.40 = (bf16[256,2,128]{2,1,0:T(2,128)(2,1)S(1)}, bf16[256,2,128]{2,1,0:T(2,128)(2,1)}, u32[]{:S(2)}) copy-start(bf16[256,2,128]{2,1,0:T(2,128)(2,1)} %param.13) | copy-start | bytes 393220
  10.6 13.1 %collective-permute-start.7 = (bf16[1,688,128]{2,1,0:T(8,128)(2,1)S(1)}, bf16[1,688,128]{2,1,0:T(8,128)(2,1)S(1)}, u32[]{:S(2)}, u32[]{:S(2)}) collective-permute-start(bf16[1,688,128]{2,1,0:T(8,128)(2,1)S(1)} %maximum_bitcast_fusion), channel_id=1, source_target_pairs={{0,8},{4,12},{8,0},{12,4},{16,24},{20,28},{24,16},{28,20},{32,40},... | collective-permute-start | bytes 528392 | tf_op jit(solution)/shard_map/ppermute | solution.py:69
  23.7 6.0 %collective-permute-start.8 = (bf16[2,688,128]{2,1,0:T(8,128)(2,1)S(1)}, bf16[2,688,128]{2,1,0:T(8,128)(2,1)S(1)}, u32[]{:S(2)}, u32[]{:S(2)}) collective-permute-start(bf16[2,688,128]{2,1,0:T(8,128)(2,1)S(1)} %pad_maximum_fusion.25), channel_id=1, source_target_pairs={{0,4},{4,0},{8,12},{12,8},{16,20},{20,16},{24,28},{28,24},{32,36},... | collective-permute-start | bytes 1056776 | tf_op jit(solution)/shard_map/ppermute | solution.py:69
  26.6 22.2 %collective-permute-start.1 = (bf16[2,1376,128]{2,1,0:T(8,128)(2,1)}, bf16[2,1376,128]{2,1,0:T(8,128)(2,1)S(1)}, u32[]{:S(2)}, u32[]{:S(2)}) collective-permute-start(bf16[2,1376,128]{2,1,0:T(8,128)(2,1)} %pad_maximum_fusion.10), channel_id=1, source_target_pairs={{0,4},{4,0},{8,12},{12,8},{16,20},{20,16},{24,28},{28,24},{32,36},... | collective-permute-start | bytes 2113544 | tf_op jit(solution)/shard_map/ppermute | solution.py:69
  29.7 15.0 %collective-permute-start.11 = (bf16[4,176,128]{2,1,0:T(8,128)(2,1)S(1)}, bf16[4,176,128]{2,1,0:T(8,128)(2,1)S(1)}, u32[]{:S(2)}, u32[]{:S(2)}) collective-permute-start(bf16[4,176,128]{2,1,0:T(8,128)(2,1)S(1)} %pad_maximum_fusion.31), channel_id=1, source_target_pairs={{0,32},{4,36},{8,40},{12,44},{16,48},{20,52},{24,56},{28,60},{32,0... | collective-permute-start | bytes 540680 | tf_op jit(solution)/shard_map/ppermute | solution.py:69
  38.0 205.0 %copy-start.46 = (pred[256,2]{0,1:T(4,128)(4,1)}, pred[256,2]{0,1:T(4,128)(4,1)S(1)}, u32[]{:S(2)}) copy-start(pred[256,2]{0,1:T(4,128)(4,1)S(1)} %broadcast_in_dim.631) | copy-start | bytes 1540
  38.8 152.3 %copy-start.48 = (pred[256,2]{0,1:T(4,128)(4,1)}, pred[256,2]{0,1:T(4,128)(4,1)S(1)}, u32[]{:S(2)}) copy-start(pred[256,2]{0,1:T(4,128)(4,1)S(1)} %broadcast_in_dim.625) | copy-start | bytes 1540
  44.7 12.8 %collective-permute-start.12 = (bf16[8,176,128]{2,1,0:T(8,128)(2,1)S(1)}, bf16[8,176,128]{2,1,0:T(8,128)(2,1)S(1)}, u32[]{:S(2)}, u32[]{:S(2)}) collective-permute-start(bf16[8,176,128]{2,1,0:T(8,128)(2,1)S(1)} %pad_maximum_fusion.24), channel_id=1, source_target_pairs={{0,16},{4,20},{8,24},{12,28},{16,0},{20,4},{24,8},{28,12},{32,48},... | collective-permute-start | bytes 1081352 | tf_op jit(solution)/shard_map/ppermute | solution.py:69
  49.0 24.5 %collective-permute-start.2 = (bf16[4,352,128]{2,1,0:T(8,128)(2,1)S(1)}, bf16[4,352,128]{2,1,0:T(8,128)(2,1)S(1)}, u32[]{:S(2)}, u32[]{:S(2)}) collective-permute-start(bf16[4,352,128]{2,1,0:T(8,128)(2,1)S(1)} %pad_maximum_fusion.23), channel_id=1, source_target_pairs={{0,32},{4,36},{8,40},{12,44},{16,48},{20,52},{24,56},{28,60},{32,0... | collective-permute-start | bytes 1081352 | tf_op jit(solution)/shard_map/ppermute | solution.py:69
  58.4 24.1 %copy-start.11 = (bf16[16,48,128]{2,1,0:T(8,128)(2,1)}, bf16[16,48,128]{2,1,0:T(8,128)(2,1)S(1)}, u32[]{:S(2)}) copy-start(bf16[16,48,128]{2,1,0:T(8,128)(2,1)S(1)} %pad_maximum_fusion.30) | copy-start | bytes 589828
  58.4 11.9 %collective-permute-start.15 = (bf16[16,48,128]{2,1,0:T(8,128)(2,1)S(1)}, bf16[16,48,128]{2,1,0:T(8,128)(2,1)S(1)}, u32[]{:S(2)}, u32[]{:S(2)}) collective-permute-start(bf16[16,48,128]{2,1,0:T(8,128)(2,1)S(1)} %pad_maximum_fusion.30), channel_id=1, source_target_pairs={{0,128},{4,132},{8,136},{12,140},{16,144},{20,148},{24,152},{28,15... | collective-permute-start | bytes 589832 | tf_op jit(solution)/shard_map/ppermute | solution.py:69
  70.3 12.2 %collective-permute-start.16 = (bf16[32,48,128]{2,1,0:T(8,128)(2,1)S(1)}, bf16[32,48,128]{2,1,0:T(8,128)(2,1)S(1)}, u32[]{:S(2)}, u32[]{:S(2)}) collective-permute-start(bf16[32,48,128]{2,1,0:T(8,128)(2,1)S(1)} %pad_maximum_fusion.22), channel_id=1, source_target_pairs={{0,64},{4,68},{8,72},{12,76},{16,80},{20,84},{24,88},{28,92},{32,9... | collective-permute-start | bytes 1179656 | tf_op jit(solution)/shard_map/ppermute | solution.py:69
  73.6 19.4 %collective-permute-start.3 = (bf16[8,352,128]{2,1,0:T(8,128)(2,1)S(1)}, bf16[8,352,128]{2,1,0:T(8,128)(2,1)S(1)}, u32[]{:S(2)}, u32[]{:S(2)}) collective-permute-start(bf16[8,352,128]{2,1,0:T(8,128)(2,1)S(1)} %pad_maximum_fusion.8), channel_id=1, source_target_pairs={{0,16},{4,20},{8,24},{12,28},{16,0},{20,4},{24,8},{28,12},{32,48},... | collective-permute-start | bytes 2162696 | tf_op jit(solution)/shard_map/ppermute | solution.py:69
  82.5 19.5 %collective-permute-start.19 = (bf16[64,16,128]{2,1,0:T(8,128)(2,1)S(1)}, bf16[64,16,128]{2,1,0:T(8,128)(2,1)S(1)}, u32[]{:S(2)}, u32[]{:S(2)}) collective-permute-start(bf16[64,16,128]{2,1,0:T(8,128)(2,1)S(1)} %pad_maximum_fusion.27), channel_id=1, source_target_pairs={{256,0},{260,4},{264,8},{268,12},{272,16},{276,20},{280,24},{284,2... | collective-permute-start | bytes 786440 | tf_op jit(solution)/shard_map/ppermute | solution.py:69
  93.1 24.9 %collective-permute-start.4 = (bf16[16,96,128]{2,1,0:T(8,128)(2,1)S(1)}, bf16[16,96,128]{2,1,0:T(8,128)(2,1)S(1)}, u32[]{:S(2)}, u32[]{:S(2)}) collective-permute-start(bf16[16,96,128]{2,1,0:T(8,128)(2,1)S(1)} %pad_maximum_fusion.20), channel_id=1, source_target_pairs={{0,128},{4,132},{8,136},{12,140},{16,144},{20,148},{24,152},{28,15... | collective-permute-start | bytes 1179656 | tf_op jit(solution)/shard_map/ppermute | solution.py:69
  103.8 19.2 %copy-start.34 = (bf16[64,2,128]{2,0,1:T(8,128)(2,1)S(1)}, bf16[64,2,128]{2,0,1:T(8,128)(2,1)}, u32[]{:S(2)}) copy-start(bf16[64,2,128]{2,0,1:T(8,128)(2,1)} %copy-done.33) | copy-start | bytes 98308
  103.8 19.2 %copy-start.37 = (pred[64,1024]{1,0:T(8,128)(4,1)S(1)}, pred[64,1024]{1,0:T(8,128)(4,1)}, u32[]{:S(2)}) copy-start(pred[64,1024]{1,0:T(8,128)(4,1)} %broadcast_compare_fusion.3) | copy-start | bytes 196612
  119.0 21.7 %collective-permute-start.5 = (bf16[32,96,128]{2,1,0:T(8,128)(2,1)}, bf16[32,96,128]{2,1,0:T(8,128)(2,1)}, u32[]{:S(2)}, u32[]{:S(2)}) collective-permute-start(bf16[32,96,128]{2,1,0:T(8,128)(2,1)} %pad_maximum_fusion.5), channel_id=1, source_target_pairs={{0,64},{4,68},{8,72},{12,76},{16,80},{20,84},{24,88},{28,92},{32,9... | collective-permute-start | bytes 2359304 | tf_op jit(solution)/shard_map/ppermute | solution.py:69
  126.5 22.3 %copy-start.4 = (bf16[16,96,128]{2,1,0:T(8,128)(2,1)S(1)}, bf16[16,96,128]{2,1,0:T(8,128)(2,1)}, u32[]{:S(2)}) copy-start(bf16[16,96,128]{2,1,0:T(8,128)(2,1)} %copy-done.3) | copy-start | bytes 1179652
  142.5 27.8 %collective-permute-start.6 = (bf16[64,32,128]{2,1,0:T(8,128)(2,1)}, bf16[64,32,128]{2,1,0:T(8,128)(2,1)}, u32[]{:S(2)}, u32[]{:S(2)}) collective-permute-start(bf16[64,32,128]{2,1,0:T(8,128)(2,1)} %pad_maximum_fusion.17), channel_id=1, source_target_pairs={{0,256},{4,260},{8,264},{12,268},{16,272},{20,276},{24,280},{28,28... | collective-permute-start | bytes 1572872 | tf_op jit(solution)/shard_map/ppermute | solution.py:69
  153.5 16.8 %copy-start.70 = (f32[16,2]{0,1:T(2,128)}, f32[16,2]{0,1:T(2,128)S(1)}, u32[]{:S(2)}) copy-start(f32[16,2]{0,1:T(2,128)S(1)} %add_bitcast_fusion.2) | copy-start | bytes 388
  191.0 17.6 %copy-start.77 = (pred[32,2]{0,1:T(4,128)(4,1)S(1)}, pred[32,2]{0,1:T(4,128)(4,1)}, u32[]{:S(2)}) copy-start(pred[32,2]{0,1:T(4,128)(4,1)} %copy-done.76) | copy-start | bytes 196
  191.1 19.2 %copy-start.75 = (pred[16,2]{0,1:T(4,128)(4,1)S(1)}, pred[16,2]{0,1:T(4,128)(4,1)}, u32[]{:S(2)}) copy-start(pred[16,2]{0,1:T(4,128)(4,1)} %copy-done.74) | copy-start | bytes 100
  191.1 22.5 %copy-start.73 = (pred[4,2]{0,1:T(4,128)(4,1)S(1)}, pred[4,2]{0,1:T(4,128)(4,1)}, u32[]{:S(2)}) copy-start(pred[4,2]{0,1:T(4,128)(4,1)} %copy-done.72) | copy-start | bytes 28
  222.5 24.2 %copy-start.10 = (bf16[768,128]{1,0:T(8,128)(2,1)}, bf16[768,128]{1,0:T(8,128)(2,1)S(1)}, u32[]{:S(2)}) copy-start(bf16[768,128]{1,0:T(8,128)(2,1)S(1)} %constant_dynamic-update-slice_fusion.8) | copy-start | bytes 589828
  222.5 7.6 %collective-permute-start.9 = (bf16[1,768,128]{2,1,0:T(8,128)(2,1)S(1)}, bf16[1,768,128]{2,1,0:T(8,128)(2,1)S(1)}, u32[]{:S(2)}, u32[]{:S(2)}) collective-permute-start(bf16[1,768,128]{2,1,0:T(8,128)(2,1)S(1)} %bitcast.332), channel_id=1, source_target_pairs={{0,8},{4,12},{8,0},{12,4},{16,24},{20,28},{24,16},{28,20},{32,40},... | collective-permute-start | bytes 589832 | tf_op jit(solution)/shard_map/ppermute | solution.py:69
  226.5 16.4 %copy-start.21 = (bf16[256,2,128]{0,2,1:T(8,128)(2,1)S(1)}, bf16[256,2,128]{0,2,1:T(8,128)(2,1)}, u32[]{:S(2)}) copy-start(bf16[256,2,128]{0,2,1:T(8,128)(2,1)} %copy-done.20) | copy-start | bytes 393220
  231.5 14.4 %collective-permute-start.10 = (bf16[2,768,128]{2,1,0:T(8,128)(2,1)}, bf16[2,768,128]{2,1,0:T(8,128)(2,1)S(1)}, u32[]{:S(2)}, u32[]{:S(2)}) collective-permute-start(bf16[2,768,128]{2,1,0:T(8,128)(2,1)} %pad_maximum_fusion.21), channel_id=1, source_target_pairs={{0,4},{4,0},{8,12},{12,8},{16,20},{20,16},{24,28},{28,24},{32,36},... | collective-permute-start | bytes 1179656 | tf_op jit(solution)/shard_map/ppermute | solution.py:69
  247.6 18.7 %collective-permute-start.13 = (bf16[4,224,128]{2,1,0:T(8,128)(2,1)S(1)}, bf16[4,224,128]{2,1,0:T(8,128)(2,1)S(1)}, u32[]{:S(2)}, u32[]{:S(2)}) collective-permute-start(bf16[4,224,128]{2,1,0:T(8,128)(2,1)S(1)} %pad_maximum_fusion.29), channel_id=1, source_target_pairs={{0,32},{4,36},{8,40},{12,44},{16,48},{20,52},{24,56},{28,60},{32,0... | collective-permute-start | bytes 688136 | tf_op jit(solution)/shard_map/ppermute | solution.py:69
  251.7 19.3 %copy-start.19 = (bf16[256,2,128]{2,1,0:T(2,128)(2,1)S(1)}, bf16[256,2,128]{2,1,0:T(2,128)(2,1)}, u32[]{:S(2)}) copy-start(bf16[256,2,128]{2,1,0:T(2,128)(2,1)} %param.11) | copy-start | bytes 393220
  266.4 15.8 %collective-permute-start.14 = (bf16[8,224,128]{2,1,0:T(8,128)(2,1)S(1)}, bf16[8,224,128]{2,1,0:T(8,128)(2,1)S(1)}, u32[]{:S(2)}, u32[]{:S(2)}) collective-permute-start(bf16[8,224,128]{2,1,0:T(8,128)(2,1)S(1)} %pad_maximum_fusion.19), channel_id=1, source_target_pairs={{0,16},{4,20},{8,24},{12,28},{16,0},{20,4},{24,8},{28,12},{32,48},... | collective-permute-start | bytes 1376264 | tf_op jit(solution)/shard_map/ppermute | solution.py:69
  282.2 15.5 %collective-permute-start.17 = (bf16[16,80,128]{2,1,0:T(8,128)(2,1)S(1)}, bf16[16,80,128]{2,1,0:T(8,128)(2,1)}, u32[]{:S(2)}, u32[]{:S(2)}) collective-permute-start(bf16[16,80,128]{2,1,0:T(8,128)(2,1)S(1)} %pad_maximum_fusion.26), channel_id=1, source_target_pairs={{0,128},{4,132},{8,136},{12,140},{16,144},{20,148},{24,152},{28,15... | collective-permute-start | bytes 983048 | tf_op jit(solution)/shard_map/ppermute | solution.py:69
  285.7 18.0 %copy-start.39 = (bf16[64,2,128]{2,0,1:T(8,128)(2,1)S(1)}, bf16[64,2,128]{2,0,1:T(8,128)(2,1)}, u32[]{:S(2)}) copy-start(bf16[64,2,128]{2,0,1:T(8,128)(2,1)} %copy-done.38) | copy-start | bytes 98308
  286.8 19.0 %copy-start.32 = (bf16[64,2,128]{2,0,1:T(8,128)(2,1)S(1)}, bf16[64,2,128]{2,0,1:T(8,128)(2,1)}, u32[]{:S(2)}) copy-start(bf16[64,2,128]{2,0,1:T(8,128)(2,1)} %copy-done.31) | copy-start | bytes 98308
  287.6 18.3 %copy-start.58 = (f32[2,1024]{1,0:T(2,128)S(1)}, f32[2,1024]{1,0:T(2,128)}, u32[]{:S(2)}) copy-start(f32[2,1024]{1,0:T(2,128)} %sub.438) | copy-start | bytes 24580
  299.6 18.2 %collective-permute-start.18 = (bf16[32,80,128]{2,1,0:T(8,128)(2,1)}, bf16[32,80,128]{2,1,0:T(8,128)(2,1)}, u32[]{:S(2)}, u32[]{:S(2)}) collective-permute-start(bf16[32,80,128]{2,1,0:T(8,128)(2,1)} %pad_maximum_fusion.12), channel_id=1, source_target_pairs={{0,64},{4,68},{8,72},{12,76},{16,80},{20,84},{24,88},{28,92},{32,9... | collective-permute-start | bytes 1966088 | tf_op jit(solution)/shard_map/ppermute | solution.py:69
  319.8 30.0 %collective-permute-start.20 = (bf16[64,32,128]{2,1,0:T(8,128)(2,1)}, bf16[64,32,128]{2,1,0:T(8,128)(2,1)}, u32[]{:S(2)}, u32[]{:S(2)}) collective-permute-start(bf16[64,32,128]{2,1,0:T(8,128)(2,1)} %get-tuple-element.33), channel_id=1, source_target_pairs={{256,0},{260,4},{264,8},{268,12},{272,16},{276,20},{280,24},{284,2... | collective-permute-start | bytes 1572872 | tf_op jit(solution)/shard_map/ppermute | solution.py:69
  332.1 22.4 %copy-start.69 = (bf16[8,2,128]{2,0,1:T(8,128)(2,1)S(1)}, bf16[8,2,128]{2,0,1:T(8,128)(2,1)}, u32[]{:S(2)}) copy-start(bf16[8,2,128]{2,0,1:T(8,128)(2,1)} %copy-done.68) | copy-start | bytes 12292
  332.1 22.4 %copy-start.80 = (pred[1024,8]{0,1:T(8,128)(4,1)S(1)}, pred[1024,8]{0,1:T(8,128)(4,1)}, u32[]{:S(2)}) copy-start(pred[1024,8]{0,1:T(8,128)(4,1)} %broadcast_compare_fusion.6) | copy-start | bytes 24580
  (63 other events, 438.5 us)
